TPU v7x, 512 devices: a whole 4x4x16 slice. The times are simulated.
512 devices in a mesh: expert: 64 (over x, y, z_hi, core), dp: 8 (over z_lo).
Axes of the slice: x: 4, y: 4, z: 16 (z_hi: 2, z_lo: 8; z = z_hi * 8 + z_lo), core: 2. Of those that a mesh axis runs over, the one named last changes fastest.
Arguments:
- tokens: bfloat16 [256, 2048], P('dp'), may hold values from -6 to 6
- w_gate: bfloat16 [128, 768, 2048], P('expert', 'dp'), may hold values from -2 to 2
- w_up: bfloat16 [128, 768, 2048], P('expert', 'dp'), may hold values from -2 to 2
- w_down: bfloat16 [128, 768, 2048], P('expert', 'dp'), may hold values from -2 to 2
Outputs:
- cosine: float32 [256, 128, 128], P('expert')
All inputs are finite; a program needn't handle non-finite values.
Results may differ from a plain program's by a relative error of at most 0.0014.
Values may be sent and summed in bfloat16 or wider, within the bound.
No kernel may reach another device: no remote copies, remote signals or barrier semaphores. Data moves between devices by JAX's collectives and lax.ppermute only.
A program may use at most 64 MiB of HBM per device.

v0:
```python
import jax
import jax.numpy as jnp
from jax import lax
from jax.sharding import PartitionSpec as P


def shards(tokens, w_gate, w_up, w_down):
    block_rows = lax.all_gather(tokens, "dp", axis=0, tiled=True)
    gate = jnp.einsum("td,ehd->teh", block_rows, w_gate, preferred_element_type=jnp.float32)
    upward = jnp.einsum("td,ehd->teh", block_rows, w_up, preferred_element_type=jnp.float32)
    hidden = (jax.nn.silu(gate) * upward).astype(jnp.bfloat16)
    partial_out = jnp.einsum("teh,ehf->etf", hidden, w_down, preferred_element_type=jnp.float32)
    regrouped = lax.all_to_all(partial_out, "expert", split_axis=1, concat_axis=0, tiled=True)
    summed = lax.psum_scatter(regrouped, "dp", scatter_dimension=2, tiled=True)
    features = summed.astype(jnp.bfloat16)
    partial_gram = jnp.einsum(
        "etf,gtf->teg", features, features, preferred_element_type=jnp.float32
    )
    gram = lax.psum(partial_gram, "dp")
    diagonal = jnp.diagonal(gram, axis1=1, axis2=2)
    inverse = lax.rsqrt(diagonal + 1e-06)
    return gram * inverse[:, :, None] * inverse[:, None, :]


def solution(mesh):
    placed = (
        P("dp", None),
        P("expert", "dp", None),
        P("expert", "dp", None),
        P("expert", "dp", None),
    )
    return jax.shard_map(
        shards, mesh=mesh, in_specs=placed, out_specs=P("expert", None, None), check_vma=False
    )
```

profile of v0, /device:TPU:2, one launch (start us, length us, event | category | flops | bytes accessed | tf_op | source)
XLA Modules:
  0.0 533.4 jit_solution(13189591269529900272)
XLA Ops:
  6.5 0.0 copy-start
  6.5 0.0 all-gather.2.cloned.1.call-start
  6.5 0.7 all-gather.2.cloned.1.call-update
  7.3 0.0 reduce-scatter.2.cloned.1.call-start
  7.3 73.8 %all-gather.2.cloned.1.call-done = bf16[256,2048]{1,0:T(8,128)(2,1)} async-done(((bf16[32,2048]{1,0:T(8,128)(2,1)}), bf16[256,2048]{1,0:T(8,128)(2,1)}) %all-gather.2.cloned.1.call-update) | async-done | bytes 1048592 | tf_op jit(solution)/shard_map/all_gather | solution.py:8
  81.1 1.9 fusion.4
  83.0 0.0 copy-done
  83.1 5.1 fusion.1
  88.1 5.4 %copy.9 = f32[2,256,2048]{2,0,1:T(2,128)S(1)} copy(f32[2,256,2048]{2,1,0:T(8,128)} %fusion.1) | data formatting | bytes 8388608 | tf_op jit(solution)/shard_map/teh,ehf->etf/dot_general | solution.py:12
  93.6 191.2 %all_to_all.18 = f32[2,256,2048]{2,0,1:T(2,128)S(1)} all-to-all(f32[2,256,2048]{2,0,1:T(2,128)S(1)} %copy.9), channel_id=1, replica_groups=mesh['expert'=64,'dp'=8] {'expert'}, dimensions={1} | all-to-all | bytes 8388608 | tf_op jit(solution)/shard_map/all_to_all | solution.py:13
  284.8 3.9 copy.10
  288.7 6.0 %all_to_all.16 = f32[128,4,2048]{2,0,1:T(8,128)} reshape(f32[64,2,4,2048]{3,1,0,2:T(2,128)} %copy.10) | data formatting | bytes 8388608 | tf_op jit(solution)/shard_map/all_to_all | solution.py:13
  294.7 0.0 reduce-scatter.2.cloned.1.call-update
  294.7 0.0 all-reduce.2.cloned.1.call-start
  294.8 104.0 %reduce-scatter.2.cloned.1.call-done = f32[128,4,256]{2,0,1:T(8,128)} async-done(((f32[128,4,2048]{2,0,1:T(8,128)}), f32[128,4,256]{2,0,1:T(8,128)}) %reduce-scatter.2.cloned.1.call-update) | async-done | bytes 524304 | tf_op jit(solution)/shard_map/reduce_scatter | solution.py:14
  398.8 2.1 fusion.6
  401.0 0.0 all-reduce.2.cloned.1.call-update
  401.0 117.3 %all-reduce.2.cloned.1.call-done = f32[4,128,128]{2,1,0:T(8,128)} async-done(((f32[4,128,128]{2,1,0:T(8,128)}), f32[4,128,128]{2,1,0:T(8,128)}) %all-reduce.2.cloned.1.call-update) | async-done | bytes 262160 | tf_op jit(solution)/shard_map/psum | solution.py:19
  518.3 0.0 copy-start.1
  518.3 5.8 %copy.11 = f32[4,128,128]{0,2,1:T(8,128)} copy(f32[4,128,128]{2,1,0:T(8,128)} %all-reduce.2.cloned.1.call-done) | data formatting | bytes 524288 | tf_op jit(solution)/shard_map/psum | solution.py:19
  524.1 1.7 gather_fusion
  525.9 0.1 copy.12
  526.0 0.0 copy-done.1
  526.0 0.9 multiply_multiply_fusion
  (2 shorter events, 0.0 us)
Async XLA Ops:
  6.5 76.5 %copy-start = (bf16[2,96,2048]{2,1,0:T(8,128)(2,1)S(1)}, bf16[2,96,2048]{2,1,0:T(8,128)(2,1)}, u32[]{:S(2)}) copy-start(bf16[2,96,2048]{2,1,0:T(8,128)(2,1)} %param.7) | copy-start | bytes 2359300
  6.5 74.6 %all-gather.2.cloned.1.call-start = ((), (), s32[]{:S(2)}) async-start(), calls=%async_computation.2 | async-start | bytes 1179648 | tf_op jit(solution)/shard_map/all_gather | solution.py:8
  7.3 391.6 %reduce-scatter.2.cloned.1.call-start = ((), (), s32[]{:S(2)}) async-start(), calls=%async_computation.3 | async-start | bytes 4718592 | tf_op jit(solution)/shard_map/reduce_scatter | solution.py:14
  294.7 223.6 %all-reduce.2.cloned.1.call-start = ((), (), s32[]{:S(2)}) async-start(), calls=%async_computation.4 | async-start | bytes 524288 | tf_op jit(solution)/shard_map/psum | solution.py:19
  518.3 7.6 %copy-start.1 = (f32[4,128,128]{2,1,0:T(8,128)S(1)}, f32[4,128,128]{2,1,0:T(8,128)}, u32[]{:S(2)}) copy-start(f32[4,128,128]{2,1,0:T(8,128)} %all-reduce.2.cloned.1.call-done) | copy-start | bytes 786436
Sparse Core Ops, SparseCore 0:
  9.4 71.6 all-gather.1
  294.9 103.9 reduce-scatter.1
  401.7 116.5 all-reduce.1
where the time goes:
time: 534 us; the launch traced here: 533 us
  waiting for transfers between devices  296 us (55%)
  blocking collectives  191 us (36%)
  local copies, waits for them, and re-layouts  23 us (4%)
  between operations  13.1 us (2%)
  matrix products  9.16 us (2%)
    all_to_all x1, blocking collectives, shards(): lax.all_to_all(partial_out, 'expert', split_axis=1, concat_axis=0, tiled=...  191 us
    psum x1, waiting for transfers between devices, shards(): gram = lax.psum(partial_gram, 'dp')  117 us
    reduce_scatter x1, waiting for transfers between devices, shards(): summed = lax.psum_scatter(regrouped, 'dp', scatter_dimension=2, tiled=True)  104 us
    all_gather x1, waiting for transfers between devices, shards(): block_rows = lax.all_gather(tokens, 'dp', axis=0, tiled=True)  73.8 us
  transfers between devices with their start and end apart: 3, of which 3 were waited for; matrix products, arithmetic and copies ran while one was open for 0% of the time, Pallas kernels for 0%

commit v1 on v0

v1 whole, which is shorter than its diff:
```python
import jax
import jax.numpy as jnp
from jax import lax
from jax.sharding import PartitionSpec as P


def all_reduce_dp(x, n):
    pieces = x.reshape((n, -1))
    mine = lax.all_to_all(pieces, "dp", 0, 0, tiled=True).sum(0, keepdims=True)
    spread = jnp.broadcast_to(mine, pieces.shape)
    return lax.all_to_all(spread, "dp", 0, 0, tiled=True).reshape(x.shape)


def shards(tokens, w_gate, w_up, w_down):
    n = lax.axis_size("dp")
    down_cols = lax.all_to_all(w_down, "dp", 2, 1, tiled=True)
    block_rows = lax.all_gather(tokens, "dp", axis=0, tiled=True)
    gate = jnp.einsum("td,ehd->eth", block_rows, w_gate, preferred_element_type=jnp.float32)
    upward = jnp.einsum("td,ehd->eth", block_rows, w_up, preferred_element_type=jnp.float32)
    hidden = (jax.nn.silu(gate) * upward).astype(jnp.bfloat16)
    hidden_all = lax.all_gather(hidden, "dp", axis=2, tiled=True)
    outputs = jnp.einsum("eth,ehf->etf", hidden_all, down_cols, preferred_element_type=jnp.float32)
    features = outputs.astype(jnp.bfloat16)
    regrouped = lax.all_to_all(features, "expert", 1, 0, tiled=True)
    partial_gram = jnp.einsum(
        "etf,gtf->teg", regrouped, regrouped, preferred_element_type=jnp.float32
    )
    gram = all_reduce_dp(partial_gram, n)
    diagonal = jnp.diagonal(gram, axis1=1, axis2=2)
    inverse = lax.rsqrt(diagonal + 1e-06)
    return gram * inverse[:, :, None] * inverse[:, None, :]


def solution(mesh):
    placed = (
        P("dp", None),
        P("expert", "dp", None),
        P("expert", "dp", None),
        P("expert", "dp", None),
    )
    return jax.shard_map(
        shards, mesh=mesh, in_specs=placed, out_specs=P("expert", None, None), check_vma=False
    )
```

time: 534 us -> 246 us (0.46)
  the two profiles are of different devices: /device:TPU:2 before, /device:TPU:32 now
where the time goes in v1:
time: 246 us
  blocking collectives  109 us (44%)
  waiting for transfers between devices  87.5 us (36%)
  starting transfers between devices  18.1 us (7%)
  between operations  13.5 us (5%)
  local copies, waits for them, and re-layouts  12.3 us (5%)
  matrix products  4.34 us (2%)
    all_gather x1, waiting for transfers between devices, shards(): block_rows = lax.all_gather(tokens, 'dp', axis=0, tiled=True)  70.8 us
    all_gather x1, blocking collectives, shards(): hidden_all = lax.all_gather(hidden, 'dp', axis=2, tiled=True)  50 us
    all_to_all x1, blocking collectives, shards(): regrouped = lax.all_to_all(features, 'expert', 1, 0, tiled=True)  34.7 us
    all_to_all x1, blocking collectives, all_reduce_dp(): mine = lax.all_to_all(pieces, 'dp', 0, 0, tiled=True).sum(0, keepdims=True)  24.1 us
    all_to_all x1, waiting for transfers between devices, all_reduce_dp(): return lax.all_to_all(spread, 'dp', 0, 0, tiled=True).reshape(x.shape)  15.9 us
    all_to_all x1, starting transfers between devices, shards(): down_cols = lax.all_to_all(w_down, 'dp', 2, 1, tiled=True)  12.6 us
    all_to_all x1, starting transfers between devices, all_reduce_dp(): return lax.all_to_all(spread, 'dp', 0, 0, tiled=True).reshape(x.shape)  5.52 us
  transfers between devices with their start and end apart: 3, of which 2 were waited for; matrix products, arithmetic and copies ran while one was open for 2% of the time, Pallas kernels for 0%

profile of v1, /device:TPU:32, one launch (start us, length us, event | category | flops | bytes accessed | tf_op | source)
XLA Modules:
  0.0 245.6 jit_solution(15436667646739890963)
XLA Ops:
  6.5 0.0 copy-start
  6.5 3.7 %copy.13 = bf16[2,96,2048]{1,0,2:T(2,128)(2,1)} copy(bf16[2,96,2048]{2,1,0:T(8,128)(2,1)} %param.7) | data formatting | bytes 1572864 | tf_op args[3]
  10.2 12.6 %all-to-all-start = ((bf16[2,96,2048]{1,0,2:T(2,128)(2,1)}), bf16[2,96,2048]{1,0,2:T(2,128)(2,1)S(1)}, u32[]{:S(2)}, u32[]{:S(2)}) async-start(bf16[2,96,2048]{1,0,2:T(2,128)(2,1)} %copy.13), calls=%async_computation | async-start | bytes 2097152 | tf_op jit(solution)/shard_map/all_to_all | solution.py:16
  22.9 0.0 all-gather.2.cloned.1.call-start
  22.9 0.7 all-gather.2.cloned.1.call-update
  23.6 70.8 %all-gather.2.cloned.1.call-done = bf16[256,2048]{1,0:T(8,128)(2,1)} async-done(((bf16[32,2048]{1,0:T(8,128)(2,1)}), bf16[256,2048]{1,0:T(8,128)(2,1)}) %all-gather.2.cloned.1.call-update) | async-done | bytes 1048592 | tf_op jit(solution)/shard_map/all_gather | solution.py:17
  94.4 0.0 copy-done
  94.4 1.7 convolution_bitcast_fusion.1
  96.2 2.0 fusion.1
  98.1 50.0 %all_gather.7 = bf16[2,256,768]{1,2,0:T(8,128)(2,1)S(1)} all-gather(bf16[2,256,96]{1,2,0:T(8,128)(2,1)S(1)} %fusion.1), channel_id=1, replica_groups=mesh['expert'=64,'dp'=8] {'dp'}, dimensions={2}, use_global_device_ids=true | all-gather | bytes 884736 | tf_op jit(solution)/shard_map/all_gather | solution.py:21
  148.1 0.0 all-to-all-done
  148.1 0.8 copy.14
  148.9 0.4 convolution_convert_fusion
  149.3 0.3 copy.15
  149.6 34.7 %all_to_all.51 = bf16[2,256,256]{2,0,1:T(2,128)(2,1)S(1)} all-to-all(bf16[2,256,256]{2,0,1:T(2,128)(2,1)S(1)} %copy.15), channel_id=1, replica_groups=mesh['expert'=64,'dp'=8] {'expert'}, dimensions={1} | all-to-all | bytes 524288 | tf_op jit(solution)/shard_map/all_to_all | solution.py:24
  184.3 0.2 copy.22
  184.5 0.1 all_to_all.43
  184.6 0.2 fusion.4
  184.8 24.1 %all_to_all.52 = f32[8,1,8192]{2,1,0:T(1,128)S(1)} all-to-all(f32[8,1,8192]{2,1,0:T(1,128)S(1)} %bitcast.41), channel_id=1, replica_groups=mesh['expert'=64,'dp'=8] {'dp'}, dimensions={0} | all-to-all | bytes 524288 | tf_op jit(solution)/shard_map/all_to_all | solution.py:9
  209.0 0.2 reduce_sum.9
  209.2 0.8 broadcast_in_dim.4
  210.0 5.5 %all-to-all-start.3 = ((f32[8,1,8192]{2,1,0:T(1,128)}), f32[8,1,8192]{2,1,0:T(1,128)S(1)}, u32[]{:S(2)}, u32[]{:S(2)}) async-start(f32[8,1,8192]{2,1,0:T(1,128)} %broadcast_in_dim.4), calls=%async_computation.3 | async-start | bytes 524288 | tf_op jit(solution)/shard_map/all_to_all | solution.py:11
  215.5 15.9 %all-to-all-done.3 = f32[8,1,8192]{2,1,0:T(1,128)S(1)} async-done(((f32[8,1,8192]{2,1,0:T(1,128)}), f32[8,1,8192]{2,1,0:T(1,128)S(1)}, u32[]{:S(2)}, u32[]{:S(2)}) %all-to-all-start.3) | async-done | bytes 262176 | tf_op jit(solution)/shard_map/all_to_all | solution.py:11
  231.4 4.6 %copy.18 = f32[4,128,128]{0,2,1:T(8,128)} copy(f32[4,128,128]{2,1,0:T(8,128)S(1)} %bitcast.39) | data formatting | bytes 524288 | tf_op jit(solution)/shard_map/reshape | solution.py:11
  236.1 1.7 gather_fusion
  237.8 0.1 copy.19
  237.9 0.9 multiply_multiply_fusion
  (2 shorter events, 0.0 us)
Async XLA Ops:
  6.5 87.9 %copy-start = (bf16[2,96,2048]{2,1,0:T(8,128)(2,1)S(1)}, bf16[2,96,2048]{2,1,0:T(8,128)(2,1)}, u32[]{:S(2)}) copy-start(bf16[2,96,2048]{2,1,0:T(8,128)(2,1)} %param.5) | copy-start | bytes 2359300
  10.2 137.9 %all-to-all-start = ((bf16[2,96,2048]{1,0,2:T(2,128)(2,1)}), bf16[2,96,2048]{1,0,2:T(2,128)(2,1)S(1)}, u32[]{:S(2)}, u32[]{:S(2)}) async-start(bf16[2,96,2048]{1,0,2:T(2,128)(2,1)} %copy.13), calls=%async_computation | async-start | bytes 2097152 | tf_op jit(solution)/shard_map/all_to_all | solution.py:16
  22.9 71.6 %all-gather.2.cloned.1.call-start = ((), (), s32[]{:S(2)}) async-start(), calls=%async_computation.4 | async-start | bytes 1179648 | tf_op jit(solution)/shard_map/all_gather | solution.py:17
  210.0 21.4 %all-to-all-start.3 = ((f32[8,1,8192]{2,1,0:T(1,128)}), f32[8,1,8192]{2,1,0:T(1,128)S(1)}, u32[]{:S(2)}, u32[]{:S(2)}) async-start(f32[8,1,8192]{2,1,0:T(1,128)} %broadcast_in_dim.4), calls=%async_computation.3 | async-start | bytes 524288 | tf_op jit(solution)/shard_map/all_to_all | solution.py:11
Sparse Core Ops, SparseCore 0:
  25.7 68.6 all-gather.1

commit v2 on v1

v2 whole, which is shorter than its diff:
```python
import jax
import jax.numpy as jnp
from jax import lax
from jax.sharding import PartitionSpec as P

BOTH = ("expert", "dp")


def z_ring_pairs(mesh, shift):
    axes = mesh.axis_names
    devs = mesh.devices.reshape(-1)
    index_of = {}
    for i, d in enumerate(devs):
        x, y, z = d.coords[:3]
        index_of[(x, y, z, d.core_on_chip)] = i
    z_len = 1 + max(k[2] for k in index_of)
    pairs = []
    for (x, y, z, c), i in index_of.items():
        pairs.append((i, index_of[(x, y, (z + shift) % z_len, c)]))
    assert axes == BOTH
    return sorted(pairs)


def gather_blocks(block, rings, n):
    k = lax.axis_index("dp")
    shifts = tuple(s for s, _ in rings)
    received = [block] + [lax.ppermute(block, BOTH, pairs) for _, pairs in rings]
    stacked = jnp.stack(received)
    source = (k - jnp.array((0,) + shifts)) % n
    ordered = jnp.take(stacked, jnp.argsort(source), axis=0)
    return ordered


def all_reduce_dp(x, n):
    pieces = x.reshape((n, -1))
    mine = lax.all_to_all(pieces, "dp", 0, 0, tiled=True).sum(0, keepdims=True)
    spread = jnp.broadcast_to(mine, pieces.shape)
    return lax.all_to_all(spread, "dp", 0, 0, tiled=True).reshape(x.shape)


def make_shards(mesh):
    n = mesh.shape["dp"]
    half = n // 2
    shifts = tuple(range(1, half + 1)) + tuple(-s for s in range(1, n - half))
    rings = tuple((s, z_ring_pairs(mesh, s)) for s in shifts)
    dp_shifts = tuple(range(1, n))

    def shards(tokens, w_gate, w_up, w_down):
        block_rows = gather_blocks(tokens, rings, n).reshape((-1, tokens.shape[1]))
        down_cols = lax.all_to_all(w_down, "dp", 2, 1, tiled=True)
        gate = jnp.einsum("td,ehd->eth", block_rows, w_gate, preferred_element_type=jnp.float32)
        upward = jnp.einsum("td,ehd->eth", block_rows, w_up, preferred_element_type=jnp.float32)
        hidden = (jax.nn.silu(gate) * upward).astype(jnp.bfloat16)
        k = lax.axis_index("dp")
        got = [hidden] + [
            lax.ppermute(hidden, "dp", [(i, (i + s) % n) for i in range(n)]) for s in dp_shifts
        ]
        stacked = jnp.stack(got)
        source = (k - jnp.arange(n)) % n
        hidden_all = jnp.take(stacked, jnp.argsort(source), axis=0)
        outputs = jnp.einsum(
            "keth,ekhf->etf",
            hidden_all,
            down_cols.reshape(w_down.shape[0], n, -1, down_cols.shape[2]),
            preferred_element_type=jnp.float32,
        )
        features = outputs.astype(jnp.bfloat16)
        regrouped = lax.all_to_all(features, "expert", 1, 0, tiled=True)
        partial_gram = jnp.einsum(
            "etf,gtf->teg", regrouped, regrouped, preferred_element_type=jnp.float32
        )
        gram = all_reduce_dp(partial_gram, n)
        eye = jnp.eye(gram.shape[1], dtype=jnp.bool_)
        diagonal = jnp.sum(jnp.where(eye[None], gram, 0.0), axis=2)
        inverse = lax.rsqrt(diagonal + 1e-06)
        return gram * inverse[:, :, None] * inverse[:, None, :]

    return shards


def solution(mesh):
    placed = (
        P("dp", None),
        P("expert", "dp", None),
        P("expert", "dp", None),
        P("expert", "dp", None),
    )
    return jax.shard_map(
        make_shards(mesh), mesh=mesh, in_specs=placed, out_specs=P("expert", None, None), check_vma=False
    )
```

time: 246 us -> 230 us (0.935)
  starting transfers between devices: 18.1 us -> 76.9 us
  blocking collectives: 109 us -> 62.6 us
  waiting for transfers between devices: 87.5 us -> 67.5 us
  between operations: 13.5 us -> 0.34 us
  local copies, waits for them, and re-layouts: 12.3 us -> 16.5 us
  matrix products: 4.34 us -> 1.74 us
    all_gather x1 -> x0, waiting for transfers between devices: 70.8 us -> none  [shards(): block_rows = lax.all_gather(tokens, 'dp', axis=0, tiled=True)]
    ppermute x0 -> x14, starting transfers between devices: none -> 65.4 us  [the longest x7 37.3 us: gather_blocks(): lax.ppermute(block, BOTH, pairs)]
    ppermute x0 -> x14, waiting for transfers between devices: none -> 51.6 us  [the longest x7 45.1 us: gather_blocks(): lax.ppermute(block, BOTH, pairs)]
    all_gather x1 -> x0, blocking collectives: 50 us -> none  [shards(): hidden_all = lax.all_gather(hidden, 'dp', axis=2, tiled=True)]
    all_to_all x1, starting transfers between devices: 12.6 us -> 6 us  [shards(): down_cols = lax.all_to_all(w_down, 'dp', 2, 1, tiled=True)]
    unnamed x3 -> x24, local copies, waits for them, and re-layouts: 3.69 us -> 10.3 us
    all_to_all x1, blocking collectives: 34.7 us -> 40.9 us  [shards(): regrouped = lax.all_to_all(features, 'expert', 1, 0, tiled=True)]
    reshape x1 -> x0, local copies, waits for them, and re-layouts: 4.64 us -> none  [all_reduce_dp(): return lax.all_to_all(spread, 'dp', 0, 0, tiled=True).reshape(x.shape)]
  transfers between devices with their start and end apart: 3 -> 16, of which waited for: 2 -> 5; matrix products, arithmetic and copies ran while one was open for 2% -> 7% of each run, Pallas kernels for 0% -> 0%
where the time goes in v2:
time: 230 us; the launch traced here: 229 us
  starting transfers between devices  76.9 us (33%)
  waiting for transfers between devices  67.5 us (29%)
  blocking collectives  62.6 us (27%)
  local copies, waits for them, and re-layouts  16.5 us (7%)
  other arithmetic  3.38 us (1%)
    ppermute x7, waiting for transfers between devices, gather_blocks(): lax.ppermute(block, BOTH, pairs)  45.1 us
    all_to_all x1, blocking collectives, shards(): regrouped = lax.all_to_all(features, 'expert', 1, 0, tiled=True)  40.9 us
    ppermute x7, starting transfers between devices, gather_blocks(): lax.ppermute(block, BOTH, pairs)  37.3 us
    ppermute x7, starting transfers between devices, shards(): lax.ppermute(hidden, 'dp', [(i, (i + s) % n) for i in range(n)])  28.2 us
    all_to_all x1, blocking collectives, all_reduce_dp(): mine = lax.all_to_all(pieces, 'dp', 0, 0, tiled=True).sum(0, keepdims=True)  21.7 us
    all_to_all x1, waiting for transfers between devices, all_reduce_dp(): return lax.all_to_all(spread, 'dp', 0, 0, tiled=True).reshape(x.shape)  15.9 us
    unnamed x24, local copies, waits for them, and re-layouts  10.3 us
    ppermute x7, waiting for transfers between devices, shards(): lax.ppermute(hidden, 'dp', [(i, (i + s) % n) for i in range(n)])  6.49 us
  transfers between devices with their start and end apart: 16, of which 5 were waited for; matrix products, arithmetic and copies ran while one was open for 7% of the time, Pallas kernels for 0%

profile of v2, /device:TPU:32, one launch (start us, length us, event | category | flops | bytes accessed | tf_op | source)
XLA Modules:
  0.0 229.0 jit_solution(12297476542977205519)
XLA Ops:
  0.0 3.9 %collective-permute-start = (bf16[32,2048]{1,0:T(8,128)(2,1)}, bf16[32,2048]{1,0:T(8,128)(2,1)S(1)}, u32[]{:S(2)}, u32[]{:S(2)}) collective-permute-start(bf16[32,2048]{1,0:T(8,128)(2,1)} %param.5), channel_id=1, source_target_pairs={{0,1},{1,2},{2,3},{3,4},{4,5},{5,6},{6,7},{7,16},{8,9},{9,10},{10,... | collective-permute-start | bytes 393224 | tf_op jit(solution)/shard_map/ppermute | solution.py:27
  4.0 6.4 %collective-permute-start.1 = (bf16[32,2048]{1,0:T(8,128)(2,1)}, bf16[32,2048]{1,0:T(8,128)(2,1)S(1)}, u32[]{:S(2)}, u32[]{:S(2)}) collective-permute-start(bf16[32,2048]{1,0:T(8,128)(2,1)} %param.5), channel_id=1, source_target_pairs={{0,2},{1,3},{2,4},{3,5},{4,6},{5,7},{6,16},{7,17},{8,10},{9,11},{1... | collective-permute-start | bytes 393224 | tf_op jit(solution)/shard_map/ppermute | solution.py:27
  10.4 6.5 %collective-permute-start.2 = (bf16[32,2048]{1,0:T(8,128)(2,1)}, bf16[32,2048]{1,0:T(8,128)(2,1)S(1)}, u32[]{:S(2)}, u32[]{:S(2)}) collective-permute-start(bf16[32,2048]{1,0:T(8,128)(2,1)} %param.5), channel_id=1, source_target_pairs={{0,3},{1,4},{2,5},{3,6},{4,7},{5,16},{6,17},{7,18},{8,11},{9,12},{... | collective-permute-start | bytes 393224 | tf_op jit(solution)/shard_map/ppermute | solution.py:27
  16.9 6.4 %collective-permute-start.3 = (bf16[32,2048]{1,0:T(8,128)(2,1)}, bf16[32,2048]{1,0:T(8,128)(2,1)S(1)}, u32[]{:S(2)}, u32[]{:S(2)}) collective-permute-start(bf16[32,2048]{1,0:T(8,128)(2,1)} %param.5), channel_id=1, source_target_pairs={{0,4},{1,5},{2,6},{3,7},{4,16},{5,17},{6,18},{7,19},{8,12},{9,13},... | collective-permute-start | bytes 393224 | tf_op jit(solution)/shard_map/ppermute | solution.py:27
  23.3 2.9 %collective-permute-start.4 = (bf16[32,2048]{1,0:T(8,128)(2,1)}, bf16[32,2048]{1,0:T(8,128)(2,1)S(1)}, u32[]{:S(2)}, u32[]{:S(2)}) collective-permute-start(bf16[32,2048]{1,0:T(8,128)(2,1)} %param.5), channel_id=1, source_target_pairs={{0,23},{1,0},{2,1},{3,2},{4,3},{5,4},{6,5},{7,6},{8,31},{9,8},{10,... | collective-permute-start | bytes 393224 | tf_op jit(solution)/shard_map/ppermute | solution.py:27
  26.2 3.6 %copy.11 = bf16[2,96,2048]{1,0,2:T(2,128)(2,1)} copy(bf16[2,96,2048]{2,1,0:T(8,128)(2,1)} %param.8) | data formatting | bytes 1572864 | tf_op args[3]
  29.8 6.0 %all-to-all-start = ((bf16[2,96,2048]{1,0,2:T(2,128)(2,1)}), bf16[2,96,2048]{1,0,2:T(2,128)(2,1)S(1)}, u32[]{:S(2)}, u32[]{:S(2)}) async-start(bf16[2,96,2048]{1,0,2:T(2,128)(2,1)} %copy.11), calls=%async_computation | async-start | bytes 2097152 | tf_op jit(solution)/shard_map/all_to_all | solution.py:50
  35.9 0.7 bitcast_dynamic-update-slice_fusion.7
  36.5 0.7 copy-done.4
  37.2 1.0 sort.32
  38.2 1.0 sort.31
  39.1 0.1 broadcast_in_dim.50
  39.2 0.1 broadcast_in_dim.51
  39.3 0.0 collective-permute-done
  39.3 8.6 %collective-permute-start.5 = (bf16[32,2048]{1,0:T(8,128)(2,1)S(1)}, bf16[32,2048]{1,0:T(8,128)(2,1)S(1)}, u32[]{:S(2)}, u32[]{:S(2)}) collective-permute-start(bf16[32,2048]{1,0:T(8,128)(2,1)S(1)} %copy-done.3), channel_id=1, source_target_pairs={{0,22},{1,23},{2,0},{3,1},{4,2},{5,3},{6,4},{7,5},{8,30},{9,31},{1... | collective-permute-start | bytes 393224 | tf_op jit(solution)/shard_map/ppermute | solution.py:27
  47.9 0.6 bitcast_dynamic-update-slice_fusion.6
  48.6 0.0 collective-permute-done.1
  48.6 2.5 %collective-permute-start.6 = (bf16[32,2048]{1,0:T(8,128)(2,1)S(1)}, bf16[32,2048]{1,0:T(8,128)(2,1)S(1)}, u32[]{:S(2)}, u32[]{:S(2)}) collective-permute-start(bf16[32,2048]{1,0:T(8,128)(2,1)S(1)} %copy-done.3), channel_id=1, source_target_pairs={{0,21},{1,22},{2,23},{3,0},{4,1},{5,2},{6,3},{7,4},{8,29},{9,30},{... | collective-permute-start | bytes 393224 | tf_op jit(solution)/shard_map/ppermute | solution.py:27
  51.0 0.7 bitcast_dynamic-update-slice_fusion.5
  51.7 0.0 collective-permute-done.2
  51.7 0.7 bitcast_dynamic-update-slice_fusion.4
  52.4 0.7 bitcast_dynamic-update-slice_fusion.3
  53.0 0.0 collective-permute-done.4
  53.0 0.7 bitcast_dynamic-update-slice_fusion.2
  53.7 27.5 %collective-permute-done.5 = bf16[32,2048]{1,0:T(8,128)(2,1)S(1)} collective-permute-done((bf16[32,2048]{1,0:T(8,128)(2,1)S(1)}, bf16[32,2048]{1,0:T(8,128)(2,1)S(1)}, u32[]{:S(2)}, u32[]{:S(2)}) %collective-permute-start.5) | collective-permute-done | bytes 131104 | tf_op jit(solution)/shard_map/ppermute | solution.py:27
  81.2 0.7 bitcast_dynamic-update-slice_fusion.1
  81.8 17.6 %collective-permute-done.6 = bf16[32,2048]{1,0:T(8,128)(2,1)S(1)} collective-permute-done((bf16[32,2048]{1,0:T(8,128)(2,1)S(1)}, bf16[32,2048]{1,0:T(8,128)(2,1)S(1)}, u32[]{:S(2)}, u32[]{:S(2)}) %collective-permute-start.6) | collective-permute-done | bytes 131104 | tf_op jit(solution)/shard_map/ppermute | solution.py:27
  99.4 0.7 bitcast_dynamic-update-slice_fusion
  100.1 1.8 gather_fusion
  101.9 0.0 copy-start.2
  102.0 0.2 bitcast_select_fusion
  102.2 0.9 copy-done.2
  103.1 0.5 convolution_bitcast_fusion.2
  103.6 0.5 bitcast_dynamic-update-slice_fusion.15
  104.1 1.9 collective-permute-start.7
  106.1 2.0 collective-permute-start.8
  108.1 1.9 collective-permute-start.9
  110.0 9.2 %collective-permute-start.10 = (bf16[2,256,96]{1,2,0:T(8,128)(2,1)S(1)}, bf16[2,256,96]{1,2,0:T(8,128)(2,1)S(1)}, u32[]{:S(2)}, u32[]{:S(2)}) collective-permute-start(bf16[2,256,96]{1,2,0:T(8,128)(2,1)S(1)} %get-tuple-element.10), channel_id=1, source_target_pairs={{0,4},{1,5},{2,6},{3,7},{4,0},{5,1},{6,2},{7,3},{8,12},{9,13},{10,... | collective-permute-start | bytes 294920 | tf_op jit(solution)/shard_map/ppermute | solution.py:56
  119.2 2.8 %collective-permute-start.11 = (bf16[2,256,96]{1,2,0:T(8,128)(2,1)S(1)}, bf16[2,256,96]{1,2,0:T(8,128)(2,1)S(1)}, u32[]{:S(2)}, u32[]{:S(2)}) collective-permute-start(bf16[2,256,96]{1,2,0:T(8,128)(2,1)S(1)} %get-tuple-element.10), channel_id=1, source_target_pairs={{0,5},{1,6},{2,7},{3,0},{4,1},{5,2},{6,3},{7,4},{8,13},{9,14},{10,... | collective-permute-start | bytes 294920 | tf_op jit(solution)/shard_map/ppermute | solution.py:56
  122.0 0.0 collective-permute-done.7
  122.1 7.8 %collective-permute-start.12 = (bf16[2,256,96]{1,2,0:T(8,128)(2,1)S(1)}, bf16[2,256,96]{1,2,0:T(8,128)(2,1)S(1)}, u32[]{:S(2)}, u32[]{:S(2)}) collective-permute-start(bf16[2,256,96]{1,2,0:T(8,128)(2,1)S(1)} %get-tuple-element.10), channel_id=1, source_target_pairs={{0,6},{1,7},{2,0},{3,1},{4,2},{5,3},{6,4},{7,5},{8,14},{9,15},{10,... | collective-permute-start | bytes 294920 | tf_op jit(solution)/shard_map/ppermute | solution.py:56
  129.9 0.0 collective-permute-done.8
  129.9 2.5 %collective-permute-start.13 = (bf16[2,256,96]{1,2,0:T(8,128)(2,1)S(1)}, bf16[2,256,96]{1,2,0:T(8,128)(2,1)S(1)}, u32[]{:S(2)}, u32[]{:S(2)}) collective-permute-start(bf16[2,256,96]{1,2,0:T(8,128)(2,1)S(1)} %get-tuple-element.10), channel_id=1, source_target_pairs={{0,7},{1,0},{2,1},{3,2},{4,3},{5,4},{6,5},{7,6},{8,15},{9,8},{10,9... | collective-permute-start | bytes 294920 | tf_op jit(solution)/shard_map/ppermute | solution.py:56
  132.4 0.0 collective-permute-done.9
  132.4 1.9 collective-permute-done.10
  134.4 4.5 %collective-permute-done.11 = bf16[2,256,96]{1,2,0:T(8,128)(2,1)S(1)} collective-permute-done((bf16[2,256,96]{1,2,0:T(8,128)(2,1)S(1)}, bf16[2,256,96]{1,2,0:T(8,128)(2,1)S(1)}, u32[]{:S(2)}, u32[]{:S(2)}) %collective-permute-start.11) | collective-permute-done | bytes 98336 | tf_op jit(solution)/shard_map/ppermute | solution.py:56
  139.0 0.0 collective-permute-done.13
  139.0 1.5 gather_fusion.1
  140.5 0.0 all-to-all-done
  140.5 0.7 copy.13
  141.2 0.5 copy-done.1
  141.6 0.5 fusion
  142.1 0.3 copy.14
  142.4 40.9 %all_to_all.48 = bf16[2,256,256]{2,0,1:T(2,128)(2,1)S(1)} all-to-all(bf16[2,256,256]{2,0,1:T(2,128)(2,1)S(1)} %copy.14), channel_id=1, replica_groups=mesh['expert'=64,'dp'=8] {'expert'}, dimensions={1} | all-to-all | bytes 524288 | tf_op jit(solution)/shard_map/all_to_all | solution.py:68
  183.3 0.2 copy.20
  183.5 0.1 all_to_all.40
  183.6 0.2 fusion.14
  183.8 21.7 %all_to_all.49 = f32[8,1,8192]{2,1,0:T(1,128)S(1)} all-to-all(f32[8,1,8192]{2,1,0:T(1,128)S(1)} %bitcast.80), channel_id=1, replica_groups=mesh['expert'=64,'dp'=8] {'dp'}, dimensions={0} | all-to-all | bytes 524288 | tf_op jit(solution)/shard_map/all_to_all | solution.py:36
  205.6 0.2 reduce_sum.18
  205.8 0.8 broadcast_in_dim.57
  206.6 5.5 %all-to-all-start.3 = ((f32[8,1,8192]{2,1,0:T(1,128)}), f32[8,1,8192]{2,1,0:T(1,128)S(1)}, u32[]{:S(2)}, u32[]{:S(2)}) async-start(f32[8,1,8192]{2,1,0:T(1,128)} %broadcast_in_dim.57), calls=%async_computation.3 | async-start | bytes 524288 | tf_op jit(solution)/shard_map/all_to_all | solution.py:38
  212.1 15.9 %all-to-all-done.3 = f32[8,1,8192]{2,1,0:T(1,128)S(1)} async-done(((f32[8,1,8192]{2,1,0:T(1,128)}), f32[8,1,8192]{2,1,0:T(1,128)S(1)}, u32[]{:S(2)}, u32[]{:S(2)}) %all-to-all-start.3) | async-done | bytes 262176 | tf_op jit(solution)/shard_map/all_to_all | solution.py:38
  228.0 0.1 fusion.9
  228.2 0.9 fusion.10
  (26 shorter events, 0.1 us)
Async XLA Ops:
  0.0 103.6 %copy-start = (bf16[2,96,2048]{2,1,0:T(8,128)(2,1)S(1)}, bf16[2,96,2048]{2,1,0:T(8,128)(2,1)}, u32[]{:S(2)}) copy-start(bf16[2,96,2048]{2,1,0:T(8,128)(2,1)} %param.7) | copy-start | bytes 2359300
  0.0 39.3 %collective-permute-start = (bf16[32,2048]{1,0:T(8,128)(2,1)}, bf16[32,2048]{1,0:T(8,128)(2,1)S(1)}, u32[]{:S(2)}, u32[]{:S(2)}) collective-permute-start(bf16[32,2048]{1,0:T(8,128)(2,1)} %param.5), channel_id=1, source_target_pairs={{0,1},{1,2},{2,3},{3,4},{4,5},{5,6},{6,7},{7,16},{8,9},{9,10},{10,... | collective-permute-start | bytes 393224 | tf_op jit(solution)/shard_map/ppermute | solution.py:27
  4.0 44.6 %collective-permute-start.1 = (bf16[32,2048]{1,0:T(8,128)(2,1)}, bf16[32,2048]{1,0:T(8,128)(2,1)S(1)}, u32[]{:S(2)}, u32[]{:S(2)}) collective-permute-start(bf16[32,2048]{1,0:T(8,128)(2,1)} %param.5), channel_id=1, source_target_pairs={{0,2},{1,3},{2,4},{3,5},{4,6},{5,7},{6,16},{7,17},{8,10},{9,11},{1... | collective-permute-start | bytes 393224 | tf_op jit(solution)/shard_map/ppermute | solution.py:27
  10.4 41.4 %collective-permute-start.2 = (bf16[32,2048]{1,0:T(8,128)(2,1)}, bf16[32,2048]{1,0:T(8,128)(2,1)S(1)}, u32[]{:S(2)}, u32[]{:S(2)}) collective-permute-start(bf16[32,2048]{1,0:T(8,128)(2,1)} %param.5), channel_id=1, source_target_pairs={{0,3},{1,4},{2,5},{3,6},{4,7},{5,16},{6,17},{7,18},{8,11},{9,12},{... | collective-permute-start | bytes 393224 | tf_op jit(solution)/shard_map/ppermute | solution.py:27
  16.9 35.5 %collective-permute-start.3 = (bf16[32,2048]{1,0:T(8,128)(2,1)}, bf16[32,2048]{1,0:T(8,128)(2,1)S(1)}, u32[]{:S(2)}, u32[]{:S(2)}) collective-permute-start(bf16[32,2048]{1,0:T(8,128)(2,1)} %param.5), channel_id=1, source_target_pairs={{0,4},{1,5},{2,6},{3,7},{4,16},{5,17},{6,18},{7,19},{8,12},{9,13},... | collective-permute-start | bytes 393224 | tf_op jit(solution)/shard_map/ppermute | solution.py:27
  23.3 29.7 %collective-permute-start.4 = (bf16[32,2048]{1,0:T(8,128)(2,1)}, bf16[32,2048]{1,0:T(8,128)(2,1)S(1)}, u32[]{:S(2)}, u32[]{:S(2)}) collective-permute-start(bf16[32,2048]{1,0:T(8,128)(2,1)} %param.5), channel_id=1, source_target_pairs={{0,23},{1,0},{2,1},{3,2},{4,3},{5,4},{6,5},{7,6},{8,31},{9,8},{10,... | collective-permute-start | bytes 393224 | tf_op jit(solution)/shard_map/ppermute | solution.py:27
  29.8 6.0 %copy-start.3 = (bf16[32,2048]{1,0:T(8,128)(2,1)S(1)}, bf16[32,2048]{1,0:T(8,128)(2,1)}, u32[]{:S(2)}) copy-start(bf16[32,2048]{1,0:T(8,128)(2,1)} %param.5) | copy-start | bytes 393220
  29.8 110.7 %all-to-all-start = ((bf16[2,96,2048]{1,0,2:T(2,128)(2,1)}), bf16[2,96,2048]{1,0,2:T(2,128)(2,1)S(1)}, u32[]{:S(2)}, u32[]{:S(2)}) async-start(bf16[2,96,2048]{1,0,2:T(2,128)(2,1)} %copy.11), calls=%async_computation | async-start | bytes 2097152 | tf_op jit(solution)/shard_map/all_to_all | solution.py:50
  36.5 0.7 copy-start.4
  39.3 41.8 %collective-permute-start.5 = (bf16[32,2048]{1,0:T(8,128)(2,1)S(1)}, bf16[32,2048]{1,0:T(8,128)(2,1)S(1)}, u32[]{:S(2)}, u32[]{:S(2)}) collective-permute-start(bf16[32,2048]{1,0:T(8,128)(2,1)S(1)} %copy-done.3), channel_id=1, source_target_pairs={{0,22},{1,23},{2,0},{3,1},{4,2},{5,3},{6,4},{7,5},{8,30},{9,31},{1... | collective-permute-start | bytes 393224 | tf_op jit(solution)/shard_map/ppermute | solution.py:27
  48.6 50.9 %collective-permute-start.6 = (bf16[32,2048]{1,0:T(8,128)(2,1)S(1)}, bf16[32,2048]{1,0:T(8,128)(2,1)S(1)}, u32[]{:S(2)}, u32[]{:S(2)}) collective-permute-start(bf16[32,2048]{1,0:T(8,128)(2,1)S(1)} %copy-done.3), channel_id=1, source_target_pairs={{0,21},{1,22},{2,23},{3,0},{4,1},{5,2},{6,3},{7,4},{8,29},{9,30},{... | collective-permute-start | bytes 393224 | tf_op jit(solution)/shard_map/ppermute | solution.py:27
  101.9 1.1 copy-start.2
  104.1 17.9 %collective-permute-start.7 = (bf16[2,256,96]{1,2,0:T(8,128)(2,1)S(1)}, bf16[2,256,96]{1,2,0:T(8,128)(2,1)S(1)}, u32[]{:S(2)}, u32[]{:S(2)}) collective-permute-start(bf16[2,256,96]{1,2,0:T(8,128)(2,1)S(1)} %get-tuple-element.10), channel_id=1, source_target_pairs={{0,1},{1,2},{2,3},{3,4},{4,5},{5,6},{6,7},{7,0},{8,9},{9,10},{10,1... | collective-permute-start | bytes 294920 | tf_op jit(solution)/shard_map/ppermute | solution.py:56
  106.1 23.8 %collective-permute-start.8 = (bf16[2,256,96]{1,2,0:T(8,128)(2,1)S(1)}, bf16[2,256,96]{1,2,0:T(8,128)(2,1)S(1)}, u32[]{:S(2)}, u32[]{:S(2)}) collective-permute-start(bf16[2,256,96]{1,2,0:T(8,128)(2,1)S(1)} %get-tuple-element.10), channel_id=1, source_target_pairs={{0,2},{1,3},{2,4},{3,5},{4,6},{5,7},{6,0},{7,1},{8,10},{9,11},{10,... | collective-permute-start | bytes 294920 | tf_op jit(solution)/shard_map/ppermute | solution.py:56
  108.1 24.3 %collective-permute-start.9 = (bf16[2,256,96]{1,2,0:T(8,128)(2,1)S(1)}, bf16[2,256,96]{1,2,0:T(8,128)(2,1)S(1)}, u32[]{:S(2)}, u32[]{:S(2)}) collective-permute-start(bf16[2,256,96]{1,2,0:T(8,128)(2,1)S(1)} %get-tuple-element.10), channel_id=1, source_target_pairs={{0,3},{1,4},{2,5},{3,6},{4,7},{5,0},{6,1},{7,2},{8,11},{9,12},{10,... | collective-permute-start | bytes 294920 | tf_op jit(solution)/shard_map/ppermute | solution.py:56
  110.0 24.4 %collective-permute-start.10 = (bf16[2,256,96]{1,2,0:T(8,128)(2,1)S(1)}, bf16[2,256,96]{1,2,0:T(8,128)(2,1)S(1)}, u32[]{:S(2)}, u32[]{:S(2)}) collective-permute-start(bf16[2,256,96]{1,2,0:T(8,128)(2,1)S(1)} %get-tuple-element.10), channel_id=1, source_target_pairs={{0,4},{1,5},{2,6},{3,7},{4,0},{5,1},{6,2},{7,3},{8,12},{9,13},{10,... | collective-permute-start | bytes 294920 | tf_op jit(solution)/shard_map/ppermute | solution.py:56
  119.2 19.7 %collective-permute-start.11 = (bf16[2,256,96]{1,2,0:T(8,128)(2,1)S(1)}, bf16[2,256,96]{1,2,0:T(8,128)(2,1)S(1)}, u32[]{:S(2)}, u32[]{:S(2)}) collective-permute-start(bf16[2,256,96]{1,2,0:T(8,128)(2,1)S(1)} %get-tuple-element.10), channel_id=1, source_target_pairs={{0,5},{1,6},{2,7},{3,0},{4,1},{5,2},{6,3},{7,4},{8,13},{9,14},{10,... | collective-permute-start | bytes 294920 | tf_op jit(solution)/shard_map/ppermute | solution.py:56
  122.1 16.9 %collective-permute-start.12 = (bf16[2,256,96]{1,2,0:T(8,128)(2,1)S(1)}, bf16[2,256,96]{1,2,0:T(8,128)(2,1)S(1)}, u32[]{:S(2)}, u32[]{:S(2)}) collective-permute-start(bf16[2,256,96]{1,2,0:T(8,128)(2,1)S(1)} %get-tuple-element.10), channel_id=1, source_target_pairs={{0,6},{1,7},{2,0},{3,1},{4,2},{5,3},{6,4},{7,5},{8,14},{9,15},{10,... | collective-permute-start | bytes 294920 | tf_op jit(solution)/shard_map/ppermute | solution.py:56
  129.9 9.1 %collective-permute-start.13 = (bf16[2,256,96]{1,2,0:T(8,128)(2,1)S(1)}, bf16[2,256,96]{1,2,0:T(8,128)(2,1)S(1)}, u32[]{:S(2)}, u32[]{:S(2)}) collective-permute-start(bf16[2,256,96]{1,2,0:T(8,128)(2,1)S(1)} %get-tuple-element.10), channel_id=1, source_target_pairs={{0,7},{1,0},{2,1},{3,2},{4,3},{5,4},{6,5},{7,6},{8,15},{9,8},{10,9... | collective-permute-start | bytes 294920 | tf_op jit(solution)/shard_map/ppermute | solution.py:56
  140.5 1.1 copy-start.1
  206.6 21.4 %all-to-all-start.3 = ((f32[8,1,8192]{2,1,0:T(1,128)}), f32[8,1,8192]{2,1,0:T(1,128)S(1)}, u32[]{:S(2)}, u32[]{:S(2)}) async-start(f32[8,1,8192]{2,1,0:T(1,128)} %broadcast_in_dim.57), calls=%async_computation.3 | async-start | bytes 524288 | tf_op jit(solution)/shard_map/all_to_all | solution.py:38

commit v3 on v2

--- a/solution.py
+++ b/solution.py
@@ -46,7 +46,14 @@
     dp_shifts = tuple(range(1, n))
 
     def shards(tokens, w_gate, w_up, w_down):
-        block_rows = gather_blocks(tokens, rings, n).reshape((-1, tokens.shape[1]))
+        c = lax.axis_index("expert") % 2
+        width = tokens.shape[1] // 2
+        part = lax.dynamic_slice_in_dim(tokens, c * width, width, axis=1)
+        mine = gather_blocks(part, rings, n).reshape((-1, width))
+        other = lax.ppermute(mine, "expert", [(i, i ^ 1) for i in range(mesh.shape["expert"])])
+        low = jnp.where(c == 0, mine, other)
+        high = jnp.where(c == 0, other, mine)
+        block_rows = jnp.concatenate([low, high], axis=1)
         down_cols = lax.all_to_all(w_down, "dp", 2, 1, tiled=True)
         gate = jnp.einsum("td,ehd->eth", block_rows, w_gate, preferred_element_type=jnp.float32)
         upward = jnp.einsum("td,ehd->eth", block_rows, w_up, preferred_element_type=jnp.float32)

time: 230 us -> 224 us (0.974)
  local copies, waits for them, and re-layouts: 16.5 us -> 8.73 us
  starting transfers between devices: 76.9 us -> 81.5 us
  blocking collectives: 62.6 us -> 59.9 us
    ppermute x7, waiting for transfers between devices: 45.1 us -> 7.94 us  [gather_blocks(): lax.ppermute(block, BOTH, pairs)]
    ppermute x7, waiting for transfers between devices: 6.49 us -> 42.6 us  [shards(): lax.ppermute(hidden, 'dp', [(i, (i + s) % n) for i in range(n)])]
    ppermute x7, starting transfers between devices: 28.2 us -> 36.1 us  [shards(): lax.ppermute(hidden, 'dp', [(i, (i + s) % n) for i in range(n)])]
    unnamed x24 -> x22, local copies, waits for them, and re-layouts: 10.3 us -> 4.4 us
    ppermute x7, starting transfers between devices: 37.3 us -> 32.6 us  [gather_blocks(): lax.ppermute(block, BOTH, pairs)]
    all_to_all x1, blocking collectives: 40.9 us -> 38.4 us  [shards(): regrouped = lax.all_to_all(features, 'expert', 1, 0, tiled=True)]
  transfers between devices with their start and end apart: 16 -> 17, of which waited for: 5 -> 8; matrix products, arithmetic and copies ran while one was open for 7% -> 3% of each run, Pallas kernels for 0% -> 0%
where the time goes in v3:
time: 224 us; the launch traced here: 223 us
  starting transfers between devices  81.5 us (36%)
  waiting for transfers between devices  66.5 us (30%)
  blocking collectives  59.9 us (27%)
  local copies, waits for them, and re-layouts  8.73 us (4%)
  other arithmetic  4.14 us (2%)
    ppermute x7, waiting for transfers between devices, shards(): lax.ppermute(hidden, 'dp', [(i, (i + s) % n) for i in range(n)])  42.6 us
    all_to_all x1, blocking collectives, shards(): regrouped = lax.all_to_all(features, 'expert', 1, 0, tiled=True)  38.4 us
    ppermute x7, starting transfers between devices, shards(): lax.ppermute(hidden, 'dp', [(i, (i + s) % n) for i in range(n)])  36.1 us
    ppermute x7, starting transfers between devices, gather_blocks(): lax.ppermute(block, BOTH, pairs)  32.6 us
    all_to_all x1, blocking collectives, all_reduce_dp(): mine = lax.all_to_all(pieces, 'dp', 0, 0, tiled=True).sum(0, keepdims=True)  21.5 us
    all_to_all x1, waiting for transfers between devices, all_reduce_dp(): return lax.all_to_all(spread, 'dp', 0, 0, tiled=True).reshape(x.shape)  15.9 us
    ppermute x7, waiting for transfers between devices, gather_blocks(): lax.ppermute(block, BOTH, pairs)  7.94 us
    all_to_all x1, starting transfers between devices, all_reduce_dp(): return lax.all_to_all(spread, 'dp', 0, 0, tiled=True).reshape(x.shape)  5.52 us
  transfers between devices with their start and end apart: 17, of which 8 were waited for; matrix products, arithmetic and copies ran while one was open for 3% of the time, Pallas kernels for 0%

profile of v3, /device:TPU:32, one launch (start us, length us, event | category | flops | bytes accessed | tf_op | source)
XLA Modules:
  0.0 222.9 jit_solution(16702046733266158411)
XLA Ops:
  0.0 0.0 copy-start
  0.0 0.9 bitcast_dynamic-update-slice_fusion.15
  0.9 3.8 %collective-permute-start = (bf16[32,1024]{1,0:T(8,128)(2,1)S(1)}, bf16[32,1024]{1,0:T(8,128)(2,1)S(1)}, u32[]{:S(2)}, u32[]{:S(2)}) collective-permute-start(bf16[32,1024]{1,0:T(8,128)(2,1)S(1)} %get-tuple-element.10), channel_id=1, source_target_pairs={{0,1},{1,2},{2,3},{3,4},{4,5},{5,6},{6,7},{7,16},{8,9},{9,10},{10,... | collective-permute-start | bytes 196616 | tf_op jit(solution)/shard_map/ppermute | solution.py:27
  4.8 6.4 %collective-permute-start.1 = (bf16[32,1024]{1,0:T(8,128)(2,1)S(1)}, bf16[32,1024]{1,0:T(8,128)(2,1)S(1)}, u32[]{:S(2)}, u32[]{:S(2)}) collective-permute-start(bf16[32,1024]{1,0:T(8,128)(2,1)S(1)} %get-tuple-element.10), channel_id=1, source_target_pairs={{0,2},{1,3},{2,4},{3,5},{4,6},{5,7},{6,16},{7,17},{8,10},{9,11},{1... | collective-permute-start | bytes 196616 | tf_op jit(solution)/shard_map/ppermute | solution.py:27
  11.2 6.5 %collective-permute-start.2 = (bf16[32,1024]{1,0:T(8,128)(2,1)S(1)}, bf16[32,1024]{1,0:T(8,128)(2,1)S(1)}, u32[]{:S(2)}, u32[]{:S(2)}) collective-permute-start(bf16[32,1024]{1,0:T(8,128)(2,1)S(1)} %get-tuple-element.10), channel_id=1, source_target_pairs={{0,3},{1,4},{2,5},{3,6},{4,7},{5,16},{6,17},{7,18},{8,11},{9,12},{... | collective-permute-start | bytes 196616 | tf_op jit(solution)/shard_map/ppermute | solution.py:27
  17.7 6.4 %collective-permute-start.3 = (bf16[32,1024]{1,0:T(8,128)(2,1)S(1)}, bf16[32,1024]{1,0:T(8,128)(2,1)S(1)}, u32[]{:S(2)}, u32[]{:S(2)}) collective-permute-start(bf16[32,1024]{1,0:T(8,128)(2,1)S(1)} %get-tuple-element.10), channel_id=1, source_target_pairs={{0,4},{1,5},{2,6},{3,7},{4,16},{5,17},{6,18},{7,19},{8,12},{9,13},... | collective-permute-start | bytes 196616 | tf_op jit(solution)/shard_map/ppermute | solution.py:27
  24.1 2.9 %collective-permute-start.4 = (bf16[32,1024]{1,0:T(8,128)(2,1)S(1)}, bf16[32,1024]{1,0:T(8,128)(2,1)S(1)}, u32[]{:S(2)}, u32[]{:S(2)}) collective-permute-start(bf16[32,1024]{1,0:T(8,128)(2,1)S(1)} %get-tuple-element.10), channel_id=1, source_target_pairs={{0,23},{1,0},{2,1},{3,2},{4,3},{5,4},{6,5},{7,6},{8,31},{9,8},{10,... | collective-permute-start | bytes 196616 | tf_op jit(solution)/shard_map/ppermute | solution.py:27
  27.0 0.7 and_select_fusion
  27.7 1.0 sort.32
  28.7 0.1 broadcast_in_dim.50
  28.8 0.1 broadcast_in_dim.51
  28.9 0.0 collective-permute-done
  28.9 4.6 %collective-permute-start.5 = (bf16[32,1024]{1,0:T(8,128)(2,1)S(1)}, bf16[32,1024]{1,0:T(8,128)(2,1)S(1)}, u32[]{:S(2)}, u32[]{:S(2)}) collective-permute-start(bf16[32,1024]{1,0:T(8,128)(2,1)S(1)} %get-tuple-element.10), channel_id=1, source_target_pairs={{0,22},{1,23},{2,0},{3,1},{4,2},{5,3},{6,4},{7,5},{8,30},{9,31},{1... | collective-permute-start | bytes 196616 | tf_op jit(solution)/shard_map/ppermute | solution.py:27
  33.5 0.0 collective-permute-done.1
  33.5 1.9 collective-permute-start.6
  35.4 0.0 collective-permute-done.2
  35.4 0.0 collective-permute-done.3
  35.5 0.0 collective-permute-done.4
  35.5 0.6 collective-permute-done.5
  36.1 7.3 %collective-permute-done.6 = bf16[32,1024]{1,0:T(8,128)(2,1)S(1)} collective-permute-done((bf16[32,1024]{1,0:T(8,128)(2,1)S(1)}, bf16[32,1024]{1,0:T(8,128)(2,1)S(1)}, u32[]{:S(2)}, u32[]{:S(2)}) %collective-permute-start.6) | collective-permute-done | bytes 65568 | tf_op jit(solution)/shard_map/ppermute | solution.py:27
  43.4 0.6 gather_fusion
  44.0 0.1 bitcast_select_fusion
  44.2 1.9 collective-permute-start.7
  46.1 0.0 copy-done.2
  46.1 2.0 copy.11
  48.1 5.4 %all-to-all-start = ((bf16[2,96,2048]{1,0,2:T(2,128)(2,1)}), bf16[2,96,2048]{1,0,2:T(2,128)(2,1)S(1)}, u32[]{:S(2)}, u32[]{:S(2)}) async-start(bf16[2,96,2048]{1,0,2:T(2,128)(2,1)} %copy.11), calls=%async_computation | async-start | bytes 2097152 | tf_op jit(solution)/shard_map/all_to_all | solution.py:57
  53.5 1.0 sort.31
  54.5 0.0 copy-start.3
  54.5 0.0 collective-permute-done.7
  54.5 0.2 broadcast_select_fusion.1
  54.7 0.9 copy-done.3
  55.6 0.5 convolution_bitcast_fusion.2
  56.1 0.5 bitcast_dynamic-update-slice_fusion.7
  56.7 3.4 %collective-permute-start.8 = (bf16[2,256,96]{1,2,0:T(8,128)(2,1)S(1)}, bf16[2,256,96]{1,2,0:T(8,128)(2,1)S(1)}, u32[]{:S(2)}, u32[]{:S(2)}) collective-permute-start(bf16[2,256,96]{1,2,0:T(8,128)(2,1)S(1)} %get-tuple-element.14), channel_id=1, source_target_pairs={{0,1},{1,2},{2,3},{3,4},{4,5},{5,6},{6,7},{7,0},{8,9},{9,10},{10,1... | collective-permute-start | bytes 294920 | tf_op jit(solution)/shard_map/ppermute | solution.py:63
  60.1 5.5 %collective-permute-start.9 = (bf16[2,256,96]{1,2,0:T(8,128)(2,1)S(1)}, bf16[2,256,96]{1,2,0:T(8,128)(2,1)S(1)}, u32[]{:S(2)}, u32[]{:S(2)}) collective-permute-start(bf16[2,256,96]{1,2,0:T(8,128)(2,1)S(1)} %get-tuple-element.14), channel_id=1, source_target_pairs={{0,2},{1,3},{2,4},{3,5},{4,6},{5,7},{6,0},{7,1},{8,10},{9,11},{10,... | collective-permute-start | bytes 294920 | tf_op jit(solution)/shard_map/ppermute | solution.py:63
  65.5 5.2 %collective-permute-start.10 = (bf16[2,256,96]{1,2,0:T(8,128)(2,1)S(1)}, bf16[2,256,96]{1,2,0:T(8,128)(2,1)S(1)}, u32[]{:S(2)}, u32[]{:S(2)}) collective-permute-start(bf16[2,256,96]{1,2,0:T(8,128)(2,1)S(1)} %get-tuple-element.14), channel_id=1, source_target_pairs={{0,3},{1,4},{2,5},{3,6},{4,7},{5,0},{6,1},{7,2},{8,11},{9,12},{10,... | collective-permute-start | bytes 294920 | tf_op jit(solution)/shard_map/ppermute | solution.py:63
  70.7 3.4 %collective-permute-start.11 = (bf16[2,256,96]{1,2,0:T(8,128)(2,1)S(1)}, bf16[2,256,96]{1,2,0:T(8,128)(2,1)S(1)}, u32[]{:S(2)}, u32[]{:S(2)}) collective-permute-start(bf16[2,256,96]{1,2,0:T(8,128)(2,1)S(1)} %get-tuple-element.14), channel_id=1, source_target_pairs={{0,4},{1,5},{2,6},{3,7},{4,0},{5,1},{6,2},{7,3},{8,12},{9,13},{10,... | collective-permute-start | bytes 294920 | tf_op jit(solution)/shard_map/ppermute | solution.py:63
  74.1 5.8 %collective-permute-start.12 = (bf16[2,256,96]{1,2,0:T(8,128)(2,1)S(1)}, bf16[2,256,96]{1,2,0:T(8,128)(2,1)S(1)}, u32[]{:S(2)}, u32[]{:S(2)}) collective-permute-start(bf16[2,256,96]{1,2,0:T(8,128)(2,1)S(1)} %get-tuple-element.14), channel_id=1, source_target_pairs={{0,5},{1,6},{2,7},{3,0},{4,1},{5,2},{6,3},{7,4},{8,13},{9,14},{10,... | collective-permute-start | bytes 294920 | tf_op jit(solution)/shard_map/ppermute | solution.py:63
  79.9 20.6 %collective-permute-done.8 = bf16[2,256,96]{1,2,0:T(8,128)(2,1)S(1)} collective-permute-done((bf16[2,256,96]{1,2,0:T(8,128)(2,1)S(1)}, bf16[2,256,96]{1,2,0:T(8,128)(2,1)S(1)}, u32[]{:S(2)}, u32[]{:S(2)}) %collective-permute-start.8) | collective-permute-done | bytes 98336 | tf_op jit(solution)/shard_map/ppermute | solution.py:63
  100.5 1.9 collective-permute-start.13
  102.5 0.2 collective-permute-done.9
  102.7 11.0 %collective-permute-start.14 = (bf16[2,256,96]{1,2,0:T(8,128)(2,1)S(1)}, bf16[2,256,96]{1,2,0:T(8,128)(2,1)S(1)}, u32[]{:S(2)}, u32[]{:S(2)}) collective-permute-start(bf16[2,256,96]{1,2,0:T(8,128)(2,1)S(1)} %get-tuple-element.14), channel_id=1, source_target_pairs={{0,7},{1,0},{2,1},{3,2},{4,3},{5,4},{6,5},{7,6},{8,15},{9,8},{10,9... | collective-permute-start | bytes 294920 | tf_op jit(solution)/shard_map/ppermute | solution.py:63
  113.7 0.0 collective-permute-done.10
  113.7 12.5 %collective-permute-done.11 = bf16[2,256,96]{1,2,0:T(8,128)(2,1)S(1)} collective-permute-done((bf16[2,256,96]{1,2,0:T(8,128)(2,1)S(1)}, bf16[2,256,96]{1,2,0:T(8,128)(2,1)S(1)}, u32[]{:S(2)}, u32[]{:S(2)}) %collective-permute-start.11) | collective-permute-done | bytes 98336 | tf_op jit(solution)/shard_map/ppermute | solution.py:63
  126.2 8.1 %collective-permute-done.12 = bf16[2,256,96]{1,2,0:T(8,128)(2,1)S(1)} collective-permute-done((bf16[2,256,96]{1,2,0:T(8,128)(2,1)S(1)}, bf16[2,256,96]{1,2,0:T(8,128)(2,1)S(1)}, u32[]{:S(2)}, u32[]{:S(2)}) %collective-permute-start.12) | collective-permute-done | bytes 98336 | tf_op jit(solution)/shard_map/ppermute | solution.py:63
  134.4 0.0 collective-permute-done.13
  134.4 1.2 collective-permute-done.14
  135.6 1.5 gather_fusion.1
  137.1 0.0 all-to-all-done
  137.1 0.7 copy.13
  137.8 0.5 copy-done.1
  138.2 0.5 fusion
  138.7 0.3 copy.14
  139.0 38.4 %all_to_all.48 = bf16[2,256,256]{2,0,1:T(2,128)(2,1)S(1)} all-to-all(bf16[2,256,256]{2,0,1:T(2,128)(2,1)S(1)} %copy.14), channel_id=1, replica_groups=mesh['expert'=64,'dp'=8] {'expert'}, dimensions={1} | all-to-all | bytes 524288 | tf_op jit(solution)/shard_map/all_to_all | solution.py:75
  177.4 0.2 copy.20
  177.5 0.1 all_to_all.40
  177.7 0.2 fusion.14
  177.9 21.5 %all_to_all.49 = f32[8,1,8192]{2,1,0:T(1,128)S(1)} all-to-all(f32[8,1,8192]{2,1,0:T(1,128)S(1)} %bitcast.81), channel_id=1, replica_groups=mesh['expert'=64,'dp'=8] {'dp'}, dimensions={0} | all-to-all | bytes 524288 | tf_op jit(solution)/shard_map/all_to_all | solution.py:36
  199.4 0.2 reduce_sum.18
  199.6 0.8 broadcast_in_dim.57
  200.4 5.5 %all-to-all-start.3 = ((f32[8,1,8192]{2,1,0:T(1,128)}), f32[8,1,8192]{2,1,0:T(1,128)S(1)}, u32[]{:S(2)}, u32[]{:S(2)}) async-start(f32[8,1,8192]{2,1,0:T(1,128)} %broadcast_in_dim.57), calls=%async_computation.3 | async-start | bytes 524288 | tf_op jit(solution)/shard_map/all_to_all | solution.py:38
  206.0 15.9 %all-to-all-done.3 = f32[8,1,8192]{2,1,0:T(1,128)S(1)} async-done(((f32[8,1,8192]{2,1,0:T(1,128)}), f32[8,1,8192]{2,1,0:T(1,128)S(1)}, u32[]{:S(2)}, u32[]{:S(2)}) %all-to-all-start.3) | async-done | bytes 262176 | tf_op jit(solution)/shard_map/all_to_all | solution.py:38
  221.9 0.1 fusion.7
  222.0 0.9 fusion.8
  (27 shorter events, 0.2 us)
Async XLA Ops:
  0.0 56.1 %copy-start = (bf16[2,96,2048]{2,1,0:T(8,128)(2,1)S(1)}, bf16[2,96,2048]{2,1,0:T(8,128)(2,1)}, u32[]{:S(2)}) copy-start(bf16[2,96,2048]{2,1,0:T(8,128)(2,1)} %param.7) | copy-start | bytes 2359300
  0.9 27.9 %collective-permute-start = (bf16[32,1024]{1,0:T(8,128)(2,1)S(1)}, bf16[32,1024]{1,0:T(8,128)(2,1)S(1)}, u32[]{:S(2)}, u32[]{:S(2)}) collective-permute-start(bf16[32,1024]{1,0:T(8,128)(2,1)S(1)} %get-tuple-element.10), channel_id=1, source_target_pairs={{0,1},{1,2},{2,3},{3,4},{4,5},{5,6},{6,7},{7,16},{8,9},{9,10},{10,... | collective-permute-start | bytes 196616 | tf_op jit(solution)/shard_map/ppermute | solution.py:27
  4.8 28.7 %collective-permute-start.1 = (bf16[32,1024]{1,0:T(8,128)(2,1)S(1)}, bf16[32,1024]{1,0:T(8,128)(2,1)S(1)}, u32[]{:S(2)}, u32[]{:S(2)}) collective-permute-start(bf16[32,1024]{1,0:T(8,128)(2,1)S(1)} %get-tuple-element.10), channel_id=1, source_target_pairs={{0,2},{1,3},{2,4},{3,5},{4,6},{5,7},{6,16},{7,17},{8,10},{9,11},{1... | collective-permute-start | bytes 196616 | tf_op jit(solution)/shard_map/ppermute | solution.py:27
  11.2 24.3 %collective-permute-start.2 = (bf16[32,1024]{1,0:T(8,128)(2,1)S(1)}, bf16[32,1024]{1,0:T(8,128)(2,1)S(1)}, u32[]{:S(2)}, u32[]{:S(2)}) collective-permute-start(bf16[32,1024]{1,0:T(8,128)(2,1)S(1)} %get-tuple-element.10), channel_id=1, source_target_pairs={{0,3},{1,4},{2,5},{3,6},{4,7},{5,16},{6,17},{7,18},{8,11},{9,12},{... | collective-permute-start | bytes 196616 | tf_op jit(solution)/shard_map/ppermute | solution.py:27
  17.7 17.7 %collective-permute-start.3 = (bf16[32,1024]{1,0:T(8,128)(2,1)S(1)}, bf16[32,1024]{1,0:T(8,128)(2,1)S(1)}, u32[]{:S(2)}, u32[]{:S(2)}) collective-permute-start(bf16[32,1024]{1,0:T(8,128)(2,1)S(1)} %get-tuple-element.10), channel_id=1, source_target_pairs={{0,4},{1,5},{2,6},{3,7},{4,16},{5,17},{6,18},{7,19},{8,12},{9,13},... | collective-permute-start | bytes 196616 | tf_op jit(solution)/shard_map/ppermute | solution.py:27
  24.1 11.4 %collective-permute-start.4 = (bf16[32,1024]{1,0:T(8,128)(2,1)S(1)}, bf16[32,1024]{1,0:T(8,128)(2,1)S(1)}, u32[]{:S(2)}, u32[]{:S(2)}) collective-permute-start(bf16[32,1024]{1,0:T(8,128)(2,1)S(1)} %get-tuple-element.10), channel_id=1, source_target_pairs={{0,23},{1,0},{2,1},{3,2},{4,3},{5,4},{6,5},{7,6},{8,31},{9,8},{10,... | collective-permute-start | bytes 196616 | tf_op jit(solution)/shard_map/ppermute | solution.py:27
  28.9 7.2 %collective-permute-start.5 = (bf16[32,1024]{1,0:T(8,128)(2,1)S(1)}, bf16[32,1024]{1,0:T(8,128)(2,1)S(1)}, u32[]{:S(2)}, u32[]{:S(2)}) collective-permute-start(bf16[32,1024]{1,0:T(8,128)(2,1)S(1)} %get-tuple-element.10), channel_id=1, source_target_pairs={{0,22},{1,23},{2,0},{3,1},{4,2},{5,3},{6,4},{7,5},{8,30},{9,31},{1... | collective-permute-start | bytes 196616 | tf_op jit(solution)/shard_map/ppermute | solution.py:27
  33.5 10.0 %collective-permute-start.6 = (bf16[32,1024]{1,0:T(8,128)(2,1)S(1)}, bf16[32,1024]{1,0:T(8,128)(2,1)S(1)}, u32[]{:S(2)}, u32[]{:S(2)}) collective-permute-start(bf16[32,1024]{1,0:T(8,128)(2,1)S(1)} %get-tuple-element.10), channel_id=1, source_target_pairs={{0,21},{1,22},{2,23},{3,0},{4,1},{5,2},{6,3},{7,4},{8,29},{9,30},{... | collective-permute-start | bytes 196616 | tf_op jit(solution)/shard_map/ppermute | solution.py:27
  43.4 2.7 %copy-start.2 = (bf16[2,96,2048]{2,1,0:T(8,128)(2,1)S(1)}, bf16[2,96,2048]{2,1,0:T(8,128)(2,1)}, u32[]{:S(2)}) copy-start(bf16[2,96,2048]{2,1,0:T(8,128)(2,1)} %param.8) | copy-start | bytes 2359300
  44.2 10.4 %collective-permute-start.7 = (bf16[256,1024]{1,0:T(8,128)(2,1)S(1)}, bf16[256,1024]{1,0:T(8,128)(2,1)S(1)}, u32[]{:S(2)}, u32[]{:S(2)}) collective-permute-start(bf16[256,1024]{1,0:T(8,128)(2,1)S(1)} %bitcast_select_fusion), channel_id=1, source_target_pairs={{0,8},{8,0},{16,24},{24,16},{32,40},{40,32},{48,56},{56,48},{64,72... | collective-permute-start | bytes 1572872 | tf_op jit(solution)/shard_map/ppermute | solution.py:53
  48.1 89.0 %all-to-all-start = ((bf16[2,96,2048]{1,0,2:T(2,128)(2,1)}), bf16[2,96,2048]{1,0,2:T(2,128)(2,1)S(1)}, u32[]{:S(2)}, u32[]{:S(2)}) async-start(bf16[2,96,2048]{1,0,2:T(2,128)(2,1)} %copy.11), calls=%async_computation | async-start | bytes 2097152 | tf_op jit(solution)/shard_map/all_to_all | solution.py:57
  54.5 1.1 copy-start.3
  56.7 43.9 %collective-permute-start.8 = (bf16[2,256,96]{1,2,0:T(8,128)(2,1)S(1)}, bf16[2,256,96]{1,2,0:T(8,128)(2,1)S(1)}, u32[]{:S(2)}, u32[]{:S(2)}) collective-permute-start(bf16[2,256,96]{1,2,0:T(8,128)(2,1)S(1)} %get-tuple-element.14), channel_id=1, source_target_pairs={{0,1},{1,2},{2,3},{3,4},{4,5},{5,6},{6,7},{7,0},{8,9},{9,10},{10,1... | collective-permute-start | bytes 294920 | tf_op jit(solution)/shard_map/ppermute | solution.py:63
  60.1 42.6 %collective-permute-start.9 = (bf16[2,256,96]{1,2,0:T(8,128)(2,1)S(1)}, bf16[2,256,96]{1,2,0:T(8,128)(2,1)S(1)}, u32[]{:S(2)}, u32[]{:S(2)}) collective-permute-start(bf16[2,256,96]{1,2,0:T(8,128)(2,1)S(1)} %get-tuple-element.14), channel_id=1, source_target_pairs={{0,2},{1,3},{2,4},{3,5},{4,6},{5,7},{6,0},{7,1},{8,10},{9,11},{10,... | collective-permute-start | bytes 294920 | tf_op jit(solution)/shard_map/ppermute | solution.py:63
  65.5 48.1 %collective-permute-start.10 = (bf16[2,256,96]{1,2,0:T(8,128)(2,1)S(1)}, bf16[2,256,96]{1,2,0:T(8,128)(2,1)S(1)}, u32[]{:S(2)}, u32[]{:S(2)}) collective-permute-start(bf16[2,256,96]{1,2,0:T(8,128)(2,1)S(1)} %get-tuple-element.14), channel_id=1, source_target_pairs={{0,3},{1,4},{2,5},{3,6},{4,7},{5,0},{6,1},{7,2},{8,11},{9,12},{10,... | collective-permute-start | bytes 294920 | tf_op jit(solution)/shard_map/ppermute | solution.py:63
  70.7 55.5 %collective-permute-start.11 = (bf16[2,256,96]{1,2,0:T(8,128)(2,1)S(1)}, bf16[2,256,96]{1,2,0:T(8,128)(2,1)S(1)}, u32[]{:S(2)}, u32[]{:S(2)}) collective-permute-start(bf16[2,256,96]{1,2,0:T(8,128)(2,1)S(1)} %get-tuple-element.14), channel_id=1, source_target_pairs={{0,4},{1,5},{2,6},{3,7},{4,0},{5,1},{6,2},{7,3},{8,12},{9,13},{10,... | collective-permute-start | bytes 294920 | tf_op jit(solution)/shard_map/ppermute | solution.py:63
  74.1 60.2 %collective-permute-start.12 = (bf16[2,256,96]{1,2,0:T(8,128)(2,1)S(1)}, bf16[2,256,96]{1,2,0:T(8,128)(2,1)S(1)}, u32[]{:S(2)}, u32[]{:S(2)}) collective-permute-start(bf16[2,256,96]{1,2,0:T(8,128)(2,1)S(1)} %get-tuple-element.14), channel_id=1, source_target_pairs={{0,5},{1,6},{2,7},{3,0},{4,1},{5,2},{6,3},{7,4},{8,13},{9,14},{10,... | collective-permute-start | bytes 294920 | tf_op jit(solution)/shard_map/ppermute | solution.py:63
  100.5 33.8 %collective-permute-start.13 = (bf16[2,256,96]{1,2,0:T(8,128)(2,1)S(1)}, bf16[2,256,96]{1,2,0:T(8,128)(2,1)S(1)}, u32[]{:S(2)}, u32[]{:S(2)}) collective-permute-start(bf16[2,256,96]{1,2,0:T(8,128)(2,1)S(1)} %get-tuple-element.14), channel_id=1, source_target_pairs={{0,6},{1,7},{2,0},{3,1},{4,2},{5,3},{6,4},{7,5},{8,14},{9,15},{10,... | collective-permute-start | bytes 294920 | tf_op jit(solution)/shard_map/ppermute | solution.py:63
  102.7 32.9 %collective-permute-start.14 = (bf16[2,256,96]{1,2,0:T(8,128)(2,1)S(1)}, bf16[2,256,96]{1,2,0:T(8,128)(2,1)S(1)}, u32[]{:S(2)}, u32[]{:S(2)}) collective-permute-start(bf16[2,256,96]{1,2,0:T(8,128)(2,1)S(1)} %get-tuple-element.14), channel_id=1, source_target_pairs={{0,7},{1,0},{2,1},{3,2},{4,3},{5,4},{6,5},{7,6},{8,15},{9,8},{10,9... | collective-permute-start | bytes 294920 | tf_op jit(solution)/shard_map/ppermute | solution.py:63
  137.1 1.1 copy-start.1
  200.4 21.4 %all-to-all-start.3 = ((f32[8,1,8192]{2,1,0:T(1,128)}), f32[8,1,8192]{2,1,0:T(1,128)S(1)}, u32[]{:S(2)}, u32[]{:S(2)}) async-start(f32[8,1,8192]{2,1,0:T(1,128)} %broadcast_in_dim.57), calls=%async_computation.3 | async-start | bytes 524288 | tf_op jit(solution)/shard_map/all_to_all | solution.py:38

commit v4 on v3

--- a/solution.py
+++ b/solution.py
@@ -31,6 +31,21 @@
     return ordered
 
 
+def doubling_gather(block, n):
+    k = lax.axis_index("dp")
+    have = block[None]
+    codes = [0]
+    step = n // 2
+    while step:
+        pairs = [(i, i ^ step) for i in range(n)]
+        have = jnp.concatenate([have, lax.ppermute(have, "dp", pairs)], axis=0)
+        codes = codes + [c ^ step for c in codes]
+        step //= 2
+    where = jnp.array(codes)
+    position = jnp.argsort(where)
+    return jnp.take(have, position[jnp.arange(n) ^ k], axis=0)
+
+
 def all_reduce_dp(x, n):
     pieces = x.reshape((n, -1))
     mine = lax.all_to_all(pieces, "dp", 0, 0, tiled=True).sum(0, keepdims=True)
@@ -58,13 +73,7 @@
         gate = jnp.einsum("td,ehd->eth", block_rows, w_gate, preferred_element_type=jnp.float32)
         upward = jnp.einsum("td,ehd->eth", block_rows, w_up, preferred_element_type=jnp.float32)
         hidden = (jax.nn.silu(gate) * upward).astype(jnp.bfloat16)
-        k = lax.axis_index("dp")
-        got = [hidden] + [
-            lax.ppermute(hidden, "dp", [(i, (i + s) % n) for i in range(n)]) for s in dp_shifts
-        ]
-        stacked = jnp.stack(got)
-        source = (k - jnp.arange(n)) % n
-        hidden_all = jnp.take(stacked, jnp.argsort(source), axis=0)
+        hidden_all = doubling_gather(hidden, n)
         outputs = jnp.einsum(
             "keth,ekhf->etf",
             hidden_all,

time: 224 us -> 220 us (0.982)
  starting transfers between devices: 81.5 us -> 56.3 us
  waiting for transfers between devices: 66.5 us -> 89 us
    ppermute x7, waiting for transfers between devices: 7.94 us -> 43.1 us  [gather_blocks(): lax.ppermute(block, BOTH, pairs)]
    ppermute x7 -> x3, starting transfers between devices: 36.1 us -> 5.76 us  [doubling_gather(): have = jnp.concatenate([have, lax.ppermute(have, 'dp', pairs)], axis=0)]
    ppermute x7 -> x3, waiting for transfers between devices: 42.6 us -> 28.1 us  [doubling_gather(): have = jnp.concatenate([have, lax.ppermute(have, 'dp', pairs)], axis=0)]
    ppermute x7, starting transfers between devices: 32.6 us -> 37.1 us  [gather_blocks(): lax.ppermute(block, BOTH, pairs)]
    unnamed x22 -> x16, local copies, waits for them, and re-layouts: 4.4 us -> 5.2 us
  transfers between devices with their start and end apart: 17 -> 13, of which waited for: 8 -> 7; matrix products, arithmetic and copies ran while one was open for 3% -> 4% of each run, Pallas kernels for 0% -> 0%
where the time goes in v4:
time: 220 us; the launch traced here: 219 us
  waiting for transfers between devices  89 us (40%)
  blocking collectives  59.7 us (27%)
  starting transfers between devices  56.3 us (26%)
  local copies, waits for them, and re-layouts  9.26 us (4%)
  other arithmetic  2.67 us (1%)
    ppermute x7, waiting for transfers between devices, gather_blocks(): lax.ppermute(block, BOTH, pairs)  43.1 us
    all_to_all x1, blocking collectives, shards(): regrouped = lax.all_to_all(features, 'expert', 1, 0, tiled=True)  40.2 us
    ppermute x7, starting transfers between devices, gather_blocks(): lax.ppermute(block, BOTH, pairs)  37.1 us
    ppermute x3, waiting for transfers between devices, doubling_gather(): have = jnp.concatenate([have, lax.ppermute(have, 'dp', pairs)], axis=0)  28.1 us
    all_to_all x1, blocking collectives, all_reduce_dp(): mine = lax.all_to_all(pieces, 'dp', 0, 0, tiled=True).sum(0, keepdims=True)  19.5 us
    all_to_all x1, waiting for transfers between devices, all_reduce_dp(): return lax.all_to_all(spread, 'dp', 0, 0, tiled=True).reshape(x.shape)  15.9 us
    all_to_all x1, starting transfers between devices, shards(): down_cols = lax.all_to_all(w_down, 'dp', 2, 1, tiled=True)  6 us
    ppermute x3, starting transfers between devices, doubling_gather(): have = jnp.concatenate([have, lax.ppermute(have, 'dp', pairs)], axis=0)  5.76 us
  transfers between devices with their start and end apart: 13, of which 7 were waited for; matrix products, arithmetic and copies ran while one was open for 4% of the time, Pallas kernels for 0%

profile of v4, /device:TPU:32, one launch (start us, length us, event | category | flops | bytes accessed | tf_op | source)
XLA Modules:
  0.0 219.1 jit_solution(19881680518710319)
XLA Ops:
  0.0 0.0 copy-start
  0.0 0.9 bitcast_dynamic-update-slice_fusion.7
  0.9 3.8 %collective-permute-start = (bf16[32,1024]{1,0:T(8,128)(2,1)S(1)}, bf16[32,1024]{1,0:T(8,128)(2,1)S(1)}, u32[]{:S(2)}, u32[]{:S(2)}) collective-permute-start(bf16[32,1024]{1,0:T(8,128)(2,1)S(1)} %get-tuple-element.10), channel_id=1, source_target_pairs={{0,1},{1,2},{2,3},{3,4},{4,5},{5,6},{6,7},{7,16},{8,9},{9,10},{10,... | collective-permute-start | bytes 196616 | tf_op jit(solution)/shard_map/ppermute | solution.py:27
  4.8 6.4 %collective-permute-start.1 = (bf16[32,1024]{1,0:T(8,128)(2,1)S(1)}, bf16[32,1024]{1,0:T(8,128)(2,1)S(1)}, u32[]{:S(2)}, u32[]{:S(2)}) collective-permute-start(bf16[32,1024]{1,0:T(8,128)(2,1)S(1)} %get-tuple-element.10), channel_id=1, source_target_pairs={{0,2},{1,3},{2,4},{3,5},{4,6},{5,7},{6,16},{7,17},{8,10},{9,11},{1... | collective-permute-start | bytes 196616 | tf_op jit(solution)/shard_map/ppermute | solution.py:27
  11.2 6.5 %collective-permute-start.2 = (bf16[32,1024]{1,0:T(8,128)(2,1)S(1)}, bf16[32,1024]{1,0:T(8,128)(2,1)S(1)}, u32[]{:S(2)}, u32[]{:S(2)}) collective-permute-start(bf16[32,1024]{1,0:T(8,128)(2,1)S(1)} %get-tuple-element.10), channel_id=1, source_target_pairs={{0,3},{1,4},{2,5},{3,6},{4,7},{5,16},{6,17},{7,18},{8,11},{9,12},{... | collective-permute-start | bytes 196616 | tf_op jit(solution)/shard_map/ppermute | solution.py:27
  17.7 6.4 %collective-permute-start.3 = (bf16[32,1024]{1,0:T(8,128)(2,1)S(1)}, bf16[32,1024]{1,0:T(8,128)(2,1)S(1)}, u32[]{:S(2)}, u32[]{:S(2)}) collective-permute-start(bf16[32,1024]{1,0:T(8,128)(2,1)S(1)} %get-tuple-element.10), channel_id=1, source_target_pairs={{0,4},{1,5},{2,6},{3,7},{4,16},{5,17},{6,18},{7,19},{8,12},{9,13},... | collective-permute-start | bytes 196616 | tf_op jit(solution)/shard_map/ppermute | solution.py:27
  24.1 2.9 %collective-permute-start.4 = (bf16[32,1024]{1,0:T(8,128)(2,1)S(1)}, bf16[32,1024]{1,0:T(8,128)(2,1)S(1)}, u32[]{:S(2)}, u32[]{:S(2)}) collective-permute-start(bf16[32,1024]{1,0:T(8,128)(2,1)S(1)} %get-tuple-element.10), channel_id=1, source_target_pairs={{0,23},{1,0},{2,1},{3,2},{4,3},{5,4},{6,5},{7,6},{8,31},{9,8},{10,... | collective-permute-start | bytes 196616 | tf_op jit(solution)/shard_map/ppermute | solution.py:27
  27.0 3.6 %copy.12 = bf16[2,96,2048]{1,0,2:T(2,128)(2,1)} copy(bf16[2,96,2048]{2,1,0:T(8,128)(2,1)} %param.9) | data formatting | bytes 1572864 | tf_op args[3]
  30.6 0.0 copy-start.3
  30.6 6.0 %all-to-all-start = ((bf16[2,96,2048]{1,0,2:T(2,128)(2,1)}), bf16[2,96,2048]{1,0,2:T(2,128)(2,1)S(1)}, u32[]{:S(2)}, u32[]{:S(2)}) async-start(bf16[2,96,2048]{1,0,2:T(2,128)(2,1)} %copy.12), calls=%async_computation | async-start | bytes 2097152 | tf_op jit(solution)/shard_map/all_to_all | solution.py:72
  36.6 0.0 copy-done.3
  36.7 1.0 sort.35
  37.6 0.1 broadcast_in_dim.52
  37.7 0.1 broadcast_in_dim.53
  37.8 0.0 collective-permute-done
  37.8 8.6 %collective-permute-start.5 = (bf16[32,1024]{1,0:T(8,128)(2,1)S(1)}, bf16[32,1024]{1,0:T(8,128)(2,1)S(1)}, u32[]{:S(2)}, u32[]{:S(2)}) collective-permute-start(bf16[32,1024]{1,0:T(8,128)(2,1)S(1)} %get-tuple-element.10), channel_id=1, source_target_pairs={{0,22},{1,23},{2,0},{3,1},{4,2},{5,3},{6,4},{7,5},{8,30},{9,31},{1... | collective-permute-start | bytes 196616 | tf_op jit(solution)/shard_map/ppermute | solution.py:27
  46.5 0.0 collective-permute-done.1
  46.5 2.5 %collective-permute-start.6 = (bf16[32,1024]{1,0:T(8,128)(2,1)S(1)}, bf16[32,1024]{1,0:T(8,128)(2,1)S(1)}, u32[]{:S(2)}, u32[]{:S(2)}) collective-permute-start(bf16[32,1024]{1,0:T(8,128)(2,1)S(1)} %get-tuple-element.10), channel_id=1, source_target_pairs={{0,21},{1,22},{2,23},{3,0},{4,1},{5,2},{6,3},{7,4},{8,29},{9,30},{... | collective-permute-start | bytes 196616 | tf_op jit(solution)/shard_map/ppermute | solution.py:27
  49.0 0.0 collective-permute-done.2
  49.0 0.0 collective-permute-done.3
  49.0 0.0 collective-permute-done.4
  49.0 24.4 %collective-permute-done.5 = bf16[32,1024]{1,0:T(8,128)(2,1)S(1)} collective-permute-done((bf16[32,1024]{1,0:T(8,128)(2,1)S(1)}, bf16[32,1024]{1,0:T(8,128)(2,1)S(1)}, u32[]{:S(2)}, u32[]{:S(2)}) %collective-permute-start.5) | collective-permute-done | bytes 65568 | tf_op jit(solution)/shard_map/ppermute | solution.py:27
  73.5 18.7 %collective-permute-done.6 = bf16[32,1024]{1,0:T(8,128)(2,1)S(1)} collective-permute-done((bf16[32,1024]{1,0:T(8,128)(2,1)S(1)}, bf16[32,1024]{1,0:T(8,128)(2,1)S(1)}, u32[]{:S(2)}, u32[]{:S(2)}) %collective-permute-start.6) | collective-permute-done | bytes 65568 | tf_op jit(solution)/shard_map/ppermute | solution.py:27
  92.2 0.6 gather_fusion.1
  92.8 0.1 bitcast_select_fusion
  92.9 1.9 collective-permute-start.7
  94.8 1.9 collective-permute-done.7
  96.7 0.2 broadcast_select_fusion.1
  96.9 0.0 copy-done
  96.9 0.0 copy-start.2
  96.9 0.5 convolution_bitcast_fusion.2
  97.4 0.6 copy-done.2
  98.0 0.0 copy-start.1
  98.0 0.5 fusion.3
  98.5 1.9 collective-permute-start.8
  100.5 10.4 %collective-permute-done.8 = bf16[1,2,256,96]{2,3,1,0:T(8,128)(2,1)S(1)} collective-permute-done((bf16[1,2,256,96]{2,3,1,0:T(8,128)(2,1)S(1)}, bf16[1,2,256,96]{2,3,1,0:T(8,128)(2,1)S(1)}, u32[]{:S(2)}, u32[]{:S(2)}) %collective-permute-start.8) | collective-permute-done | bytes 98336 | tf_op jit(solution)/shard_map/ppermute | solution.py:41
  110.9 1.9 collective-permute-start.9
  112.8 0.0 copy-done.1
  112.8 0.6 gather_fusion
  113.5 7.0 %collective-permute-done.9 = bf16[2,2,256,96]{2,3,1,0:T(8,128)(2,1)S(1)} collective-permute-done((bf16[2,2,256,96]{2,3,1,0:T(8,128)(2,1)S(1)}, bf16[2,2,256,96]{2,3,1,0:T(8,128)(2,1)S(1)}, u32[]{:S(2)}, u32[]{:S(2)}) %collective-permute-start.9) | collective-permute-done | bytes 196640 | tf_op jit(solution)/shard_map/ppermute | solution.py:41
  120.5 1.9 collective-permute-start.10
  122.5 10.7 %collective-permute-done.10 = bf16[4,2,256,96]{2,3,1,0:T(8,128)(2,1)S(1)} collective-permute-done((bf16[4,2,256,96]{2,3,1,0:T(8,128)(2,1)S(1)}, bf16[4,2,256,96]{2,3,1,0:T(8,128)(2,1)S(1)}, u32[]{:S(2)}, u32[]{:S(2)}) %collective-permute-start.10) | collective-permute-done | bytes 393248 | tf_op jit(solution)/shard_map/ppermute | solution.py:41
  133.2 0.1 pad_maximum_fusion
  133.3 0.6 gather_fusion.2
  133.9 0.0 all-to-all-done
  133.9 0.7 copy.14
  134.6 0.5 fusion
  135.1 0.3 copy.15
  135.4 40.2 %all_to_all.48 = bf16[2,256,256]{2,0,1:T(2,128)(2,1)S(1)} all-to-all(bf16[2,256,256]{2,0,1:T(2,128)(2,1)S(1)} %copy.15), channel_id=1, replica_groups=mesh['expert'=64,'dp'=8] {'expert'}, dimensions={1} | all-to-all | bytes 524288 | tf_op jit(solution)/shard_map/all_to_all | solution.py:84
  175.5 0.2 copy.21
  175.7 0.1 all_to_all.40
  175.8 0.2 fusion.16
  176.0 19.5 %all_to_all.49 = f32[8,1,8192]{2,1,0:T(1,128)S(1)} all-to-all(f32[8,1,8192]{2,1,0:T(1,128)S(1)} %bitcast.73), channel_id=1, replica_groups=mesh['expert'=64,'dp'=8] {'dp'}, dimensions={0} | all-to-all | bytes 524288 | tf_op jit(solution)/shard_map/all_to_all | solution.py:51
  195.6 0.2 reduce_sum.18
  195.8 0.8 broadcast_in_dim.59
  196.6 5.5 %all-to-all-start.3 = ((f32[8,1,8192]{2,1,0:T(1,128)}), f32[8,1,8192]{2,1,0:T(1,128)S(1)}, u32[]{:S(2)}, u32[]{:S(2)}) async-start(f32[8,1,8192]{2,1,0:T(1,128)} %broadcast_in_dim.59), calls=%async_computation.3 | async-start | bytes 524288 | tf_op jit(solution)/shard_map/all_to_all | solution.py:53
  202.2 15.9 %all-to-all-done.3 = f32[8,1,8192]{2,1,0:T(1,128)S(1)} async-done(((f32[8,1,8192]{2,1,0:T(1,128)}), f32[8,1,8192]{2,1,0:T(1,128)S(1)}, u32[]{:S(2)}, u32[]{:S(2)}) %all-to-all-start.3) | async-done | bytes 262176 | tf_op jit(solution)/shard_map/all_to_all | solution.py:53
  218.0 0.1 fusion.8
  218.2 0.9 fusion.9
  (21 shorter events, 0.2 us)
Async XLA Ops:
  0.0 96.9 %copy-start = (bf16[2,96,2048]{2,1,0:T(8,128)(2,1)S(1)}, bf16[2,96,2048]{2,1,0:T(8,128)(2,1)}, u32[]{:S(2)}) copy-start(bf16[2,96,2048]{2,1,0:T(8,128)(2,1)} %param.7) | copy-start | bytes 2359300
  0.9 36.9 %collective-permute-start = (bf16[32,1024]{1,0:T(8,128)(2,1)S(1)}, bf16[32,1024]{1,0:T(8,128)(2,1)S(1)}, u32[]{:S(2)}, u32[]{:S(2)}) collective-permute-start(bf16[32,1024]{1,0:T(8,128)(2,1)S(1)} %get-tuple-element.10), channel_id=1, source_target_pairs={{0,1},{1,2},{2,3},{3,4},{4,5},{5,6},{6,7},{7,16},{8,9},{9,10},{10,... | collective-permute-start | bytes 196616 | tf_op jit(solution)/shard_map/ppermute | solution.py:27
  4.8 41.7 %collective-permute-start.1 = (bf16[32,1024]{1,0:T(8,128)(2,1)S(1)}, bf16[32,1024]{1,0:T(8,128)(2,1)S(1)}, u32[]{:S(2)}, u32[]{:S(2)}) collective-permute-start(bf16[32,1024]{1,0:T(8,128)(2,1)S(1)} %get-tuple-element.10), channel_id=1, source_target_pairs={{0,2},{1,3},{2,4},{3,5},{4,6},{5,7},{6,16},{7,17},{8,10},{9,11},{1... | collective-permute-start | bytes 196616 | tf_op jit(solution)/shard_map/ppermute | solution.py:27
  11.2 37.8 %collective-permute-start.2 = (bf16[32,1024]{1,0:T(8,128)(2,1)S(1)}, bf16[32,1024]{1,0:T(8,128)(2,1)S(1)}, u32[]{:S(2)}, u32[]{:S(2)}) collective-permute-start(bf16[32,1024]{1,0:T(8,128)(2,1)S(1)} %get-tuple-element.10), channel_id=1, source_target_pairs={{0,3},{1,4},{2,5},{3,6},{4,7},{5,16},{6,17},{7,18},{8,11},{9,12},{... | collective-permute-start | bytes 196616 | tf_op jit(solution)/shard_map/ppermute | solution.py:27
  17.7 31.3 %collective-permute-start.3 = (bf16[32,1024]{1,0:T(8,128)(2,1)S(1)}, bf16[32,1024]{1,0:T(8,128)(2,1)S(1)}, u32[]{:S(2)}, u32[]{:S(2)}) collective-permute-start(bf16[32,1024]{1,0:T(8,128)(2,1)S(1)} %get-tuple-element.10), channel_id=1, source_target_pairs={{0,4},{1,5},{2,6},{3,7},{4,16},{5,17},{6,18},{7,19},{8,12},{9,13},... | collective-permute-start | bytes 196616 | tf_op jit(solution)/shard_map/ppermute | solution.py:27
  24.1 24.9 %collective-permute-start.4 = (bf16[32,1024]{1,0:T(8,128)(2,1)S(1)}, bf16[32,1024]{1,0:T(8,128)(2,1)S(1)}, u32[]{:S(2)}, u32[]{:S(2)}) collective-permute-start(bf16[32,1024]{1,0:T(8,128)(2,1)S(1)} %get-tuple-element.10), channel_id=1, source_target_pairs={{0,23},{1,0},{2,1},{3,2},{4,3},{5,4},{6,5},{7,6},{8,31},{9,8},{10,... | collective-permute-start | bytes 196616 | tf_op jit(solution)/shard_map/ppermute | solution.py:27
  30.6 6.0 %copy-start.3 = (s32[8]{0:T(128)S(1)}, s32[8]{0:T(128)}, u32[]{:S(2)}) copy-start(s32[8]{0:T(128)} %constant.86) | copy-start | bytes 100
  30.6 103.3 %all-to-all-start = ((bf16[2,96,2048]{1,0,2:T(2,128)(2,1)}), bf16[2,96,2048]{1,0,2:T(2,128)(2,1)S(1)}, u32[]{:S(2)}, u32[]{:S(2)}) async-start(bf16[2,96,2048]{1,0,2:T(2,128)(2,1)} %copy.12), calls=%async_computation | async-start | bytes 2097152 | tf_op jit(solution)/shard_map/all_to_all | solution.py:72
  37.8 35.6 %collective-permute-start.5 = (bf16[32,1024]{1,0:T(8,128)(2,1)S(1)}, bf16[32,1024]{1,0:T(8,128)(2,1)S(1)}, u32[]{:S(2)}, u32[]{:S(2)}) collective-permute-start(bf16[32,1024]{1,0:T(8,128)(2,1)S(1)} %get-tuple-element.10), channel_id=1, source_target_pairs={{0,22},{1,23},{2,0},{3,1},{4,2},{5,3},{6,4},{7,5},{8,30},{9,31},{1... | collective-permute-start | bytes 196616 | tf_op jit(solution)/shard_map/ppermute | solution.py:27
  46.5 45.7 %collective-permute-start.6 = (bf16[32,1024]{1,0:T(8,128)(2,1)S(1)}, bf16[32,1024]{1,0:T(8,128)(2,1)S(1)}, u32[]{:S(2)}, u32[]{:S(2)}) collective-permute-start(bf16[32,1024]{1,0:T(8,128)(2,1)S(1)} %get-tuple-element.10), channel_id=1, source_target_pairs={{0,21},{1,22},{2,23},{3,0},{4,1},{5,2},{6,3},{7,4},{8,29},{9,30},{... | collective-permute-start | bytes 196616 | tf_op jit(solution)/shard_map/ppermute | solution.py:27
  92.9 3.8 %collective-permute-start.7 = (bf16[256,1024]{1,0:T(8,128)(2,1)S(1)}, bf16[256,1024]{1,0:T(8,128)(2,1)S(1)}, u32[]{:S(2)}, u32[]{:S(2)}) collective-permute-start(bf16[256,1024]{1,0:T(8,128)(2,1)S(1)} %bitcast_select_fusion), channel_id=1, source_target_pairs={{0,8},{8,0},{16,24},{24,16},{32,40},{40,32},{48,56},{56,48},{64,72... | collective-permute-start | bytes 1572872 | tf_op jit(solution)/shard_map/ppermute | solution.py:68
  96.9 1.1 copy-start.2
  98.0 14.8 %copy-start.1 = (s32[8]{0:T(128)S(1)}, s32[8]{0:T(128)}, u32[]{:S(2)}) copy-start(s32[8]{0:T(128)} %constant.85) | copy-start | bytes 100
  98.5 12.3 %collective-permute-start.8 = (bf16[1,2,256,96]{2,3,1,0:T(8,128)(2,1)S(1)}, bf16[1,2,256,96]{2,3,1,0:T(8,128)(2,1)S(1)}, u32[]{:S(2)}, u32[]{:S(2)}) collective-permute-start(bf16[1,2,256,96]{2,3,1,0:T(8,128)(2,1)S(1)} %fusion.3), channel_id=1, source_target_pairs={{0,4},{1,5},{2,6},{3,7},{4,0},{5,1},{6,2},{7,3},{8,12},{9,13},{10,... | collective-permute-start | bytes 294920 | tf_op jit(solution)/shard_map/ppermute | solution.py:41
  110.9 9.6 %collective-permute-start.9 = (bf16[2,2,256,96]{2,3,1,0:T(8,128)(2,1)S(1)}, bf16[2,2,256,96]{2,3,1,0:T(8,128)(2,1)S(1)}, u32[]{:S(2)}, u32[]{:S(2)}) collective-permute-start(bf16[2,2,256,96]{2,3,1,0:T(8,128)(2,1)S(1)} %pad_maximum_fusion.2), channel_id=1, source_target_pairs={{0,2},{1,3},{2,0},{3,1},{4,6},{5,7},{6,4},{7,5},{8,10},{9,11},{10,... | collective-permute-start | bytes 589832 | tf_op jit(solution)/shard_map/ppermute | solution.py:41
  120.5 12.7 %collective-permute-start.10 = (bf16[4,2,256,96]{2,3,1,0:T(8,128)(2,1)S(1)}, bf16[4,2,256,96]{2,3,1,0:T(8,128)(2,1)S(1)}, u32[]{:S(2)}, u32[]{:S(2)}) collective-permute-start(bf16[4,2,256,96]{2,3,1,0:T(8,128)(2,1)S(1)} %pad_maximum_fusion.1), channel_id=1, source_target_pairs={{0,1},{1,0},{2,3},{3,2},{4,5},{5,4},{6,7},{7,6},{8,9},{9,8},{10,11... | collective-permute-start | bytes 1179656 | tf_op jit(solution)/shard_map/ppermute | solution.py:41
  196.6 21.4 %all-to-all-start.3 = ((f32[8,1,8192]{2,1,0:T(1,128)}), f32[8,1,8192]{2,1,0:T(1,128)S(1)}, u32[]{:S(2)}, u32[]{:S(2)}) async-start(f32[8,1,8192]{2,1,0:T(1,128)} %broadcast_in_dim.59), calls=%async_computation.3 | async-start | bytes 524288 | tf_op jit(solution)/shard_map/all_to_all | solution.py:53

commit v5 on v4

--- a/solution.py
+++ b/solution.py
@@ -46,6 +46,19 @@
     return jnp.take(have, position[jnp.arange(n) ^ k], axis=0)
 
 
+def transpose_blocks(w, n):
+    k = lax.axis_index("dp")
+    width = w.shape[2] // n
+    got = [lax.dynamic_slice_in_dim(w, k * width, width, axis=2)]
+    for s in range(1, n):
+        piece = lax.dynamic_slice_in_dim(w, ((k + s) % n) * width, width, axis=2)
+        got.append(lax.ppermute(piece, "dp", [(i, (i + s) % n) for i in range(n)]))
+    stacked = jnp.stack(got, axis=1)
+    source = (k - jnp.arange(n)) % n
+    ordered = jnp.take(stacked, jnp.argsort(source), axis=1)
+    return ordered.reshape(w.shape[0], -1, width)
+
+
 def all_reduce_dp(x, n):
     pieces = x.reshape((n, -1))
     mine = lax.all_to_all(pieces, "dp", 0, 0, tiled=True).sum(0, keepdims=True)
@@ -69,7 +82,7 @@
         low = jnp.where(c == 0, mine, other)
         high = jnp.where(c == 0, other, mine)
         block_rows = jnp.concatenate([low, high], axis=1)
-        down_cols = lax.all_to_all(w_down, "dp", 2, 1, tiled=True)
+        down_cols = transpose_blocks(w_down, n)
         gate = jnp.einsum("td,ehd->eth", block_rows, w_gate, preferred_element_type=jnp.float32)
         upward = jnp.einsum("td,ehd->eth", block_rows, w_up, preferred_element_type=jnp.float32)
         hidden = (jax.nn.silu(gate) * upward).astype(jnp.bfloat16)

time: 220 us -> 200 us (0.909)
  waiting for transfers between devices: 89 us -> 42.5 us
  starting transfers between devices: 56.3 us -> 83.7 us
  local copies, waits for them, and re-layouts: 9.26 us -> 6.55 us
  other arithmetic: 2.67 us -> 5.31 us
    ppermute x7, waiting for transfers between devices: 43.1 us -> 0.02 us  [gather_blocks(): lax.ppermute(block, BOTH, pairs)]
    ppermute x0 -> x7, starting transfers between devices: none -> 32.7 us  [transpose_blocks(): got.append(lax.ppermute(piece, 'dp', [(i, (i + s) % n) for i in range(n)]))]
    all_to_all x1 -> x0, starting transfers between devices: 6 us -> none  [shards(): down_cols = lax.all_to_all(w_down, 'dp', 2, 1, tiled=True)]
    ppermute x3, starting transfers between devices: 5.76 us -> 11 us  [doubling_gather(): have = jnp.concatenate([have, lax.ppermute(have, 'dp', pairs)], axis=0)]
    ppermute x7, starting transfers between devices: 37.1 us -> 32.6 us  [gather_blocks(): lax.ppermute(block, BOTH, pairs)]
    unnamed x16 -> x24, local copies, waits for them, and re-layouts: 5.2 us -> 1.71 us
  transfers between devices with their start and end apart: 13 -> 19, of which waited for: 7 -> 4; matrix products, arithmetic and copies ran while one was open for 4% -> 4% of each run, Pallas kernels for 0% -> 0%
where the time goes in v5:
time: 200 us; the launch traced here: 199 us
  starting transfers between devices  83.7 us (42%)
  blocking collectives  58.6 us (29%)
  waiting for transfers between devices  42.5 us (21%)
  local copies, waits for them, and re-layouts  6.55 us (3%)
  other arithmetic  5.31 us (3%)
    all_to_all x1, blocking collectives, shards(): regrouped = lax.all_to_all(features, 'expert', 1, 0, tiled=True)  39.1 us
    ppermute x7, starting transfers between devices, transpose_blocks(): got.append(lax.ppermute(piece, 'dp', [(i, (i + s) % n) for i in range(n)]))  32.7 us
    ppermute x7, starting transfers between devices, gather_blocks(): lax.ppermute(block, BOTH, pairs)  32.6 us
    ppermute x3, waiting for transfers between devices, doubling_gather(): have = jnp.concatenate([have, lax.ppermute(have, 'dp', pairs)], axis=0)  26.6 us
    all_to_all x1, blocking collectives, all_reduce_dp(): mine = lax.all_to_all(pieces, 'dp', 0, 0, tiled=True).sum(0, keepdims=True)  19.5 us
    all_to_all x1, waiting for transfers between devices, all_reduce_dp(): return lax.all_to_all(spread, 'dp', 0, 0, tiled=True).reshape(x.shape)  15.9 us
    ppermute x3, starting transfers between devices, doubling_gather(): have = jnp.concatenate([have, lax.ppermute(have, 'dp', pairs)], axis=0)  11 us
    all_to_all x1, starting transfers between devices, all_reduce_dp(): return lax.all_to_all(spread, 'dp', 0, 0, tiled=True).reshape(x.shape)  5.52 us
  transfers between devices with their start and end apart: 19, of which 4 were waited for; matrix products, arithmetic and copies ran while one was open for 4% of the time, Pallas kernels for 0%

profile of v5, /device:TPU:32, one launch (start us, length us, event | category | flops | bytes accessed | tf_op | source)
XLA Modules:
  0.0 199.1 jit_solution(7834840285856769042)
XLA Ops:
  0.0 1.0 bitcast_dynamic-update-slice_fusion.15
  1.0 3.8 %collective-permute-start = (bf16[32,1024]{1,0:T(8,128)(2,1)S(1)}, bf16[32,1024]{1,0:T(8,128)(2,1)S(1)}, u32[]{:S(2)}, u32[]{:S(2)}) collective-permute-start(bf16[32,1024]{1,0:T(8,128)(2,1)S(1)} %get-tuple-element.12), channel_id=1, source_target_pairs={{0,1},{1,2},{2,3},{3,4},{4,5},{5,6},{6,7},{7,16},{8,9},{9,10},{10,... | collective-permute-start | bytes 196616 | tf_op jit(solution)/shard_map/ppermute | solution.py:27
  4.8 6.4 %collective-permute-start.1 = (bf16[32,1024]{1,0:T(8,128)(2,1)S(1)}, bf16[32,1024]{1,0:T(8,128)(2,1)S(1)}, u32[]{:S(2)}, u32[]{:S(2)}) collective-permute-start(bf16[32,1024]{1,0:T(8,128)(2,1)S(1)} %get-tuple-element.12), channel_id=1, source_target_pairs={{0,2},{1,3},{2,4},{3,5},{4,6},{5,7},{6,16},{7,17},{8,10},{9,11},{1... | collective-permute-start | bytes 196616 | tf_op jit(solution)/shard_map/ppermute | solution.py:27
  11.2 6.5 %collective-permute-start.2 = (bf16[32,1024]{1,0:T(8,128)(2,1)S(1)}, bf16[32,1024]{1,0:T(8,128)(2,1)S(1)}, u32[]{:S(2)}, u32[]{:S(2)}) collective-permute-start(bf16[32,1024]{1,0:T(8,128)(2,1)S(1)} %get-tuple-element.12), channel_id=1, source_target_pairs={{0,3},{1,4},{2,5},{3,6},{4,7},{5,16},{6,17},{7,18},{8,11},{9,12},{... | collective-permute-start | bytes 196616 | tf_op jit(solution)/shard_map/ppermute | solution.py:27
  17.8 6.4 %collective-permute-start.3 = (bf16[32,1024]{1,0:T(8,128)(2,1)S(1)}, bf16[32,1024]{1,0:T(8,128)(2,1)S(1)}, u32[]{:S(2)}, u32[]{:S(2)}) collective-permute-start(bf16[32,1024]{1,0:T(8,128)(2,1)S(1)} %get-tuple-element.12), channel_id=1, source_target_pairs={{0,4},{1,5},{2,6},{3,7},{4,16},{5,17},{6,18},{7,19},{8,12},{9,13},... | collective-permute-start | bytes 196616 | tf_op jit(solution)/shard_map/ppermute | solution.py:27
  24.2 2.9 %collective-permute-start.4 = (bf16[32,1024]{1,0:T(8,128)(2,1)S(1)}, bf16[32,1024]{1,0:T(8,128)(2,1)S(1)}, u32[]{:S(2)}, u32[]{:S(2)}) collective-permute-start(bf16[32,1024]{1,0:T(8,128)(2,1)S(1)} %get-tuple-element.12), channel_id=1, source_target_pairs={{0,23},{1,0},{2,1},{3,2},{4,3},{5,4},{6,5},{7,6},{8,31},{9,8},{10,... | collective-permute-start | bytes 196616 | tf_op jit(solution)/shard_map/ppermute | solution.py:27
  27.2 0.7 and_select_fusion
  27.9 1.0 sort.49
  28.9 1.0 sort.50
  29.9 0.6 gather_fusion
  30.6 0.1 broadcast_in_dim.64
  30.6 0.1 broadcast_in_dim.65
  30.8 0.8 constant_dynamic-slice_fusion
  31.6 0.0 collective-permute-done
  31.7 4.6 %collective-permute-start.5 = (bf16[32,1024]{1,0:T(8,128)(2,1)S(1)}, bf16[32,1024]{1,0:T(8,128)(2,1)S(1)}, u32[]{:S(2)}, u32[]{:S(2)}) collective-permute-start(bf16[32,1024]{1,0:T(8,128)(2,1)S(1)} %get-tuple-element.12), channel_id=1, source_target_pairs={{0,22},{1,23},{2,0},{3,1},{4,2},{5,3},{6,4},{7,5},{8,30},{9,31},{1... | collective-permute-start | bytes 196616 | tf_op jit(solution)/shard_map/ppermute | solution.py:27
  36.2 0.0 collective-permute-done.1
  36.3 1.9 collective-permute-start.6
  38.2 0.0 collective-permute-done.2
  38.2 3.4 %collective-permute-start.11 = (bf16[2,96,256]{2,1,0:T(8,128)(2,1)}, bf16[2,96,256]{2,1,0:T(8,128)(2,1)S(1)}, u32[]{:S(2)}, u32[]{:S(2)}) collective-permute-start(bf16[2,96,256]{2,1,0:T(8,128)(2,1)} %get-tuple-element.20), channel_id=1, source_target_pairs={{0,1},{1,2},{2,3},{3,4},{4,5},{5,6},{6,7},{7,0},{8,9},{9,10},{10,1... | collective-permute-start | bytes 294920 | tf_op jit(solution)/shard_map/ppermute | solution.py:55
  41.6 0.0 collective-permute-done.3
  41.6 6.0 %collective-permute-start.12 = (bf16[2,96,256]{2,1,0:T(8,128)(2,1)}, bf16[2,96,256]{2,1,0:T(8,128)(2,1)S(1)}, u32[]{:S(2)}, u32[]{:S(2)}) collective-permute-start(bf16[2,96,256]{2,1,0:T(8,128)(2,1)} %get-tuple-element.19), channel_id=1, source_target_pairs={{0,2},{1,3},{2,4},{3,5},{4,6},{5,7},{6,0},{7,1},{8,10},{9,11},{10,... | collective-permute-start | bytes 294920 | tf_op jit(solution)/shard_map/ppermute | solution.py:55
  47.7 0.0 collective-permute-done.4
  47.7 2.6 %collective-permute-start.13 = (bf16[2,96,256]{2,1,0:T(8,128)(2,1)}, bf16[2,96,256]{2,1,0:T(8,128)(2,1)S(1)}, u32[]{:S(2)}, u32[]{:S(2)}) collective-permute-start(bf16[2,96,256]{2,1,0:T(8,128)(2,1)} %get-tuple-element.18), channel_id=1, source_target_pairs={{0,3},{1,4},{2,5},{3,6},{4,7},{5,0},{6,1},{7,2},{8,11},{9,12},{10,... | collective-permute-start | bytes 294920 | tf_op jit(solution)/shard_map/ppermute | solution.py:55
  50.3 0.0 collective-permute-done.5
  50.3 5.4 %collective-permute-start.14 = (bf16[2,96,256]{2,1,0:T(8,128)(2,1)}, bf16[2,96,256]{2,1,0:T(8,128)(2,1)S(1)}, u32[]{:S(2)}, u32[]{:S(2)}) collective-permute-start(bf16[2,96,256]{2,1,0:T(8,128)(2,1)} %get-tuple-element.17), channel_id=1, source_target_pairs={{0,4},{1,5},{2,6},{3,7},{4,0},{5,1},{6,2},{7,3},{8,12},{9,13},{10,... | collective-permute-start | bytes 294920 | tf_op jit(solution)/shard_map/ppermute | solution.py:55
  55.7 0.0 collective-permute-done.6
  55.7 5.8 %collective-permute-start.15 = (bf16[2,96,256]{2,1,0:T(8,128)(2,1)}, bf16[2,96,256]{2,1,0:T(8,128)(2,1)S(1)}, u32[]{:S(2)}, u32[]{:S(2)}) collective-permute-start(bf16[2,96,256]{2,1,0:T(8,128)(2,1)} %get-tuple-element.16), channel_id=1, source_target_pairs={{0,5},{1,6},{2,7},{3,0},{4,1},{5,2},{6,3},{7,4},{8,13},{9,14},{10,... | collective-permute-start | bytes 294920 | tf_op jit(solution)/shard_map/ppermute | solution.py:55
  61.6 0.6 gather_fusion.1
  62.2 0.1 bitcast_select_fusion
  62.3 1.9 collective-permute-start.7
  64.3 0.0 collective-permute-done.12
  64.3 3.5 %collective-permute-start.16 = (bf16[2,96,256]{2,1,0:T(8,128)(2,1)S(1)}, bf16[2,96,256]{2,1,0:T(8,128)(2,1)S(1)}, u32[]{:S(2)}, u32[]{:S(2)}) collective-permute-start(bf16[2,96,256]{2,1,0:T(8,128)(2,1)S(1)} %copy-done.3), channel_id=1, source_target_pairs={{0,6},{1,7},{2,0},{3,1},{4,2},{5,3},{6,4},{7,5},{8,14},{9,15},{10,... | collective-permute-start | bytes 294920 | tf_op jit(solution)/shard_map/ppermute | solution.py:55
  67.8 6.0 %collective-permute-start.17 = (bf16[2,96,256]{2,1,0:T(8,128)(2,1)S(1)}, bf16[2,96,256]{2,1,0:T(8,128)(2,1)S(1)}, u32[]{:S(2)}, u32[]{:S(2)}) collective-permute-start(bf16[2,96,256]{2,1,0:T(8,128)(2,1)S(1)} %get-tuple-element.15), channel_id=1, source_target_pairs={{0,7},{1,0},{2,1},{3,2},{4,3},{5,4},{6,5},{7,6},{8,15},{9,8},{10,9... | collective-permute-start | bytes 294920 | tf_op jit(solution)/shard_map/ppermute | solution.py:55
  73.9 0.0 collective-permute-done.7
  73.9 0.2 broadcast_select_fusion.1
  74.1 0.0 copy-start.4
  74.1 0.5 convolution_bitcast_fusion.2
  74.6 0.6 copy-done.4
  75.2 0.5 fusion.3
  75.7 2.4 %collective-permute-start.8 = (bf16[1,2,256,96]{2,3,1,0:T(8,128)(2,1)S(1)}, bf16[1,2,256,96]{2,3,1,0:T(8,128)(2,1)S(1)}, u32[]{:S(2)}, u32[]{:S(2)}) collective-permute-start(bf16[1,2,256,96]{2,3,1,0:T(8,128)(2,1)S(1)} %fusion.3), channel_id=1, source_target_pairs={{0,4},{1,5},{2,6},{3,7},{4,0},{5,1},{6,2},{7,3},{8,12},{9,13},{10,... | collective-permute-start | bytes 294920 | tf_op jit(solution)/shard_map/ppermute | solution.py:41
  78.2 0.0 collective-permute-done.14
  78.2 9.2 %collective-permute-done.8 = bf16[1,2,256,96]{2,3,1,0:T(8,128)(2,1)S(1)} collective-permute-done((bf16[1,2,256,96]{2,3,1,0:T(8,128)(2,1)S(1)}, bf16[1,2,256,96]{2,3,1,0:T(8,128)(2,1)S(1)}, u32[]{:S(2)}, u32[]{:S(2)}) %collective-permute-start.8) | collective-permute-done | bytes 98336 | tf_op jit(solution)/shard_map/ppermute | solution.py:41
  87.4 3.0 %collective-permute-start.9 = (bf16[2,2,256,96]{2,3,1,0:T(8,128)(2,1)S(1)}, bf16[2,2,256,96]{2,3,1,0:T(8,128)(2,1)S(1)}, u32[]{:S(2)}, u32[]{:S(2)}) collective-permute-start(bf16[2,2,256,96]{2,3,1,0:T(8,128)(2,1)S(1)} %pad_maximum_fusion.2), channel_id=1, source_target_pairs={{0,2},{1,3},{2,0},{3,1},{4,6},{5,7},{6,4},{7,5},{8,10},{9,11},{10,... | collective-permute-start | bytes 589832 | tf_op jit(solution)/shard_map/ppermute | solution.py:41
  90.5 8.6 %collective-permute-done.9 = bf16[2,2,256,96]{2,3,1,0:T(8,128)(2,1)S(1)} collective-permute-done((bf16[2,2,256,96]{2,3,1,0:T(8,128)(2,1)S(1)}, bf16[2,2,256,96]{2,3,1,0:T(8,128)(2,1)S(1)}, u32[]{:S(2)}, u32[]{:S(2)}) %collective-permute-start.9) | collective-permute-done | bytes 196640 | tf_op jit(solution)/shard_map/ppermute | solution.py:41
  99.1 5.5 %collective-permute-start.10 = (bf16[4,2,256,96]{2,3,1,0:T(8,128)(2,1)S(1)}, bf16[4,2,256,96]{2,3,1,0:T(8,128)(2,1)}, u32[]{:S(2)}, u32[]{:S(2)}) collective-permute-start(bf16[4,2,256,96]{2,3,1,0:T(8,128)(2,1)S(1)} %pad_maximum_fusion.1), channel_id=1, source_target_pairs={{0,1},{1,0},{2,3},{3,2},{4,5},{5,4},{6,7},{7,6},{8,9},{9,8},{10,11... | collective-permute-start | bytes 1179656 | tf_op jit(solution)/shard_map/ppermute | solution.py:41
  104.6 0.0 collective-permute-done.16
  104.7 0.0 collective-permute-done.17
  104.7 0.6 gather_fusion.3
  105.3 8.7 %collective-permute-done.10 = bf16[4,2,256,96]{2,3,1,0:T(8,128)(2,1)} collective-permute-done((bf16[4,2,256,96]{2,3,1,0:T(8,128)(2,1)S(1)}, bf16[4,2,256,96]{2,3,1,0:T(8,128)(2,1)}, u32[]{:S(2)}, u32[]{:S(2)}) %collective-permute-start.10) | collective-permute-done | bytes 393248 | tf_op jit(solution)/shard_map/ppermute | solution.py:41
  114.0 1.1 pad_maximum_fusion
  115.1 0.6 gather_fusion.2
  115.7 0.5 fusion
  116.2 0.3 copy.13
  116.5 39.1 %all_to_all.33 = bf16[2,256,256]{2,0,1:T(2,128)(2,1)S(1)} all-to-all(bf16[2,256,256]{2,0,1:T(2,128)(2,1)S(1)} %copy.13), channel_id=1, replica_groups=mesh['expert'=64,'dp'=8] {'expert'}, dimensions={1} | all-to-all | bytes 524288 | tf_op jit(solution)/shard_map/all_to_all | solution.py:97
  155.6 0.2 copy.17
  155.8 0.1 all_to_all.26
  155.9 0.2 fusion.20
  156.1 19.5 %all_to_all.34 = f32[8,1,8192]{2,1,0:T(1,128)S(1)} all-to-all(f32[8,1,8192]{2,1,0:T(1,128)S(1)} %bitcast.87), channel_id=1, replica_groups=mesh['expert'=64,'dp'=8] {'dp'}, dimensions={0} | all-to-all | bytes 524288 | tf_op jit(solution)/shard_map/all_to_all | solution.py:64
  175.7 0.2 reduce_sum.18
  175.9 0.8 broadcast_in_dim.74
  176.7 5.5 %all-to-all-start.2 = ((f32[8,1,8192]{2,1,0:T(1,128)}), f32[8,1,8192]{2,1,0:T(1,128)S(1)}, u32[]{:S(2)}, u32[]{:S(2)}) async-start(f32[8,1,8192]{2,1,0:T(1,128)} %broadcast_in_dim.74), calls=%async_computation.2 | async-start | bytes 524288 | tf_op jit(solution)/shard_map/all_to_all | solution.py:66
  182.2 15.9 %all-to-all-done.2 = f32[8,1,8192]{2,1,0:T(1,128)S(1)} async-done(((f32[8,1,8192]{2,1,0:T(1,128)}), f32[8,1,8192]{2,1,0:T(1,128)S(1)}, u32[]{:S(2)}, u32[]{:S(2)}) %all-to-all-start.2) | async-done | bytes 262176 | tf_op jit(solution)/shard_map/all_to_all | solution.py:66
  198.1 0.1 fusion.11
  198.3 0.9 fusion.12
  (43 shorter events, 0.3 us)
Async XLA Ops:
  0.0 74.0 %copy-start = (bf16[2,96,2048]{2,1,0:T(8,128)(2,1)S(1)}, bf16[2,96,2048]{2,1,0:T(8,128)(2,1)}, u32[]{:S(2)}) copy-start(bf16[2,96,2048]{2,1,0:T(8,128)(2,1)} %param.7) | copy-start | bytes 2359300
  0.0 29.9 %copy-start.1 = (s32[8]{0:T(128)S(1)}, s32[8]{0:T(128)}, u32[]{:S(2)}) copy-start(s32[8]{0:T(128)} %constant.142) | copy-start | bytes 100
  0.0 30.7 %copy-start.2 = (bf16[2,96,2048]{2,1,0:T(8,128)(2,1)S(1)}, bf16[2,96,2048]{2,1,0:T(8,128)(2,1)}, u32[]{:S(2)}) copy-start(bf16[2,96,2048]{2,1,0:T(8,128)(2,1)} %param.9) | copy-start | bytes 2359300
  1.0 30.6 %collective-permute-start = (bf16[32,1024]{1,0:T(8,128)(2,1)S(1)}, bf16[32,1024]{1,0:T(8,128)(2,1)S(1)}, u32[]{:S(2)}, u32[]{:S(2)}) collective-permute-start(bf16[32,1024]{1,0:T(8,128)(2,1)S(1)} %get-tuple-element.12), channel_id=1, source_target_pairs={{0,1},{1,2},{2,3},{3,4},{4,5},{5,6},{6,7},{7,16},{8,9},{9,10},{10,... | collective-permute-start | bytes 196616 | tf_op jit(solution)/shard_map/ppermute | solution.py:27
  4.8 31.4 %collective-permute-start.1 = (bf16[32,1024]{1,0:T(8,128)(2,1)S(1)}, bf16[32,1024]{1,0:T(8,128)(2,1)S(1)}, u32[]{:S(2)}, u32[]{:S(2)}) collective-permute-start(bf16[32,1024]{1,0:T(8,128)(2,1)S(1)} %get-tuple-element.12), channel_id=1, source_target_pairs={{0,2},{1,3},{2,4},{3,5},{4,6},{5,7},{6,16},{7,17},{8,10},{9,11},{1... | collective-permute-start | bytes 196616 | tf_op jit(solution)/shard_map/ppermute | solution.py:27
  11.2 27.0 %collective-permute-start.2 = (bf16[32,1024]{1,0:T(8,128)(2,1)S(1)}, bf16[32,1024]{1,0:T(8,128)(2,1)S(1)}, u32[]{:S(2)}, u32[]{:S(2)}) collective-permute-start(bf16[32,1024]{1,0:T(8,128)(2,1)S(1)} %get-tuple-element.12), channel_id=1, source_target_pairs={{0,3},{1,4},{2,5},{3,6},{4,7},{5,16},{6,17},{7,18},{8,11},{9,12},{... | collective-permute-start | bytes 196616 | tf_op jit(solution)/shard_map/ppermute | solution.py:27
  17.8 23.8 %collective-permute-start.3 = (bf16[32,1024]{1,0:T(8,128)(2,1)S(1)}, bf16[32,1024]{1,0:T(8,128)(2,1)S(1)}, u32[]{:S(2)}, u32[]{:S(2)}) collective-permute-start(bf16[32,1024]{1,0:T(8,128)(2,1)S(1)} %get-tuple-element.12), channel_id=1, source_target_pairs={{0,4},{1,5},{2,6},{3,7},{4,16},{5,17},{6,18},{7,19},{8,12},{9,13},... | collective-permute-start | bytes 196616 | tf_op jit(solution)/shard_map/ppermute | solution.py:27
  24.2 23.5 %collective-permute-start.4 = (bf16[32,1024]{1,0:T(8,128)(2,1)S(1)}, bf16[32,1024]{1,0:T(8,128)(2,1)S(1)}, u32[]{:S(2)}, u32[]{:S(2)}) collective-permute-start(bf16[32,1024]{1,0:T(8,128)(2,1)S(1)} %get-tuple-element.12), channel_id=1, source_target_pairs={{0,23},{1,0},{2,1},{3,2},{4,3},{5,4},{6,5},{7,6},{8,31},{9,8},{10,... | collective-permute-start | bytes 196616 | tf_op jit(solution)/shard_map/ppermute | solution.py:27
  31.7 18.7 %collective-permute-start.5 = (bf16[32,1024]{1,0:T(8,128)(2,1)S(1)}, bf16[32,1024]{1,0:T(8,128)(2,1)S(1)}, u32[]{:S(2)}, u32[]{:S(2)}) collective-permute-start(bf16[32,1024]{1,0:T(8,128)(2,1)S(1)} %get-tuple-element.12), channel_id=1, source_target_pairs={{0,22},{1,23},{2,0},{3,1},{4,2},{5,3},{6,4},{7,5},{8,30},{9,31},{1... | collective-permute-start | bytes 196616 | tf_op jit(solution)/shard_map/ppermute | solution.py:27
  36.3 19.5 %collective-permute-start.6 = (bf16[32,1024]{1,0:T(8,128)(2,1)S(1)}, bf16[32,1024]{1,0:T(8,128)(2,1)S(1)}, u32[]{:S(2)}, u32[]{:S(2)}) collective-permute-start(bf16[32,1024]{1,0:T(8,128)(2,1)S(1)} %get-tuple-element.12), channel_id=1, source_target_pairs={{0,21},{1,22},{2,23},{3,0},{4,1},{5,2},{6,3},{7,4},{8,29},{9,30},{... | collective-permute-start | bytes 196616 | tf_op jit(solution)/shard_map/ppermute | solution.py:27
  38.2 24.1 %collective-permute-start.11 = (bf16[2,96,256]{2,1,0:T(8,128)(2,1)}, bf16[2,96,256]{2,1,0:T(8,128)(2,1)S(1)}, u32[]{:S(2)}, u32[]{:S(2)}) collective-permute-start(bf16[2,96,256]{2,1,0:T(8,128)(2,1)} %get-tuple-element.20), channel_id=1, source_target_pairs={{0,1},{1,2},{2,3},{3,4},{4,5},{5,6},{6,7},{7,0},{8,9},{9,10},{10,1... | collective-permute-start | bytes 294920 | tf_op jit(solution)/shard_map/ppermute | solution.py:55
  41.6 22.7 %collective-permute-start.12 = (bf16[2,96,256]{2,1,0:T(8,128)(2,1)}, bf16[2,96,256]{2,1,0:T(8,128)(2,1)S(1)}, u32[]{:S(2)}, u32[]{:S(2)}) collective-permute-start(bf16[2,96,256]{2,1,0:T(8,128)(2,1)} %get-tuple-element.19), channel_id=1, source_target_pairs={{0,2},{1,3},{2,4},{3,5},{4,6},{5,7},{6,0},{7,1},{8,10},{9,11},{10,... | collective-permute-start | bytes 294920 | tf_op jit(solution)/shard_map/ppermute | solution.py:55
  47.7 20.1 %collective-permute-start.13 = (bf16[2,96,256]{2,1,0:T(8,128)(2,1)}, bf16[2,96,256]{2,1,0:T(8,128)(2,1)S(1)}, u32[]{:S(2)}, u32[]{:S(2)}) collective-permute-start(bf16[2,96,256]{2,1,0:T(8,128)(2,1)} %get-tuple-element.18), channel_id=1, source_target_pairs={{0,3},{1,4},{2,5},{3,6},{4,7},{5,0},{6,1},{7,2},{8,11},{9,12},{10,... | collective-permute-start | bytes 294920 | tf_op jit(solution)/shard_map/ppermute | solution.py:55
  50.3 27.8 %collective-permute-start.14 = (bf16[2,96,256]{2,1,0:T(8,128)(2,1)}, bf16[2,96,256]{2,1,0:T(8,128)(2,1)S(1)}, u32[]{:S(2)}, u32[]{:S(2)}) collective-permute-start(bf16[2,96,256]{2,1,0:T(8,128)(2,1)} %get-tuple-element.17), channel_id=1, source_target_pairs={{0,4},{1,5},{2,6},{3,7},{4,0},{5,1},{6,2},{7,3},{8,12},{9,13},{10,... | collective-permute-start | bytes 294920 | tf_op jit(solution)/shard_map/ppermute | solution.py:55
  55.7 34.7 %collective-permute-start.15 = (bf16[2,96,256]{2,1,0:T(8,128)(2,1)}, bf16[2,96,256]{2,1,0:T(8,128)(2,1)S(1)}, u32[]{:S(2)}, u32[]{:S(2)}) collective-permute-start(bf16[2,96,256]{2,1,0:T(8,128)(2,1)} %get-tuple-element.16), channel_id=1, source_target_pairs={{0,5},{1,6},{2,7},{3,0},{4,1},{5,2},{6,3},{7,4},{8,13},{9,14},{10,... | collective-permute-start | bytes 294920 | tf_op jit(solution)/shard_map/ppermute | solution.py:55
  62.2 2.1 %copy-start.3 = (bf16[2,96,256]{2,1,0:T(8,128)(2,1)S(1)}, bf16[2,96,256]{2,1,0:T(8,128)(2,1)}, u32[]{:S(2)}) copy-start(bf16[2,96,256]{2,1,0:T(8,128)(2,1)} %get-tuple-element.21) | copy-start | bytes 294916
  62.3 11.5 %collective-permute-start.7 = (bf16[256,1024]{1,0:T(8,128)(2,1)S(1)}, bf16[256,1024]{1,0:T(8,128)(2,1)S(1)}, u32[]{:S(2)}, u32[]{:S(2)}) collective-permute-start(bf16[256,1024]{1,0:T(8,128)(2,1)S(1)} %bitcast_select_fusion), channel_id=1, source_target_pairs={{0,8},{8,0},{16,24},{24,16},{32,40},{40,32},{48,56},{56,48},{64,72... | collective-permute-start | bytes 1572872 | tf_op jit(solution)/shard_map/ppermute | solution.py:81
  64.3 40.4 %collective-permute-start.16 = (bf16[2,96,256]{2,1,0:T(8,128)(2,1)S(1)}, bf16[2,96,256]{2,1,0:T(8,128)(2,1)S(1)}, u32[]{:S(2)}, u32[]{:S(2)}) collective-permute-start(bf16[2,96,256]{2,1,0:T(8,128)(2,1)S(1)} %copy-done.3), channel_id=1, source_target_pairs={{0,6},{1,7},{2,0},{3,1},{4,2},{5,3},{6,4},{7,5},{8,14},{9,15},{10,... | collective-permute-start | bytes 294920 | tf_op jit(solution)/shard_map/ppermute | solution.py:55
  67.8 36.9 %collective-permute-start.17 = (bf16[2,96,256]{2,1,0:T(8,128)(2,1)S(1)}, bf16[2,96,256]{2,1,0:T(8,128)(2,1)S(1)}, u32[]{:S(2)}, u32[]{:S(2)}) collective-permute-start(bf16[2,96,256]{2,1,0:T(8,128)(2,1)S(1)} %get-tuple-element.15), channel_id=1, source_target_pairs={{0,7},{1,0},{2,1},{3,2},{4,3},{5,4},{6,5},{7,6},{8,15},{9,8},{10,9... | collective-permute-start | bytes 294920 | tf_op jit(solution)/shard_map/ppermute | solution.py:55
  74.1 1.1 copy-start.4
  75.7 11.7 %collective-permute-start.8 = (bf16[1,2,256,96]{2,3,1,0:T(8,128)(2,1)S(1)}, bf16[1,2,256,96]{2,3,1,0:T(8,128)(2,1)S(1)}, u32[]{:S(2)}, u32[]{:S(2)}) collective-permute-start(bf16[1,2,256,96]{2,3,1,0:T(8,128)(2,1)S(1)} %fusion.3), channel_id=1, source_target_pairs={{0,4},{1,5},{2,6},{3,7},{4,0},{5,1},{6,2},{7,3},{8,12},{9,13},{10,... | collective-permute-start | bytes 294920 | tf_op jit(solution)/shard_map/ppermute | solution.py:41
  87.4 11.6 %collective-permute-start.9 = (bf16[2,2,256,96]{2,3,1,0:T(8,128)(2,1)S(1)}, bf16[2,2,256,96]{2,3,1,0:T(8,128)(2,1)S(1)}, u32[]{:S(2)}, u32[]{:S(2)}) collective-permute-start(bf16[2,2,256,96]{2,3,1,0:T(8,128)(2,1)S(1)} %pad_maximum_fusion.2), channel_id=1, source_target_pairs={{0,2},{1,3},{2,0},{3,1},{4,6},{5,7},{6,4},{7,5},{8,10},{9,11},{10,... | collective-permute-start | bytes 589832 | tf_op jit(solution)/shard_map/ppermute | solution.py:41
  99.1 14.9 %collective-permute-start.10 = (bf16[4,2,256,96]{2,3,1,0:T(8,128)(2,1)S(1)}, bf16[4,2,256,96]{2,3,1,0:T(8,128)(2,1)}, u32[]{:S(2)}, u32[]{:S(2)}) collective-permute-start(bf16[4,2,256,96]{2,3,1,0:T(8,128)(2,1)S(1)} %pad_maximum_fusion.1), channel_id=1, source_target_pairs={{0,1},{1,0},{2,3},{3,2},{4,5},{5,4},{6,7},{7,6},{8,9},{9,8},{10,11... | collective-permute-start | bytes 1179656 | tf_op jit(solution)/shard_map/ppermute | solution.py:41
  176.7 21.4 %all-to-all-start.2 = ((f32[8,1,8192]{2,1,0:T(1,128)}), f32[8,1,8192]{2,1,0:T(1,128)S(1)}, u32[]{:S(2)}, u32[]{:S(2)}) async-start(f32[8,1,8192]{2,1,0:T(1,128)} %broadcast_in_dim.74), calls=%async_computation.2 | async-start | bytes 524288 | tf_op jit(solution)/shard_map/all_to_all | solution.py:66

commit v6 on v5

--- a/solution.py
+++ b/solution.py
@@ -71,9 +71,8 @@
     half = n // 2
     shifts = tuple(range(1, half + 1)) + tuple(-s for s in range(1, n - half))
     rings = tuple((s, z_ring_pairs(mesh, s)) for s in shifts)
-    dp_shifts = tuple(range(1, n))
 
-    def shards(tokens, w_gate, w_up, w_down):
+    def body(tokens, w_gate, w_up, w_down):
         c = lax.axis_index("expert") % 2
         width = tokens.shape[1] // 2
         part = lax.dynamic_slice_in_dim(tokens, c * width, width, axis=1)
@@ -104,7 +103,7 @@
         inverse = lax.rsqrt(diagonal + 1e-06)
         return gram * inverse[:, :, None] * inverse[:, None, :]
 
-    return shards
+    return body
 
 
 def solution(mesh):

time: 200 us -> 200 us (level)
  no operation moved by 1% of the time
where the time goes in v6:
time: 200 us; the launch traced here: 199 us
  starting transfers between devices  83.7 us (42%)
  blocking collectives  58.6 us (29%)
  waiting for transfers between devices  42.5 us (21%)
  local copies, waits for them, and re-layouts  6.55 us (3%)
  other arithmetic  5.31 us (3%)
    all_to_all x1, blocking collectives, body(): regrouped = lax.all_to_all(features, 'expert', 1, 0, tiled=True)  39.1 us
    ppermute x7, starting transfers between devices, transpose_blocks(): got.append(lax.ppermute(piece, 'dp', [(i, (i + s) % n) for i in range(n)]))  32.7 us
    ppermute x7, starting transfers between devices, gather_blocks(): lax.ppermute(block, BOTH, pairs)  32.6 us
    ppermute x3, waiting for transfers between devices, doubling_gather(): have = jnp.concatenate([have, lax.ppermute(have, 'dp', pairs)], axis=0)  26.6 us
    all_to_all x1, blocking collectives, all_reduce_dp(): mine = lax.all_to_all(pieces, 'dp', 0, 0, tiled=True).sum(0, keepdims=True)  19.5 us
    all_to_all x1, waiting for transfers between devices, all_reduce_dp(): return lax.all_to_all(spread, 'dp', 0, 0, tiled=True).reshape(x.shape)  15.9 us
    ppermute x3, starting transfers between devices, doubling_gather(): have = jnp.concatenate([have, lax.ppermute(have, 'dp', pairs)], axis=0)  11 us
    all_to_all x1, starting transfers between devices, all_reduce_dp(): return lax.all_to_all(spread, 'dp', 0, 0, tiled=True).reshape(x.shape)  5.52 us
  transfers between devices with their start and end apart: 19, of which 4 were waited for; matrix products, arithmetic and copies ran while one was open for 4% of the time, Pallas kernels for 0%

profile of v6, /device:TPU:32, one launch (start us, length us, event | category | flops | bytes accessed | tf_op | source)
XLA Modules:
  0.0 199.1 jit_solution(7834840285856769042)
XLA Ops:
  0.0 1.0 bitcast_dynamic-update-slice_fusion.15
  1.0 3.8 %collective-permute-start = (bf16[32,1024]{1,0:T(8,128)(2,1)S(1)}, bf16[32,1024]{1,0:T(8,128)(2,1)S(1)}, u32[]{:S(2)}, u32[]{:S(2)}) collective-permute-start(bf16[32,1024]{1,0:T(8,128)(2,1)S(1)} %get-tuple-element.12), channel_id=1, source_target_pairs={{0,1},{1,2},{2,3},{3,4},{4,5},{5,6},{6,7},{7,16},{8,9},{9,10},{10,... | collective-permute-start | bytes 196616 | tf_op jit(solution)/shard_map/ppermute | solution.py:27
  4.8 6.4 %collective-permute-start.1 = (bf16[32,1024]{1,0:T(8,128)(2,1)S(1)}, bf16[32,1024]{1,0:T(8,128)(2,1)S(1)}, u32[]{:S(2)}, u32[]{:S(2)}) collective-permute-start(bf16[32,1024]{1,0:T(8,128)(2,1)S(1)} %get-tuple-element.12), channel_id=1, source_target_pairs={{0,2},{1,3},{2,4},{3,5},{4,6},{5,7},{6,16},{7,17},{8,10},{9,11},{1... | collective-permute-start | bytes 196616 | tf_op jit(solution)/shard_map/ppermute | solution.py:27
  11.2 6.5 %collective-permute-start.2 = (bf16[32,1024]{1,0:T(8,128)(2,1)S(1)}, bf16[32,1024]{1,0:T(8,128)(2,1)S(1)}, u32[]{:S(2)}, u32[]{:S(2)}) collective-permute-start(bf16[32,1024]{1,0:T(8,128)(2,1)S(1)} %get-tuple-element.12), channel_id=1, source_target_pairs={{0,3},{1,4},{2,5},{3,6},{4,7},{5,16},{6,17},{7,18},{8,11},{9,12},{... | collective-permute-start | bytes 196616 | tf_op jit(solution)/shard_map/ppermute | solution.py:27
  17.8 6.4 %collective-permute-start.3 = (bf16[32,1024]{1,0:T(8,128)(2,1)S(1)}, bf16[32,1024]{1,0:T(8,128)(2,1)S(1)}, u32[]{:S(2)}, u32[]{:S(2)}) collective-permute-start(bf16[32,1024]{1,0:T(8,128)(2,1)S(1)} %get-tuple-element.12), channel_id=1, source_target_pairs={{0,4},{1,5},{2,6},{3,7},{4,16},{5,17},{6,18},{7,19},{8,12},{9,13},... | collective-permute-start | bytes 196616 | tf_op jit(solution)/shard_map/ppermute | solution.py:27
  24.2 2.9 %collective-permute-start.4 = (bf16[32,1024]{1,0:T(8,128)(2,1)S(1)}, bf16[32,1024]{1,0:T(8,128)(2,1)S(1)}, u32[]{:S(2)}, u32[]{:S(2)}) collective-permute-start(bf16[32,1024]{1,0:T(8,128)(2,1)S(1)} %get-tuple-element.12), channel_id=1, source_target_pairs={{0,23},{1,0},{2,1},{3,2},{4,3},{5,4},{6,5},{7,6},{8,31},{9,8},{10,... | collective-permute-start | bytes 196616 | tf_op jit(solution)/shard_map/ppermute | solution.py:27
  27.2 0.7 and_select_fusion
  27.9 1.0 sort.49
  28.9 1.0 sort.50
  29.9 0.6 gather_fusion
  30.6 0.1 broadcast_in_dim.64
  30.6 0.1 broadcast_in_dim.65
  30.8 0.8 constant_dynamic-slice_fusion
  31.6 0.0 collective-permute-done
  31.7 4.6 %collective-permute-start.5 = (bf16[32,1024]{1,0:T(8,128)(2,1)S(1)}, bf16[32,1024]{1,0:T(8,128)(2,1)S(1)}, u32[]{:S(2)}, u32[]{:S(2)}) collective-permute-start(bf16[32,1024]{1,0:T(8,128)(2,1)S(1)} %get-tuple-element.12), channel_id=1, source_target_pairs={{0,22},{1,23},{2,0},{3,1},{4,2},{5,3},{6,4},{7,5},{8,30},{9,31},{1... | collective-permute-start | bytes 196616 | tf_op jit(solution)/shard_map/ppermute | solution.py:27
  36.2 0.0 collective-permute-done.1
  36.3 1.9 collective-permute-start.6
  38.2 0.0 collective-permute-done.2
  38.2 3.4 %collective-permute-start.11 = (bf16[2,96,256]{2,1,0:T(8,128)(2,1)}, bf16[2,96,256]{2,1,0:T(8,128)(2,1)S(1)}, u32[]{:S(2)}, u32[]{:S(2)}) collective-permute-start(bf16[2,96,256]{2,1,0:T(8,128)(2,1)} %get-tuple-element.20), channel_id=1, source_target_pairs={{0,1},{1,2},{2,3},{3,4},{4,5},{5,6},{6,7},{7,0},{8,9},{9,10},{10,1... | collective-permute-start | bytes 294920 | tf_op jit(solution)/shard_map/ppermute | solution.py:55
  41.6 0.0 collective-permute-done.3
  41.6 6.0 %collective-permute-start.12 = (bf16[2,96,256]{2,1,0:T(8,128)(2,1)}, bf16[2,96,256]{2,1,0:T(8,128)(2,1)S(1)}, u32[]{:S(2)}, u32[]{:S(2)}) collective-permute-start(bf16[2,96,256]{2,1,0:T(8,128)(2,1)} %get-tuple-element.19), channel_id=1, source_target_pairs={{0,2},{1,3},{2,4},{3,5},{4,6},{5,7},{6,0},{7,1},{8,10},{9,11},{10,... | collective-permute-start | bytes 294920 | tf_op jit(solution)/shard_map/ppermute | solution.py:55
  47.7 0.0 collective-permute-done.4
  47.7 2.6 %collective-permute-start.13 = (bf16[2,96,256]{2,1,0:T(8,128)(2,1)}, bf16[2,96,256]{2,1,0:T(8,128)(2,1)S(1)}, u32[]{:S(2)}, u32[]{:S(2)}) collective-permute-start(bf16[2,96,256]{2,1,0:T(8,128)(2,1)} %get-tuple-element.18), channel_id=1, source_target_pairs={{0,3},{1,4},{2,5},{3,6},{4,7},{5,0},{6,1},{7,2},{8,11},{9,12},{10,... | collective-permute-start | bytes 294920 | tf_op jit(solution)/shard_map/ppermute | solution.py:55
  50.3 0.0 collective-permute-done.5
  50.3 5.4 %collective-permute-start.14 = (bf16[2,96,256]{2,1,0:T(8,128)(2,1)}, bf16[2,96,256]{2,1,0:T(8,128)(2,1)S(1)}, u32[]{:S(2)}, u32[]{:S(2)}) collective-permute-start(bf16[2,96,256]{2,1,0:T(8,128)(2,1)} %get-tuple-element.17), channel_id=1, source_target_pairs={{0,4},{1,5},{2,6},{3,7},{4,0},{5,1},{6,2},{7,3},{8,12},{9,13},{10,... | collective-permute-start | bytes 294920 | tf_op jit(solution)/shard_map/ppermute | solution.py:55
  55.7 0.0 collective-permute-done.6
  55.7 5.8 %collective-permute-start.15 = (bf16[2,96,256]{2,1,0:T(8,128)(2,1)}, bf16[2,96,256]{2,1,0:T(8,128)(2,1)S(1)}, u32[]{:S(2)}, u32[]{:S(2)}) collective-permute-start(bf16[2,96,256]{2,1,0:T(8,128)(2,1)} %get-tuple-element.16), channel_id=1, source_target_pairs={{0,5},{1,6},{2,7},{3,0},{4,1},{5,2},{6,3},{7,4},{8,13},{9,14},{10,... | collective-permute-start | bytes 294920 | tf_op jit(solution)/shard_map/ppermute | solution.py:55
  61.6 0.6 gather_fusion.1
  62.2 0.1 bitcast_select_fusion
  62.3 0.0 collective-permute-done.11
  62.3 1.9 collective-permute-start.7
  64.3 0.0 collective-permute-done.12
  64.3 3.5 %collective-permute-start.16 = (bf16[2,96,256]{2,1,0:T(8,128)(2,1)S(1)}, bf16[2,96,256]{2,1,0:T(8,128)(2,1)S(1)}, u32[]{:S(2)}, u32[]{:S(2)}) collective-permute-start(bf16[2,96,256]{2,1,0:T(8,128)(2,1)S(1)} %copy-done.3), channel_id=1, source_target_pairs={{0,6},{1,7},{2,0},{3,1},{4,2},{5,3},{6,4},{7,5},{8,14},{9,15},{10,... | collective-permute-start | bytes 294920 | tf_op jit(solution)/shard_map/ppermute | solution.py:55
  67.8 0.0 collective-permute-done.13
  67.8 6.0 %collective-permute-start.17 = (bf16[2,96,256]{2,1,0:T(8,128)(2,1)S(1)}, bf16[2,96,256]{2,1,0:T(8,128)(2,1)S(1)}, u32[]{:S(2)}, u32[]{:S(2)}) collective-permute-start(bf16[2,96,256]{2,1,0:T(8,128)(2,1)S(1)} %get-tuple-element.15), channel_id=1, source_target_pairs={{0,7},{1,0},{2,1},{3,2},{4,3},{5,4},{6,5},{7,6},{8,15},{9,8},{10,9... | collective-permute-start | bytes 294920 | tf_op jit(solution)/shard_map/ppermute | solution.py:55
  73.9 0.2 broadcast_select_fusion.1
  74.1 0.0 copy-start.4
  74.1 0.5 convolution_bitcast_fusion.2
  74.6 0.6 copy-done.4
  75.2 0.5 fusion.3
  75.7 2.4 %collective-permute-start.8 = (bf16[1,2,256,96]{2,3,1,0:T(8,128)(2,1)S(1)}, bf16[1,2,256,96]{2,3,1,0:T(8,128)(2,1)S(1)}, u32[]{:S(2)}, u32[]{:S(2)}) collective-permute-start(bf16[1,2,256,96]{2,3,1,0:T(8,128)(2,1)S(1)} %fusion.3), channel_id=1, source_target_pairs={{0,4},{1,5},{2,6},{3,7},{4,0},{5,1},{6,2},{7,3},{8,12},{9,13},{10,... | collective-permute-start | bytes 294920 | tf_op jit(solution)/shard_map/ppermute | solution.py:41
  78.2 0.0 collective-permute-done.14
  78.2 9.2 %collective-permute-done.8 = bf16[1,2,256,96]{2,3,1,0:T(8,128)(2,1)S(1)} collective-permute-done((bf16[1,2,256,96]{2,3,1,0:T(8,128)(2,1)S(1)}, bf16[1,2,256,96]{2,3,1,0:T(8,128)(2,1)S(1)}, u32[]{:S(2)}, u32[]{:S(2)}) %collective-permute-start.8) | collective-permute-done | bytes 98336 | tf_op jit(solution)/shard_map/ppermute | solution.py:41
  87.4 3.0 %collective-permute-start.9 = (bf16[2,2,256,96]{2,3,1,0:T(8,128)(2,1)S(1)}, bf16[2,2,256,96]{2,3,1,0:T(8,128)(2,1)S(1)}, u32[]{:S(2)}, u32[]{:S(2)}) collective-permute-start(bf16[2,2,256,96]{2,3,1,0:T(8,128)(2,1)S(1)} %pad_maximum_fusion.2), channel_id=1, source_target_pairs={{0,2},{1,3},{2,0},{3,1},{4,6},{5,7},{6,4},{7,5},{8,10},{9,11},{10,... | collective-permute-start | bytes 589832 | tf_op jit(solution)/shard_map/ppermute | solution.py:41
  90.5 8.6 %collective-permute-done.9 = bf16[2,2,256,96]{2,3,1,0:T(8,128)(2,1)S(1)} collective-permute-done((bf16[2,2,256,96]{2,3,1,0:T(8,128)(2,1)S(1)}, bf16[2,2,256,96]{2,3,1,0:T(8,128)(2,1)S(1)}, u32[]{:S(2)}, u32[]{:S(2)}) %collective-permute-start.9) | collective-permute-done | bytes 196640 | tf_op jit(solution)/shard_map/ppermute | solution.py:41
  99.1 5.5 %collective-permute-start.10 = (bf16[4,2,256,96]{2,3,1,0:T(8,128)(2,1)S(1)}, bf16[4,2,256,96]{2,3,1,0:T(8,128)(2,1)}, u32[]{:S(2)}, u32[]{:S(2)}) collective-permute-start(bf16[4,2,256,96]{2,3,1,0:T(8,128)(2,1)S(1)} %pad_maximum_fusion.1), channel_id=1, source_target_pairs={{0,1},{1,0},{2,3},{3,2},{4,5},{5,4},{6,7},{7,6},{8,9},{9,8},{10,11... | collective-permute-start | bytes 1179656 | tf_op jit(solution)/shard_map/ppermute | solution.py:41
  104.7 0.0 collective-permute-done.17
  104.7 0.6 gather_fusion.3
  105.3 8.7 %collective-permute-done.10 = bf16[4,2,256,96]{2,3,1,0:T(8,128)(2,1)} collective-permute-done((bf16[4,2,256,96]{2,3,1,0:T(8,128)(2,1)S(1)}, bf16[4,2,256,96]{2,3,1,0:T(8,128)(2,1)}, u32[]{:S(2)}, u32[]{:S(2)}) %collective-permute-start.10) | collective-permute-done | bytes 393248 | tf_op jit(solution)/shard_map/ppermute | solution.py:41
  114.0 1.1 pad_maximum_fusion
  115.1 0.6 gather_fusion.2
  115.7 0.5 fusion
  116.2 0.3 copy.13
  116.5 39.1 %all_to_all.33 = bf16[2,256,256]{2,0,1:T(2,128)(2,1)S(1)} all-to-all(bf16[2,256,256]{2,0,1:T(2,128)(2,1)S(1)} %copy.13), channel_id=1, replica_groups=mesh['expert'=64,'dp'=8] {'expert'}, dimensions={1} | all-to-all | bytes 524288 | tf_op jit(solution)/shard_map/all_to_all | solution.py:96
  155.6 0.2 copy.17
  155.8 0.1 all_to_all.26
  155.9 0.2 fusion.20
  156.1 19.5 %all_to_all.34 = f32[8,1,8192]{2,1,0:T(1,128)S(1)} all-to-all(f32[8,1,8192]{2,1,0:T(1,128)S(1)} %bitcast.87), channel_id=1, replica_groups=mesh['expert'=64,'dp'=8] {'dp'}, dimensions={0} | all-to-all | bytes 524288 | tf_op jit(solution)/shard_map/all_to_all | solution.py:64
  175.7 0.2 reduce_sum.18
  175.9 0.8 broadcast_in_dim.74
  176.7 5.5 %all-to-all-start.2 = ((f32[8,1,8192]{2,1,0:T(1,128)}), f32[8,1,8192]{2,1,0:T(1,128)S(1)}, u32[]{:S(2)}, u32[]{:S(2)}) async-start(f32[8,1,8192]{2,1,0:T(1,128)} %broadcast_in_dim.74), calls=%async_computation.2 | async-start | bytes 524288 | tf_op jit(solution)/shard_map/all_to_all | solution.py:66
  182.2 15.9 %all-to-all-done.2 = f32[8,1,8192]{2,1,0:T(1,128)S(1)} async-done(((f32[8,1,8192]{2,1,0:T(1,128)}), f32[8,1,8192]{2,1,0:T(1,128)S(1)}, u32[]{:S(2)}, u32[]{:S(2)}) %all-to-all-start.2) | async-done | bytes 262176 | tf_op jit(solution)/shard_map/all_to_all | solution.py:66
  198.1 0.1 fusion.11
  198.3 0.9 fusion.12
  (43 shorter events, 0.3 us)
Async XLA Ops:
  0.0 74.0 %copy-start = (bf16[2,96,2048]{2,1,0:T(8,128)(2,1)S(1)}, bf16[2,96,2048]{2,1,0:T(8,128)(2,1)}, u32[]{:S(2)}) copy-start(bf16[2,96,2048]{2,1,0:T(8,128)(2,1)} %param.7) | copy-start | bytes 2359300
  0.0 29.9 %copy-start.1 = (s32[8]{0:T(128)S(1)}, s32[8]{0:T(128)}, u32[]{:S(2)}) copy-start(s32[8]{0:T(128)} %constant.142) | copy-start | bytes 100
  0.0 30.7 %copy-start.2 = (bf16[2,96,2048]{2,1,0:T(8,128)(2,1)S(1)}, bf16[2,96,2048]{2,1,0:T(8,128)(2,1)}, u32[]{:S(2)}) copy-start(bf16[2,96,2048]{2,1,0:T(8,128)(2,1)} %param.9) | copy-start | bytes 2359300
  1.0 30.6 %collective-permute-start = (bf16[32,1024]{1,0:T(8,128)(2,1)S(1)}, bf16[32,1024]{1,0:T(8,128)(2,1)S(1)}, u32[]{:S(2)}, u32[]{:S(2)}) collective-permute-start(bf16[32,1024]{1,0:T(8,128)(2,1)S(1)} %get-tuple-element.12), channel_id=1, source_target_pairs={{0,1},{1,2},{2,3},{3,4},{4,5},{5,6},{6,7},{7,16},{8,9},{9,10},{10,... | collective-permute-start | bytes 196616 | tf_op jit(solution)/shard_map/ppermute | solution.py:27
  4.8 31.4 %collective-permute-start.1 = (bf16[32,1024]{1,0:T(8,128)(2,1)S(1)}, bf16[32,1024]{1,0:T(8,128)(2,1)S(1)}, u32[]{:S(2)}, u32[]{:S(2)}) collective-permute-start(bf16[32,1024]{1,0:T(8,128)(2,1)S(1)} %get-tuple-element.12), channel_id=1, source_target_pairs={{0,2},{1,3},{2,4},{3,5},{4,6},{5,7},{6,16},{7,17},{8,10},{9,11},{1... | collective-permute-start | bytes 196616 | tf_op jit(solution)/shard_map/ppermute | solution.py:27
  11.2 27.0 %collective-permute-start.2 = (bf16[32,1024]{1,0:T(8,128)(2,1)S(1)}, bf16[32,1024]{1,0:T(8,128)(2,1)S(1)}, u32[]{:S(2)}, u32[]{:S(2)}) collective-permute-start(bf16[32,1024]{1,0:T(8,128)(2,1)S(1)} %get-tuple-element.12), channel_id=1, source_target_pairs={{0,3},{1,4},{2,5},{3,6},{4,7},{5,16},{6,17},{7,18},{8,11},{9,12},{... | collective-permute-start | bytes 196616 | tf_op jit(solution)/shard_map/ppermute | solution.py:27
  17.8 23.8 %collective-permute-start.3 = (bf16[32,1024]{1,0:T(8,128)(2,1)S(1)}, bf16[32,1024]{1,0:T(8,128)(2,1)S(1)}, u32[]{:S(2)}, u32[]{:S(2)}) collective-permute-start(bf16[32,1024]{1,0:T(8,128)(2,1)S(1)} %get-tuple-element.12), channel_id=1, source_target_pairs={{0,4},{1,5},{2,6},{3,7},{4,16},{5,17},{6,18},{7,19},{8,12},{9,13},... | collective-permute-start | bytes 196616 | tf_op jit(solution)/shard_map/ppermute | solution.py:27
  24.2 23.5 %collective-permute-start.4 = (bf16[32,1024]{1,0:T(8,128)(2,1)S(1)}, bf16[32,1024]{1,0:T(8,128)(2,1)S(1)}, u32[]{:S(2)}, u32[]{:S(2)}) collective-permute-start(bf16[32,1024]{1,0:T(8,128)(2,1)S(1)} %get-tuple-element.12), channel_id=1, source_target_pairs={{0,23},{1,0},{2,1},{3,2},{4,3},{5,4},{6,5},{7,6},{8,31},{9,8},{10,... | collective-permute-start | bytes 196616 | tf_op jit(solution)/shard_map/ppermute | solution.py:27
  31.7 18.7 %collective-permute-start.5 = (bf16[32,1024]{1,0:T(8,128)(2,1)S(1)}, bf16[32,1024]{1,0:T(8,128)(2,1)S(1)}, u32[]{:S(2)}, u32[]{:S(2)}) collective-permute-start(bf16[32,1024]{1,0:T(8,128)(2,1)S(1)} %get-tuple-element.12), channel_id=1, source_target_pairs={{0,22},{1,23},{2,0},{3,1},{4,2},{5,3},{6,4},{7,5},{8,30},{9,31},{1... | collective-permute-start | bytes 196616 | tf_op jit(solution)/shard_map/ppermute | solution.py:27
  36.3 19.5 %collective-permute-start.6 = (bf16[32,1024]{1,0:T(8,128)(2,1)S(1)}, bf16[32,1024]{1,0:T(8,128)(2,1)S(1)}, u32[]{:S(2)}, u32[]{:S(2)}) collective-permute-start(bf16[32,1024]{1,0:T(8,128)(2,1)S(1)} %get-tuple-element.12), channel_id=1, source_target_pairs={{0,21},{1,22},{2,23},{3,0},{4,1},{5,2},{6,3},{7,4},{8,29},{9,30},{... | collective-permute-start | bytes 196616 | tf_op jit(solution)/shard_map/ppermute | solution.py:27
  38.2 24.1 %collective-permute-start.11 = (bf16[2,96,256]{2,1,0:T(8,128)(2,1)}, bf16[2,96,256]{2,1,0:T(8,128)(2,1)S(1)}, u32[]{:S(2)}, u32[]{:S(2)}) collective-permute-start(bf16[2,96,256]{2,1,0:T(8,128)(2,1)} %get-tuple-element.20), channel_id=1, source_target_pairs={{0,1},{1,2},{2,3},{3,4},{4,5},{5,6},{6,7},{7,0},{8,9},{9,10},{10,1... | collective-permute-start | bytes 294920 | tf_op jit(solution)/shard_map/ppermute | solution.py:55
  41.6 22.7 %collective-permute-start.12 = (bf16[2,96,256]{2,1,0:T(8,128)(2,1)}, bf16[2,96,256]{2,1,0:T(8,128)(2,1)S(1)}, u32[]{:S(2)}, u32[]{:S(2)}) collective-permute-start(bf16[2,96,256]{2,1,0:T(8,128)(2,1)} %get-tuple-element.19), channel_id=1, source_target_pairs={{0,2},{1,3},{2,4},{3,5},{4,6},{5,7},{6,0},{7,1},{8,10},{9,11},{10,... | collective-permute-start | bytes 294920 | tf_op jit(solution)/shard_map/ppermute | solution.py:55
  47.7 20.1 %collective-permute-start.13 = (bf16[2,96,256]{2,1,0:T(8,128)(2,1)}, bf16[2,96,256]{2,1,0:T(8,128)(2,1)S(1)}, u32[]{:S(2)}, u32[]{:S(2)}) collective-permute-start(bf16[2,96,256]{2,1,0:T(8,128)(2,1)} %get-tuple-element.18), channel_id=1, source_target_pairs={{0,3},{1,4},{2,5},{3,6},{4,7},{5,0},{6,1},{7,2},{8,11},{9,12},{10,... | collective-permute-start | bytes 294920 | tf_op jit(solution)/shard_map/ppermute | solution.py:55
  50.3 27.8 %collective-permute-start.14 = (bf16[2,96,256]{2,1,0:T(8,128)(2,1)}, bf16[2,96,256]{2,1,0:T(8,128)(2,1)S(1)}, u32[]{:S(2)}, u32[]{:S(2)}) collective-permute-start(bf16[2,96,256]{2,1,0:T(8,128)(2,1)} %get-tuple-element.17), channel_id=1, source_target_pairs={{0,4},{1,5},{2,6},{3,7},{4,0},{5,1},{6,2},{7,3},{8,12},{9,13},{10,... | collective-permute-start | bytes 294920 | tf_op jit(solution)/shard_map/ppermute | solution.py:55
  55.7 34.7 %collective-permute-start.15 = (bf16[2,96,256]{2,1,0:T(8,128)(2,1)}, bf16[2,96,256]{2,1,0:T(8,128)(2,1)S(1)}, u32[]{:S(2)}, u32[]{:S(2)}) collective-permute-start(bf16[2,96,256]{2,1,0:T(8,128)(2,1)} %get-tuple-element.16), channel_id=1, source_target_pairs={{0,5},{1,6},{2,7},{3,0},{4,1},{5,2},{6,3},{7,4},{8,13},{9,14},{10,... | collective-permute-start | bytes 294920 | tf_op jit(solution)/shard_map/ppermute | solution.py:55
  62.2 2.1 %copy-start.3 = (bf16[2,96,256]{2,1,0:T(8,128)(2,1)S(1)}, bf16[2,96,256]{2,1,0:T(8,128)(2,1)}, u32[]{:S(2)}) copy-start(bf16[2,96,256]{2,1,0:T(8,128)(2,1)} %get-tuple-element.21) | copy-start | bytes 294916
  62.3 11.5 %collective-permute-start.7 = (bf16[256,1024]{1,0:T(8,128)(2,1)S(1)}, bf16[256,1024]{1,0:T(8,128)(2,1)S(1)}, u32[]{:S(2)}, u32[]{:S(2)}) collective-permute-start(bf16[256,1024]{1,0:T(8,128)(2,1)S(1)} %bitcast_select_fusion), channel_id=1, source_target_pairs={{0,8},{8,0},{16,24},{24,16},{32,40},{40,32},{48,56},{56,48},{64,72... | collective-permute-start | bytes 1572872 | tf_op jit(solution)/shard_map/ppermute | solution.py:80
  64.3 40.4 %collective-permute-start.16 = (bf16[2,96,256]{2,1,0:T(8,128)(2,1)S(1)}, bf16[2,96,256]{2,1,0:T(8,128)(2,1)S(1)}, u32[]{:S(2)}, u32[]{:S(2)}) collective-permute-start(bf16[2,96,256]{2,1,0:T(8,128)(2,1)S(1)} %copy-done.3), channel_id=1, source_target_pairs={{0,6},{1,7},{2,0},{3,1},{4,2},{5,3},{6,4},{7,5},{8,14},{9,15},{10,... | collective-permute-start | bytes 294920 | tf_op jit(solution)/shard_map/ppermute | solution.py:55
  67.8 36.9 %collective-permute-start.17 = (bf16[2,96,256]{2,1,0:T(8,128)(2,1)S(1)}, bf16[2,96,256]{2,1,0:T(8,128)(2,1)S(1)}, u32[]{:S(2)}, u32[]{:S(2)}) collective-permute-start(bf16[2,96,256]{2,1,0:T(8,128)(2,1)S(1)} %get-tuple-element.15), channel_id=1, source_target_pairs={{0,7},{1,0},{2,1},{3,2},{4,3},{5,4},{6,5},{7,6},{8,15},{9,8},{10,9... | collective-permute-start | bytes 294920 | tf_op jit(solution)/shard_map/ppermute | solution.py:55
  74.1 1.1 copy-start.4
  75.7 11.7 %collective-permute-start.8 = (bf16[1,2,256,96]{2,3,1,0:T(8,128)(2,1)S(1)}, bf16[1,2,256,96]{2,3,1,0:T(8,128)(2,1)S(1)}, u32[]{:S(2)}, u32[]{:S(2)}) collective-permute-start(bf16[1,2,256,96]{2,3,1,0:T(8,128)(2,1)S(1)} %fusion.3), channel_id=1, source_target_pairs={{0,4},{1,5},{2,6},{3,7},{4,0},{5,1},{6,2},{7,3},{8,12},{9,13},{10,... | collective-permute-start | bytes 294920 | tf_op jit(solution)/shard_map/ppermute | solution.py:41
  87.4 11.6 %collective-permute-start.9 = (bf16[2,2,256,96]{2,3,1,0:T(8,128)(2,1)S(1)}, bf16[2,2,256,96]{2,3,1,0:T(8,128)(2,1)S(1)}, u32[]{:S(2)}, u32[]{:S(2)}) collective-permute-start(bf16[2,2,256,96]{2,3,1,0:T(8,128)(2,1)S(1)} %pad_maximum_fusion.2), channel_id=1, source_target_pairs={{0,2},{1,3},{2,0},{3,1},{4,6},{5,7},{6,4},{7,5},{8,10},{9,11},{10,... | collective-permute-start | bytes 589832 | tf_op jit(solution)/shard_map/ppermute | solution.py:41
  99.1 14.9 %collective-permute-start.10 = (bf16[4,2,256,96]{2,3,1,0:T(8,128)(2,1)S(1)}, bf16[4,2,256,96]{2,3,1,0:T(8,128)(2,1)}, u32[]{:S(2)}, u32[]{:S(2)}) collective-permute-start(bf16[4,2,256,96]{2,3,1,0:T(8,128)(2,1)S(1)} %pad_maximum_fusion.1), channel_id=1, source_target_pairs={{0,1},{1,0},{2,3},{3,2},{4,5},{5,4},{6,7},{7,6},{8,9},{9,8},{10,11... | collective-permute-start | bytes 1179656 | tf_op jit(solution)/shard_map/ppermute | solution.py:41
  176.7 21.4 %all-to-all-start.2 = ((f32[8,1,8192]{2,1,0:T(1,128)}), f32[8,1,8192]{2,1,0:T(1,128)S(1)}, u32[]{:S(2)}, u32[]{:S(2)}) async-start(f32[8,1,8192]{2,1,0:T(1,128)} %broadcast_in_dim.74), calls=%async_computation.2 | async-start | bytes 524288 | tf_op jit(solution)/shard_map/all_to_all | solution.py:66

commit v7 on v6

--- a/solution.py
+++ b/solution.py
@@ -78,12 +78,16 @@
         part = lax.dynamic_slice_in_dim(tokens, c * width, width, axis=1)
         mine = gather_blocks(part, rings, n).reshape((-1, width))
         other = lax.ppermute(mine, "expert", [(i, i ^ 1) for i in range(mesh.shape["expert"])])
-        low = jnp.where(c == 0, mine, other)
-        high = jnp.where(c == 0, other, mine)
-        block_rows = jnp.concatenate([low, high], axis=1)
+
+        def half_dot(w):
+            own_w = lax.dynamic_slice_in_dim(w, c * width, width, axis=2)
+            other_w = lax.dynamic_slice_in_dim(w, (1 - c) * width, width, axis=2)
+            first = jnp.einsum("td,ehd->eth", mine, own_w, preferred_element_type=jnp.float32)
+            return first + jnp.einsum("td,ehd->eth", other, other_w, preferred_element_type=jnp.float32)
+
         down_cols = transpose_blocks(w_down, n)
-        gate = jnp.einsum("td,ehd->eth", block_rows, w_gate, preferred_element_type=jnp.float32)
-        upward = jnp.einsum("td,ehd->eth", block_rows, w_up, preferred_element_type=jnp.float32)
+        gate = half_dot(w_gate)
+        upward = half_dot(w_up)
         hidden = (jax.nn.silu(gate) * upward).astype(jnp.bfloat16)
         hidden_all = doubling_gather(hidden, n)
         outputs = jnp.einsum(

time: 200 us -> 206 us (1.030)
  local copies, waits for them, and re-layouts: 6.55 us -> 11.5 us
    unnamed x24 -> x26, local copies, waits for them, and re-layouts: 1.71 us -> 6.25 us
  transfers between devices with their start and end apart: 19 -> 19, of which waited for: 4 -> 4; matrix products, arithmetic and copies ran while one was open for 4% -> 6% of each run, Pallas kernels for 0% -> 0%
where the time goes in v7:
time: 206 us; the launch traced here: 205 us
  starting transfers between devices  83.7 us (41%)
  blocking collectives  59 us (29%)
  waiting for transfers between devices  42.5 us (21%)
  local copies, waits for them, and re-layouts  11.5 us (6%)
  other arithmetic  5.57 us (3%)
  matrix products  2.07 us (1%)
    all_to_all x1, blocking collectives, body(): regrouped = lax.all_to_all(features, 'expert', 1, 0, tiled=True)  39.4 us
    ppermute x7, starting transfers between devices, transpose_blocks(): got.append(lax.ppermute(piece, 'dp', [(i, (i + s) % n) for i in range(n)]))  32.7 us
    ppermute x7, starting transfers between devices, gather_blocks(): lax.ppermute(block, BOTH, pairs)  32.6 us
    ppermute x3, waiting for transfers between devices, doubling_gather(): have = jnp.concatenate([have, lax.ppermute(have, 'dp', pairs)], axis=0)  26.6 us
    all_to_all x1, blocking collectives, all_reduce_dp(): mine = lax.all_to_all(pieces, 'dp', 0, 0, tiled=True).sum(0, keepdims=True)  19.5 us
    all_to_all x1, waiting for transfers between devices, all_reduce_dp(): return lax.all_to_all(spread, 'dp', 0, 0, tiled=True).reshape(x.shape)  15.9 us
    ppermute x3, starting transfers between devices, doubling_gather(): have = jnp.concatenate([have, lax.ppermute(have, 'dp', pairs)], axis=0)  10.9 us
    unnamed x26, local copies, waits for them, and re-layouts  6.25 us
  transfers between devices with their start and end apart: 19, of which 4 were waited for; matrix products, arithmetic and copies ran while one was open for 6% of the time, Pallas kernels for 0%

profile of v7, /device:TPU:32, one launch (start us, length us, event | category | flops | bytes accessed | tf_op | source)
XLA Modules:
  0.0 204.9 jit_solution(15968778365494386058)
XLA Ops:
  0.0 0.9 bitcast_dynamic-update-slice_fusion.15
  0.9 3.8 %collective-permute-start = (bf16[32,1024]{1,0:T(8,128)(2,1)S(1)}, bf16[32,1024]{1,0:T(8,128)(2,1)S(1)}, u32[]{:S(2)}, u32[]{:S(2)}) collective-permute-start(bf16[32,1024]{1,0:T(8,128)(2,1)S(1)} %get-tuple-element.12), channel_id=1, source_target_pairs={{0,1},{1,2},{2,3},{3,4},{4,5},{5,6},{6,7},{7,16},{8,9},{9,10},{10,... | collective-permute-start | bytes 196616 | tf_op jit(solution)/shard_map/ppermute | solution.py:27
  4.8 6.4 %collective-permute-start.1 = (bf16[32,1024]{1,0:T(8,128)(2,1)S(1)}, bf16[32,1024]{1,0:T(8,128)(2,1)S(1)}, u32[]{:S(2)}, u32[]{:S(2)}) collective-permute-start(bf16[32,1024]{1,0:T(8,128)(2,1)S(1)} %get-tuple-element.12), channel_id=1, source_target_pairs={{0,2},{1,3},{2,4},{3,5},{4,6},{5,7},{6,16},{7,17},{8,10},{9,11},{1... | collective-permute-start | bytes 196616 | tf_op jit(solution)/shard_map/ppermute | solution.py:27
  11.2 6.5 %collective-permute-start.2 = (bf16[32,1024]{1,0:T(8,128)(2,1)S(1)}, bf16[32,1024]{1,0:T(8,128)(2,1)S(1)}, u32[]{:S(2)}, u32[]{:S(2)}) collective-permute-start(bf16[32,1024]{1,0:T(8,128)(2,1)S(1)} %get-tuple-element.12), channel_id=1, source_target_pairs={{0,3},{1,4},{2,5},{3,6},{4,7},{5,16},{6,17},{7,18},{8,11},{9,12},{... | collective-permute-start | bytes 196616 | tf_op jit(solution)/shard_map/ppermute | solution.py:27
  17.7 6.4 %collective-permute-start.3 = (bf16[32,1024]{1,0:T(8,128)(2,1)S(1)}, bf16[32,1024]{1,0:T(8,128)(2,1)S(1)}, u32[]{:S(2)}, u32[]{:S(2)}) collective-permute-start(bf16[32,1024]{1,0:T(8,128)(2,1)S(1)} %get-tuple-element.12), channel_id=1, source_target_pairs={{0,4},{1,5},{2,6},{3,7},{4,16},{5,17},{6,18},{7,19},{8,12},{9,13},... | collective-permute-start | bytes 196616 | tf_op jit(solution)/shard_map/ppermute | solution.py:27
  24.1 2.9 %collective-permute-start.4 = (bf16[32,1024]{1,0:T(8,128)(2,1)S(1)}, bf16[32,1024]{1,0:T(8,128)(2,1)S(1)}, u32[]{:S(2)}, u32[]{:S(2)}) collective-permute-start(bf16[32,1024]{1,0:T(8,128)(2,1)S(1)} %get-tuple-element.12), channel_id=1, source_target_pairs={{0,23},{1,0},{2,1},{3,2},{4,3},{5,4},{6,5},{7,6},{8,31},{9,8},{10,... | collective-permute-start | bytes 196616 | tf_op jit(solution)/shard_map/ppermute | solution.py:27
  27.1 0.0 copy-start.3
  27.1 0.6 copy-done.3
  27.8 1.0 sort.49
  28.8 1.0 sort.50
  29.8 0.5 compare_and_fusion
  30.3 0.1 copy-done.1
  30.4 0.6 gather_fusion
  31.1 0.6 compare_and_fusion.2
  31.7 0.1 broadcast_in_dim.64
  31.8 0.1 broadcast_in_dim.65
  31.9 0.9 bitcast_dynamic-update-slice_fusion.7
  32.8 1.2 constant_dynamic-slice_fusion
  34.0 4.6 %collective-permute-start.5 = (bf16[32,1024]{1,0:T(8,128)(2,1)S(1)}, bf16[32,1024]{1,0:T(8,128)(2,1)S(1)}, u32[]{:S(2)}, u32[]{:S(2)}) collective-permute-start(bf16[32,1024]{1,0:T(8,128)(2,1)S(1)} %get-tuple-element.12), channel_id=1, source_target_pairs={{0,22},{1,23},{2,0},{3,1},{4,2},{5,3},{6,4},{7,5},{8,30},{9,31},{1... | collective-permute-start | bytes 196616 | tf_op jit(solution)/shard_map/ppermute | solution.py:27
  38.6 1.9 collective-permute-start.6
  40.6 3.4 %collective-permute-start.11 = (bf16[2,96,256]{2,1,0:T(8,128)(2,1)S(1)}, bf16[2,96,256]{2,1,0:T(8,128)(2,1)}, u32[]{:S(2)}, u32[]{:S(2)}) collective-permute-start(bf16[2,96,256]{2,1,0:T(8,128)(2,1)S(1)} %get-tuple-element.18), channel_id=1, source_target_pairs={{0,1},{1,2},{2,3},{3,4},{4,5},{5,6},{6,7},{7,0},{8,9},{9,10},{10,1... | collective-permute-start | bytes 294920 | tf_op jit(solution)/shard_map/ppermute | solution.py:55
  44.0 6.0 %collective-permute-start.12 = (bf16[2,96,256]{2,1,0:T(8,128)(2,1)S(1)}, bf16[2,96,256]{2,1,0:T(8,128)(2,1)}, u32[]{:S(2)}, u32[]{:S(2)}) collective-permute-start(bf16[2,96,256]{2,1,0:T(8,128)(2,1)S(1)} %get-tuple-element.17), channel_id=1, source_target_pairs={{0,2},{1,3},{2,4},{3,5},{4,6},{5,7},{6,0},{7,1},{8,10},{9,11},{10,... | collective-permute-start | bytes 294920 | tf_op jit(solution)/shard_map/ppermute | solution.py:55
  50.1 2.6 %collective-permute-start.13 = (bf16[2,96,256]{2,1,0:T(8,128)(2,1)S(1)}, bf16[2,96,256]{2,1,0:T(8,128)(2,1)}, u32[]{:S(2)}, u32[]{:S(2)}) collective-permute-start(bf16[2,96,256]{2,1,0:T(8,128)(2,1)S(1)} %get-tuple-element.16), channel_id=1, source_target_pairs={{0,3},{1,4},{2,5},{3,6},{4,7},{5,0},{6,1},{7,2},{8,11},{9,12},{10,... | collective-permute-start | bytes 294920 | tf_op jit(solution)/shard_map/ppermute | solution.py:55
  52.7 5.4 %collective-permute-start.14 = (bf16[2,96,256]{2,1,0:T(8,128)(2,1)S(1)}, bf16[2,96,256]{2,1,0:T(8,128)(2,1)S(1)}, u32[]{:S(2)}, u32[]{:S(2)}) collective-permute-start(bf16[2,96,256]{2,1,0:T(8,128)(2,1)S(1)} %get-tuple-element.15), channel_id=1, source_target_pairs={{0,4},{1,5},{2,6},{3,7},{4,0},{5,1},{6,2},{7,3},{8,12},{9,13},{10,... | collective-permute-start | bytes 294920 | tf_op jit(solution)/shard_map/ppermute | solution.py:55
  58.1 5.8 %collective-permute-start.15 = (bf16[2,96,256]{2,1,0:T(8,128)(2,1)S(1)}, bf16[2,96,256]{2,1,0:T(8,128)(2,1)S(1)}, u32[]{:S(2)}, u32[]{:S(2)}) collective-permute-start(bf16[2,96,256]{2,1,0:T(8,128)(2,1)S(1)} %get-tuple-element.14), channel_id=1, source_target_pairs={{0,5},{1,6},{2,7},{3,0},{4,1},{5,2},{6,3},{7,4},{8,13},{9,14},{10,... | collective-permute-start | bytes 294920 | tf_op jit(solution)/shard_map/ppermute | solution.py:55
  64.0 0.6 gather_fusion.1
  64.6 0.1 bitcast_select_fusion
  64.7 0.0 copy-start.2
  64.7 0.3 fusion.12
  65.0 0.8 copy-done.2
  65.8 0.3 fusion.10
  66.2 1.9 collective-permute-start.7
  68.1 0.9 bitcast_dynamic-update-slice_fusion.6
  69.0 3.5 %collective-permute-start.16 = (bf16[2,96,256]{2,1,0:T(8,128)(2,1)S(1)}, bf16[2,96,256]{2,1,0:T(8,128)(2,1)S(1)}, u32[]{:S(2)}, u32[]{:S(2)}) collective-permute-start(bf16[2,96,256]{2,1,0:T(8,128)(2,1)S(1)} %get-tuple-element.19), channel_id=1, source_target_pairs={{0,6},{1,7},{2,0},{3,1},{4,2},{5,3},{6,4},{7,5},{8,14},{9,15},{10,... | collective-permute-start | bytes 294920 | tf_op jit(solution)/shard_map/ppermute | solution.py:55
  72.5 0.9 bitcast_dynamic-update-slice_fusion.5
  73.4 6.0 %collective-permute-start.17 = (bf16[2,96,256]{2,1,0:T(8,128)(2,1)S(1)}, bf16[2,96,256]{2,1,0:T(8,128)(2,1)S(1)}, u32[]{:S(2)}, u32[]{:S(2)}) collective-permute-start(bf16[2,96,256]{2,1,0:T(8,128)(2,1)S(1)} %get-tuple-element.13), channel_id=1, source_target_pairs={{0,7},{1,0},{2,1},{3,2},{4,3},{5,4},{6,5},{7,6},{8,15},{9,8},{10,9... | collective-permute-start | bytes 294920 | tf_op jit(solution)/shard_map/ppermute | solution.py:55
  79.5 0.9 bitcast_dynamic-update-slice_fusion.4
  80.4 0.3 fusion.2
  80.7 0.3 fusion.22
  81.1 2.4 %collective-permute-start.8 = (bf16[1,2,256,96]{2,3,1,0:T(8,128)(2,1)S(1)}, bf16[1,2,256,96]{2,3,1,0:T(8,128)(2,1)S(1)}, u32[]{:S(2)}, u32[]{:S(2)}) collective-permute-start(bf16[1,2,256,96]{2,3,1,0:T(8,128)(2,1)S(1)} %fusion.22), channel_id=1, source_target_pairs={{0,4},{1,5},{2,6},{3,7},{4,0},{5,1},{6,2},{7,3},{8,12},{9,13},{10,... | collective-permute-start | bytes 294920 | tf_op jit(solution)/shard_map/ppermute | solution.py:41
  83.5 9.3 %collective-permute-done.8 = bf16[1,2,256,96]{2,3,1,0:T(8,128)(2,1)S(1)} collective-permute-done((bf16[1,2,256,96]{2,3,1,0:T(8,128)(2,1)S(1)}, bf16[1,2,256,96]{2,3,1,0:T(8,128)(2,1)S(1)}, u32[]{:S(2)}, u32[]{:S(2)}) %collective-permute-start.8) | collective-permute-done | bytes 98336 | tf_op jit(solution)/shard_map/ppermute | solution.py:41
  92.8 3.2 %collective-permute-start.9 = (bf16[2,2,256,96]{2,3,1,0:T(8,128)(2,1)S(1)}, bf16[2,2,256,96]{2,3,1,0:T(8,128)(2,1)S(1)}, u32[]{:S(2)}, u32[]{:S(2)}) collective-permute-start(bf16[2,2,256,96]{2,3,1,0:T(8,128)(2,1)S(1)} %pad_maximum_fusion.2), channel_id=1, source_target_pairs={{0,2},{1,3},{2,0},{3,1},{4,6},{5,7},{6,4},{7,5},{8,10},{9,11},{10,... | collective-permute-start | bytes 589832 | tf_op jit(solution)/shard_map/ppermute | solution.py:41
  96.0 8.5 %collective-permute-done.9 = bf16[2,2,256,96]{2,3,1,0:T(8,128)(2,1)S(1)} collective-permute-done((bf16[2,2,256,96]{2,3,1,0:T(8,128)(2,1)S(1)}, bf16[2,2,256,96]{2,3,1,0:T(8,128)(2,1)S(1)}, u32[]{:S(2)}, u32[]{:S(2)}) %collective-permute-start.9) | collective-permute-done | bytes 196640 | tf_op jit(solution)/shard_map/ppermute | solution.py:41
  104.5 5.4 %collective-permute-start.10 = (bf16[4,2,256,96]{2,3,1,0:T(8,128)(2,1)S(1)}, bf16[4,2,256,96]{2,3,1,0:T(8,128)(2,1)}, u32[]{:S(2)}, u32[]{:S(2)}) collective-permute-start(bf16[4,2,256,96]{2,3,1,0:T(8,128)(2,1)S(1)} %pad_maximum_fusion.1), channel_id=1, source_target_pairs={{0,1},{1,0},{2,3},{3,2},{4,5},{5,4},{6,7},{7,6},{8,9},{9,8},{10,11... | collective-permute-start | bytes 1179656 | tf_op jit(solution)/shard_map/ppermute | solution.py:41
  110.0 0.6 gather_fusion.3
  110.6 8.7 %collective-permute-done.10 = bf16[4,2,256,96]{2,3,1,0:T(8,128)(2,1)} collective-permute-done((bf16[4,2,256,96]{2,3,1,0:T(8,128)(2,1)S(1)}, bf16[4,2,256,96]{2,3,1,0:T(8,128)(2,1)}, u32[]{:S(2)}, u32[]{:S(2)}) %collective-permute-start.10) | collective-permute-done | bytes 393248 | tf_op jit(solution)/shard_map/ppermute | solution.py:41
  119.4 1.1 pad_maximum_fusion
  120.4 0.0 copy-start.4
  120.5 0.6 gather_fusion.2
  121.1 0.0 copy-done.4
  121.1 0.0 copy-done.5
  121.1 0.5 fusion
  121.7 0.3 copy.13
  121.9 39.4 %all_to_all.33 = bf16[2,256,256]{2,0,1:T(2,128)(2,1)S(1)} all-to-all(bf16[2,256,256]{2,0,1:T(2,128)(2,1)S(1)} %copy.13), channel_id=1, replica_groups=mesh['expert'=64,'dp'=8] {'expert'}, dimensions={1} | all-to-all | bytes 524288 | tf_op jit(solution)/shard_map/all_to_all | solution.py:100
  161.4 0.2 copy.17
  161.6 0.1 all_to_all.26
  161.7 0.2 fusion.36
  161.9 19.5 %all_to_all.34 = f32[8,1,8192]{2,1,0:T(1,128)S(1)} all-to-all(f32[8,1,8192]{2,1,0:T(1,128)S(1)} %bitcast.87), channel_id=1, replica_groups=mesh['expert'=64,'dp'=8] {'dp'}, dimensions={0} | all-to-all | bytes 524288 | tf_op jit(solution)/shard_map/all_to_all | solution.py:64
  181.4 0.2 reduce_sum.18
  181.6 0.8 broadcast_in_dim.74
  182.5 5.5 %all-to-all-start.2 = ((f32[8,1,8192]{2,1,0:T(1,128)}), f32[8,1,8192]{2,1,0:T(1,128)S(1)}, u32[]{:S(2)}, u32[]{:S(2)}) async-start(f32[8,1,8192]{2,1,0:T(1,128)} %broadcast_in_dim.74), calls=%async_computation.2 | async-start | bytes 524288 | tf_op jit(solution)/shard_map/all_to_all | solution.py:66
  188.0 15.9 %all-to-all-done.2 = f32[8,1,8192]{2,1,0:T(1,128)S(1)} async-done(((f32[8,1,8192]{2,1,0:T(1,128)}), f32[8,1,8192]{2,1,0:T(1,128)S(1)}, u32[]{:S(2)}, u32[]{:S(2)}) %all-to-all-start.2) | async-done | bytes 262176 | tf_op jit(solution)/shard_map/all_to_all | solution.py:66
  203.9 0.1 fusion.20
  204.1 0.9 fusion.21
  (46 shorter events, 0.3 us)
Async XLA Ops:
  0.0 64.7 %copy-start = (bf16[2,96,2048]{2,1,0:T(8,128)(2,1)S(1)}, bf16[2,96,2048]{2,1,0:T(8,128)(2,1)}, u32[]{:S(2)}) copy-start(bf16[2,96,2048]{2,1,0:T(8,128)(2,1)} %param.7) | copy-start | bytes 2359300
  0.9 33.1 %collective-permute-start = (bf16[32,1024]{1,0:T(8,128)(2,1)S(1)}, bf16[32,1024]{1,0:T(8,128)(2,1)S(1)}, u32[]{:S(2)}, u32[]{:S(2)}) collective-permute-start(bf16[32,1024]{1,0:T(8,128)(2,1)S(1)} %get-tuple-element.12), channel_id=1, source_target_pairs={{0,1},{1,2},{2,3},{3,4},{4,5},{5,6},{6,7},{7,16},{8,9},{9,10},{10,... | collective-permute-start | bytes 196616 | tf_op jit(solution)/shard_map/ppermute | solution.py:27
  4.8 33.9 %collective-permute-start.1 = (bf16[32,1024]{1,0:T(8,128)(2,1)S(1)}, bf16[32,1024]{1,0:T(8,128)(2,1)S(1)}, u32[]{:S(2)}, u32[]{:S(2)}) collective-permute-start(bf16[32,1024]{1,0:T(8,128)(2,1)S(1)} %get-tuple-element.12), channel_id=1, source_target_pairs={{0,2},{1,3},{2,4},{3,5},{4,6},{5,7},{6,16},{7,17},{8,10},{9,11},{1... | collective-permute-start | bytes 196616 | tf_op jit(solution)/shard_map/ppermute | solution.py:27
  11.2 29.4 %collective-permute-start.2 = (bf16[32,1024]{1,0:T(8,128)(2,1)S(1)}, bf16[32,1024]{1,0:T(8,128)(2,1)S(1)}, u32[]{:S(2)}, u32[]{:S(2)}) collective-permute-start(bf16[32,1024]{1,0:T(8,128)(2,1)S(1)} %get-tuple-element.12), channel_id=1, source_target_pairs={{0,3},{1,4},{2,5},{3,6},{4,7},{5,16},{6,17},{7,18},{8,11},{9,12},{... | collective-permute-start | bytes 196616 | tf_op jit(solution)/shard_map/ppermute | solution.py:27
  17.7 26.3 %collective-permute-start.3 = (bf16[32,1024]{1,0:T(8,128)(2,1)S(1)}, bf16[32,1024]{1,0:T(8,128)(2,1)S(1)}, u32[]{:S(2)}, u32[]{:S(2)}) collective-permute-start(bf16[32,1024]{1,0:T(8,128)(2,1)S(1)} %get-tuple-element.12), channel_id=1, source_target_pairs={{0,4},{1,5},{2,6},{3,7},{4,16},{5,17},{6,18},{7,19},{8,12},{9,13},... | collective-permute-start | bytes 196616 | tf_op jit(solution)/shard_map/ppermute | solution.py:27
  24.1 25.9 %collective-permute-start.4 = (bf16[32,1024]{1,0:T(8,128)(2,1)S(1)}, bf16[32,1024]{1,0:T(8,128)(2,1)S(1)}, u32[]{:S(2)}, u32[]{:S(2)}) collective-permute-start(bf16[32,1024]{1,0:T(8,128)(2,1)S(1)} %get-tuple-element.12), channel_id=1, source_target_pairs={{0,23},{1,0},{2,1},{3,2},{4,3},{5,4},{6,5},{7,6},{8,31},{9,8},{10,... | collective-permute-start | bytes 196616 | tf_op jit(solution)/shard_map/ppermute | solution.py:27
  27.1 0.7 copy-start.3
  29.8 0.7 copy-start.1
  34.0 18.7 %collective-permute-start.5 = (bf16[32,1024]{1,0:T(8,128)(2,1)S(1)}, bf16[32,1024]{1,0:T(8,128)(2,1)S(1)}, u32[]{:S(2)}, u32[]{:S(2)}) collective-permute-start(bf16[32,1024]{1,0:T(8,128)(2,1)S(1)} %get-tuple-element.12), channel_id=1, source_target_pairs={{0,22},{1,23},{2,0},{3,1},{4,2},{5,3},{6,4},{7,5},{8,30},{9,31},{1... | collective-permute-start | bytes 196616 | tf_op jit(solution)/shard_map/ppermute | solution.py:27
  38.6 19.5 %collective-permute-start.6 = (bf16[32,1024]{1,0:T(8,128)(2,1)S(1)}, bf16[32,1024]{1,0:T(8,128)(2,1)S(1)}, u32[]{:S(2)}, u32[]{:S(2)}) collective-permute-start(bf16[32,1024]{1,0:T(8,128)(2,1)S(1)} %get-tuple-element.12), channel_id=1, source_target_pairs={{0,21},{1,22},{2,23},{3,0},{4,1},{5,2},{6,3},{7,4},{8,29},{9,30},{... | collective-permute-start | bytes 196616 | tf_op jit(solution)/shard_map/ppermute | solution.py:27
  40.6 25.6 %collective-permute-start.11 = (bf16[2,96,256]{2,1,0:T(8,128)(2,1)S(1)}, bf16[2,96,256]{2,1,0:T(8,128)(2,1)}, u32[]{:S(2)}, u32[]{:S(2)}) collective-permute-start(bf16[2,96,256]{2,1,0:T(8,128)(2,1)S(1)} %get-tuple-element.18), channel_id=1, source_target_pairs={{0,1},{1,2},{2,3},{3,4},{4,5},{5,6},{6,7},{7,0},{8,9},{9,10},{10,1... | collective-permute-start | bytes 294920 | tf_op jit(solution)/shard_map/ppermute | solution.py:55
  44.0 25.0 %collective-permute-start.12 = (bf16[2,96,256]{2,1,0:T(8,128)(2,1)S(1)}, bf16[2,96,256]{2,1,0:T(8,128)(2,1)}, u32[]{:S(2)}, u32[]{:S(2)}) collective-permute-start(bf16[2,96,256]{2,1,0:T(8,128)(2,1)S(1)} %get-tuple-element.17), channel_id=1, source_target_pairs={{0,2},{1,3},{2,4},{3,5},{4,6},{5,7},{6,0},{7,1},{8,10},{9,11},{10,... | collective-permute-start | bytes 294920 | tf_op jit(solution)/shard_map/ppermute | solution.py:55
  50.1 23.3 %collective-permute-start.13 = (bf16[2,96,256]{2,1,0:T(8,128)(2,1)S(1)}, bf16[2,96,256]{2,1,0:T(8,128)(2,1)}, u32[]{:S(2)}, u32[]{:S(2)}) collective-permute-start(bf16[2,96,256]{2,1,0:T(8,128)(2,1)S(1)} %get-tuple-element.16), channel_id=1, source_target_pairs={{0,3},{1,4},{2,5},{3,6},{4,7},{5,0},{6,1},{7,2},{8,11},{9,12},{10,... | collective-permute-start | bytes 294920 | tf_op jit(solution)/shard_map/ppermute | solution.py:55
  52.7 30.7 %collective-permute-start.14 = (bf16[2,96,256]{2,1,0:T(8,128)(2,1)S(1)}, bf16[2,96,256]{2,1,0:T(8,128)(2,1)S(1)}, u32[]{:S(2)}, u32[]{:S(2)}) collective-permute-start(bf16[2,96,256]{2,1,0:T(8,128)(2,1)S(1)} %get-tuple-element.15), channel_id=1, source_target_pairs={{0,4},{1,5},{2,6},{3,7},{4,0},{5,1},{6,2},{7,3},{8,12},{9,13},{10,... | collective-permute-start | bytes 294920 | tf_op jit(solution)/shard_map/ppermute | solution.py:55
  58.1 37.8 %collective-permute-start.15 = (bf16[2,96,256]{2,1,0:T(8,128)(2,1)S(1)}, bf16[2,96,256]{2,1,0:T(8,128)(2,1)S(1)}, u32[]{:S(2)}, u32[]{:S(2)}) collective-permute-start(bf16[2,96,256]{2,1,0:T(8,128)(2,1)S(1)} %get-tuple-element.14), channel_id=1, source_target_pairs={{0,5},{1,6},{2,7},{3,0},{4,1},{5,2},{6,3},{7,4},{8,13},{9,14},{10,... | collective-permute-start | bytes 294920 | tf_op jit(solution)/shard_map/ppermute | solution.py:55
  64.7 1.1 copy-start.2
  66.2 14.2 %collective-permute-start.7 = (bf16[256,1024]{1,0:T(8,128)(2,1)S(1)}, bf16[256,1024]{1,0:T(8,128)(2,1)S(1)}, u32[]{:S(2)}, u32[]{:S(2)}) collective-permute-start(bf16[256,1024]{1,0:T(8,128)(2,1)S(1)} %bitcast_select_fusion), channel_id=1, source_target_pairs={{0,8},{8,0},{16,24},{24,16},{32,40},{40,32},{48,56},{56,48},{64,72... | collective-permute-start | bytes 1572872 | tf_op jit(solution)/shard_map/ppermute | solution.py:80
  69.0 41.0 %collective-permute-start.16 = (bf16[2,96,256]{2,1,0:T(8,128)(2,1)S(1)}, bf16[2,96,256]{2,1,0:T(8,128)(2,1)S(1)}, u32[]{:S(2)}, u32[]{:S(2)}) collective-permute-start(bf16[2,96,256]{2,1,0:T(8,128)(2,1)S(1)} %get-tuple-element.19), channel_id=1, source_target_pairs={{0,6},{1,7},{2,0},{3,1},{4,2},{5,3},{6,4},{7,5},{8,14},{9,15},{10,... | collective-permute-start | bytes 294920 | tf_op jit(solution)/shard_map/ppermute | solution.py:55
  73.4 36.6 %collective-permute-start.17 = (bf16[2,96,256]{2,1,0:T(8,128)(2,1)S(1)}, bf16[2,96,256]{2,1,0:T(8,128)(2,1)S(1)}, u32[]{:S(2)}, u32[]{:S(2)}) collective-permute-start(bf16[2,96,256]{2,1,0:T(8,128)(2,1)S(1)} %get-tuple-element.13), channel_id=1, source_target_pairs={{0,7},{1,0},{2,1},{3,2},{4,3},{5,4},{6,5},{7,6},{8,15},{9,8},{10,9... | collective-permute-start | bytes 294920 | tf_op jit(solution)/shard_map/ppermute | solution.py:55
  81.1 11.7 %collective-permute-start.8 = (bf16[1,2,256,96]{2,3,1,0:T(8,128)(2,1)S(1)}, bf16[1,2,256,96]{2,3,1,0:T(8,128)(2,1)S(1)}, u32[]{:S(2)}, u32[]{:S(2)}) collective-permute-start(bf16[1,2,256,96]{2,3,1,0:T(8,128)(2,1)S(1)} %fusion.22), channel_id=1, source_target_pairs={{0,4},{1,5},{2,6},{3,7},{4,0},{5,1},{6,2},{7,3},{8,12},{9,13},{10,... | collective-permute-start | bytes 294920 | tf_op jit(solution)/shard_map/ppermute | solution.py:41
  92.8 11.7 %collective-permute-start.9 = (bf16[2,2,256,96]{2,3,1,0:T(8,128)(2,1)S(1)}, bf16[2,2,256,96]{2,3,1,0:T(8,128)(2,1)S(1)}, u32[]{:S(2)}, u32[]{:S(2)}) collective-permute-start(bf16[2,2,256,96]{2,3,1,0:T(8,128)(2,1)S(1)} %pad_maximum_fusion.2), channel_id=1, source_target_pairs={{0,2},{1,3},{2,0},{3,1},{4,6},{5,7},{6,4},{7,5},{8,10},{9,11},{10,... | collective-permute-start | bytes 589832 | tf_op jit(solution)/shard_map/ppermute | solution.py:41
  104.5 14.8 %collective-permute-start.10 = (bf16[4,2,256,96]{2,3,1,0:T(8,128)(2,1)S(1)}, bf16[4,2,256,96]{2,3,1,0:T(8,128)(2,1)}, u32[]{:S(2)}, u32[]{:S(2)}) collective-permute-start(bf16[4,2,256,96]{2,3,1,0:T(8,128)(2,1)S(1)} %pad_maximum_fusion.1), channel_id=1, source_target_pairs={{0,1},{1,0},{2,3},{3,2},{4,5},{5,4},{6,7},{7,6},{8,9},{9,8},{10,11... | collective-permute-start | bytes 1179656 | tf_op jit(solution)/shard_map/ppermute | solution.py:41
  120.4 0.7 copy-start.4
  120.5 0.7 copy-start.5
  182.5 21.4 %all-to-all-start.2 = ((f32[8,1,8192]{2,1,0:T(1,128)}), f32[8,1,8192]{2,1,0:T(1,128)S(1)}, u32[]{:S(2)}, u32[]{:S(2)}) async-start(f32[8,1,8192]{2,1,0:T(1,128)} %broadcast_in_dim.74), calls=%async_computation.2 | async-start | bytes 524288 | tf_op jit(solution)/shard_map/all_to_all | solution.py:66
